TPU v7x, 256 devices: a whole 4x4x8 slice. The times are simulated.
256 devices in a mesh: space: 128 (over z, y, x), sub: 2 (over core).
Axes of the slice: x: 4, y: 4, z: 8, core: 2. Of those that a mesh axis runs over, the one named last changes fastest.
Arguments:
- features: bfloat16 [262144, 128], P(('space', 'sub')), may hold values from -6 to 6
- weights: bfloat16 [27, 128, 128], replicated, may hold values from -0.125 to 0.125
- cotangent: bfloat16 [262144, 128], P(('space', 'sub')), may hold values from -6 to 6
- pair_offset: int32 [65536], P(('space', 'sub')), may hold values from 0 to 26, as said below
- pair_source: int32 [65536], P(('space', 'sub')), may hold values from 0 to 2047, as said below
- pair_target: int32 [65536], P(('space', 'sub')), may hold values from 0 to 7
- pair_rows: int32 [65536, 128], P(('space', 'sub')), may hold values from -1 to 127, as said below
- pair_count: int32 [256], P(('space', 'sub')), may hold values from 64 to 256, as said below
Outputs:
- output: bfloat16 [262144, 128], P(('space', 'sub'))
- grad_features: bfloat16 [262144, 128], P(('space', 'sub'))
- grad_weights: float32 [27, 128, 128], replicated
Inputs may be any that keep to these rules, and one draw needn't show every extreme that they name: `pair_offset`: each value is a kernel offset. The input block of a pair of device d lies on device d - 1, d or d + 1 (that is, pair_source // 8 differs from d by at most one). `pair_rows`: within one pair no nonnegative row number appears twice. `pair_count`: pairs of a device at positions from its count on are not live; some device has all 256 pairs live.
All inputs are finite; a program needn't handle non-finite values.
Results may differ from a plain program's by a relative error of at most 0.001.
Values may be sent and summed in bfloat16 or wider, within the bound.
No kernel may reach another device: no remote copies, remote signals or barrier semaphores. Data moves between devices by JAX's collectives and lax.ppermute only.
A program may use at most 64 MiB of HBM per device.

v0:
```python
import math

import jax
import jax.numpy as jnp
from jax import lax
from jax.sharding import PartitionSpec as P

BLK = 128


def passed_along(value, axis, steps):
    count = lax.axis_size(axis)
    leading, last = (max(0, -steps), min(count, count - steps))
    return lax.ppermute(value, axis, [(source, source + steps) for source in range(leading, last)])


def grouped(array_in, group_size):
    return array_in.reshape((array_in.shape[0] // group_size, group_size) + array_in.shape[1:])


def picker(index, count, dtype):
    return (index[:, None] == jnp.arange(count, dtype=jnp.int32)[None, :]).astype(dtype)


def permuter(row_map, usable, dtype):
    columns = jnp.arange(row_map.shape[1], dtype=jnp.int32)
    return ((row_map[..., None] == columns[None, None, :]) & usable[..., None]).astype(dtype)


def forward_sweep(window, weights, grad_blocks, rulebook, myself, blocks):
    g_off_all, source_all, target_all, row_map_all, live_count = rulebook
    channels = window.shape[1]
    kernel_count = weights.shape[0]
    window_blocks = window.reshape(3 * blocks, BLK, channels)
    group_size = 16
    positions = jnp.arange(g_off_all.shape[0], dtype=jnp.int32)
    relative = source_all // blocks - myself
    window_block = (relative + 1) * blocks + source_all % blocks
    pieces = (
        grouped(g_off_all, group_size),
        grouped(window_block, group_size),
        grouped(target_all, group_size),
        grouped(row_map_all, group_size),
        grouped(positions, group_size),
    )
    highest = lax.Precision.HIGHEST

    def advance(state_in, item_now):
        out_sum, returned_sum, grad_sum = state_in
        g_off, g_block, g_target, row_map, g_pos = item_now
        usable = (row_map >= 0) & (g_pos < live_count[0])[:, None]
        perm = permuter(row_map, usable, jnp.bfloat16)
        block_pick = picker(g_block, 3 * blocks, jnp.bfloat16)
        rows_in = jnp.einsum(
            "gk,kbc->gbc", block_pick, window_blocks, preferred_element_type=jnp.float32
        ).astype(jnp.bfloat16)
        gathered = jnp.einsum(
            "grs,gsc->grc", perm, rows_in, preferred_element_type=jnp.float32
        ).astype(jnp.bfloat16)
        off_pick = picker(g_off, kernel_count, jnp.bfloat16)
        chosen = jnp.einsum(
            "gk,kcd->gcd", off_pick, weights, preferred_element_type=jnp.float32
        ).astype(jnp.bfloat16)
        product = jnp.einsum("gbc,gcd->gbd", gathered, chosen, preferred_element_type=jnp.float32)
        target_pick = picker(g_target, blocks, jnp.float32)
        out_sum = out_sum + jnp.einsum("gt,gbd->tbd", target_pick, product, precision=highest)
        grad_out = jnp.einsum(
            "gt,tbd->gbd",
            target_pick.astype(jnp.bfloat16),
            grad_blocks,
            preferred_element_type=jnp.float32,
        ).astype(jnp.bfloat16)
        pair_grad = jnp.einsum(
            "gbc,gbd->gcd", gathered, grad_out, preferred_element_type=jnp.float32
        )
        grad_sum = grad_sum + jnp.einsum(
            "gk,gcd->kcd", off_pick.astype(jnp.float32), pair_grad, precision=highest
        )
        moved = jnp.einsum(
            "grs,grd->gsd", perm, grad_out, preferred_element_type=jnp.float32
        ).astype(jnp.bfloat16)
        returned = jnp.einsum("gsd,gcd->gsc", moved, chosen, preferred_element_type=jnp.float32)
        returned_sum = returned_sum + jnp.einsum(
            "gk,gsc->ksc", block_pick.astype(jnp.float32), returned, precision=highest
        )
        return ((out_sum, returned_sum, grad_sum), None)

    back_blocks = 3 * blocks
    start = (
        jnp.zeros((blocks, BLK, channels), jnp.float32),
        jnp.zeros((back_blocks, BLK, channels), jnp.float32),
        jnp.zeros((kernel_count, channels, channels), jnp.float32),
    )
    (out_sum, returned_sum, grad_sum), _ = lax.scan(advance, start, pieces)
    return (out_sum, returned_sum, grad_sum)


def on_device(
    features, weights, cotangent, pair_offset, pair_source, pair_target, pair_rows, pair_count
):
    axis_count = lax.axis_size(("space", "sub"))
    myself = lax.axis_index(("space", "sub"))
    local_rows = features.shape[0]
    blocks = local_rows // BLK
    channels = features.shape[1]
    before = passed_along(features, ("space", "sub"), 1)
    next_side = passed_along(features, ("space", "sub"), -1)
    window = jnp.concatenate([before, features, next_side], axis=0)
    grad_blocks = cotangent.reshape(blocks, BLK, channels)
    rulebook = (pair_offset, pair_source, pair_target, pair_rows, pair_count)
    out_sum, returned_sum, grad_sum = forward_sweep(
        window, weights, grad_blocks, rulebook, myself, blocks
    )
    low_part = returned_sum[:blocks].reshape(local_rows, channels)
    middle = returned_sum[blocks : 2 * blocks].reshape(local_rows, channels)
    high_part = returned_sum[2 * blocks :].reshape(local_rows, channels)
    from_next = passed_along(low_part, ("space", "sub"), -1)
    from_prev = passed_along(high_part, ("space", "sub"), 1)
    grad_features = (middle + from_next + from_prev).astype(jnp.bfloat16)
    output = out_sum.reshape(local_rows, channels).astype(jnp.bfloat16)
    grad_sum = grad_sum * (1.0 / math.sqrt(axis_count * local_rows))
    grand_total = lax.psum(grad_sum, ("space", "sub"))
    return (output, grad_features, grand_total)


def solution(mesh):
    placed = (
        P(("space", "sub"), None),
        P(),
        P(("space", "sub"), None),
        P(("space", "sub")),
        P(("space", "sub")),
        P(("space", "sub")),
        P(("space", "sub"), None),
        P(("space", "sub")),
    )
    return jax.shard_map(
        on_device,
        mesh=mesh,
        in_specs=placed,
        out_specs=(P(("space", "sub"), None), P(("space", "sub"), None), P()),
        check_vma=False,
    )
```

profile of v0, /device:TPU:127, one launch (start us, length us, event | category | flops | bytes accessed | tf_op | source)
XLA Modules:
  0.0 590.4 jit_solution(12657344990175107696)
XLA Ops:
  10.0 8.4 %collective-permute-start = (bf16[1024,128]{1,0:T(8,128)(2,1)}, bf16[1024,128]{1,0:T(8,128)(2,1)S(1)}, u32[]{:S(2)}, u32[]{:S(2)}) collective-permute-start(bf16[1024,128]{1,0:T(8,128)(2,1)} %param.10), channel_id=1, source_target_pairs={{0,1},{1,2},{2,3},{3,4},{4,5},{5,6},{6,7},{7,8},{8,9},{9,10},{10,1... | collective-permute-start | bytes 786440 | tf_op jit(solution)/shard_map/ppermute | solution.py:14
  23.4 291.4 %while.15 = (s32[]{:T(128)}, f32[8,128,128]{2,0,1:T(8,128)}, f32[24,128,128]{2,0,1:T(8,128)}, f32[27,128,128]{2,0,1:T(8,128)}, s32[16,16]{1,0:T(8,128)S(1)}, /*i...) while((s32[]{:T(128)}, f32[8,128,128]{2,0,1:T(8,128)}, ...), condition=%wide.region_1.2_spmd.clone, body=%wide.region_0.1_spmd.clone.sunk | while | flops 556112000 | bytes 45096096 | solution.py:94
  48.2 4.0 select_add_fusion.4
  66.6 4.0 select_add_fusion.4
  80.5 2.9 convolution_add_fusion.2
  85.0 4.0 select_add_fusion.4
  98.9 2.9 convolution_add_fusion.2
  103.3 4.0 select_add_fusion.4
  117.2 2.9 convolution_add_fusion.2
  121.7 4.0 select_add_fusion.4
  140.1 4.0 select_add_fusion.4
  154.0 2.9 convolution_add_fusion.2
  158.4 4.0 select_add_fusion.4
  172.3 2.9 convolution_add_fusion.2
  176.8 4.0 select_add_fusion.4
  190.7 2.9 convolution_add_fusion.2
  195.1 4.0 select_add_fusion.4
  209.1 2.9 convolution_add_fusion.2
  213.5 4.0 select_add_fusion.4
  231.9 4.0 select_add_fusion.4
  245.8 2.9 convolution_add_fusion.2
  250.2 4.0 select_add_fusion.4
  264.2 2.9 convolution_add_fusion.2
  268.6 4.0 select_add_fusion.4
  282.5 2.9 convolution_add_fusion.2
  287.0 4.0 select_add_fusion.4
  300.9 2.9 convolution_add_fusion.2
  305.3 4.0 select_add_fusion.4
  314.9 3.9 copy_multiply_fusion
  320.4 8.3 %collective-permute-start.3 = (f32[1024,128]{1,0:T(8,128)S(1)}, f32[1024,128]{1,0:T(8,128)S(1)}, u32[]{:S(2)}, u32[]{:S(2)}) collective-permute-start(f32[1024,128]{1,0:T(8,128)S(1)} %bitcast.77), channel_id=1, source_target_pairs={{0,1},{1,2},{2,3},{3,4},{4,5},{5,6},{6,7},{7,8},{8,9},{9,10},{10,1... | collective-permute-start | bytes 1572872 | tf_op jit(solution)/shard_map/ppermute | solution.py:14
  335.3 9.9 %collective-permute-done.2 = f32[1024,128]{1,0:T(8,128)S(1)} collective-permute-done((f32[1024,128]{1,0:T(8,128)S(1)}, f32[1024,128]{1,0:T(8,128)S(1)}, u32[]{:S(2)}, u32[]{:S(2)}) %collective-permute-start.2) | collective-permute-done | bytes 524320 | tf_op jit(solution)/shard_map/ppermute | solution.py:14
  346.0 234.6 %all-reduce.2.cloned.1.call-done = f32[27,128,128]{2,1,0:T(8,128)} async-done(((f32[27,128,128]{2,1,0:T(8,128)}), f32[27,128,128]{2,1,0:T(8,128)}) %all-reduce.2.cloned.1.call-update) | async-done | bytes 1769488 | tf_op jit(solution)/shard_map/psum | solution.py:122
  (406 shorter events, 217.2 us)
Async XLA Ops:
  7.2 16.2 %copy-start.7 = (bf16[1024,128]{1,0:T(8,128)(2,1)S(1)}, bf16[1024,128]{1,0:T(8,128)(2,1)}, u32[]{:S(2)}) copy-start(bf16[1024,128]{1,0:T(8,128)(2,1)} %param.10) | copy-start | bytes 786436
  7.2 15.3 %copy-start.6 = (bf16[1024,128]{1,0:T(8,128)(2,1)S(1)}, bf16[1024,128]{1,0:T(8,128)(2,1)}, u32[]{:S(2)}) copy-start(bf16[1024,128]{1,0:T(8,128)(2,1)} %param.12) | copy-start | bytes 786436
  7.2 573.5 %all-reduce.2.cloned.1.call-start = ((), (), s32[]{:S(2)}) async-start(), calls=%async_computation | async-start | bytes 3538944 | tf_op jit(solution)/shard_map/psum | solution.py:122
  7.2 16.1 %collective-permute-start.1 = (bf16[1024,128]{1,0:T(8,128)(2,1)}, bf16[1024,128]{1,0:T(8,128)(2,1)S(1)}, u32[]{:S(2)}, u32[]{:S(2)}) collective-permute-start(bf16[1024,128]{1,0:T(8,128)(2,1)} %param.10), channel_id=1, source_target_pairs={{1,0},{2,1},{3,2},{4,3},{5,4},{6,5},{7,6},{8,7},{9,8},{10,9},{11,1... | collective-permute-start | bytes 786440 | tf_op jit(solution)/shard_map/ppermute | solution.py:14
  10.0 13.4 %collective-permute-start = (bf16[1024,128]{1,0:T(8,128)(2,1)}, bf16[1024,128]{1,0:T(8,128)(2,1)S(1)}, u32[]{:S(2)}, u32[]{:S(2)}) collective-permute-start(bf16[1024,128]{1,0:T(8,128)(2,1)} %param.10), channel_id=1, source_target_pairs={{0,1},{1,2},{2,3},{3,4},{4,5},{5,6},{6,7},{7,8},{8,9},{9,10},{10,1... | collective-permute-start | bytes 786440 | tf_op jit(solution)/shard_map/ppermute | solution.py:14
  23.4 3.4 copy-start.3
  35.5 3.9 copy-start.4
  53.8 3.9 copy-start.4
  72.2 3.9 copy-start.4
  76.1 3.4 copy-start.3
  90.6 3.9 copy-start.4
  94.5 3.4 copy-start.3
  108.9 3.9 copy-start.4
  112.8 3.4 copy-start.3
  127.3 3.9 copy-start.4
  131.2 3.4 copy-start.3
  145.7 3.9 copy-start.4
  149.6 3.4 copy-start.3
  164.0 3.9 copy-start.4
  167.9 3.4 copy-start.3
  182.4 3.9 copy-start.4
  200.8 3.9 copy-start.4
  219.1 3.9 copy-start.4
  237.5 3.9 copy-start.4
  241.4 3.4 copy-start.3
  255.9 3.9 copy-start.4
  259.8 3.4 copy-start.3
  274.2 3.9 copy-start.4
  292.6 3.9 copy-start.4
  311.0 3.9 copy-start.4
  320.4 14.9 %collective-permute-start.3 = (f32[1024,128]{1,0:T(8,128)S(1)}, f32[1024,128]{1,0:T(8,128)S(1)}, u32[]{:S(2)}, u32[]{:S(2)}) collective-permute-start(f32[1024,128]{1,0:T(8,128)S(1)} %bitcast.77), channel_id=1, source_target_pairs={{0,1},{1,2},{2,3},{3,4},{4,5},{5,6},{6,7},{7,8},{8,9},{9,10},{10,1... | collective-permute-start | bytes 1572872 | tf_op jit(solution)/shard_map/ppermute | solution.py:14
  328.9 16.4 %collective-permute-start.2 = (f32[1024,128]{1,0:T(8,128)S(1)}, f32[1024,128]{1,0:T(8,128)S(1)}, u32[]{:S(2)}, u32[]{:S(2)}) collective-permute-start(f32[1024,128]{1,0:T(8,128)S(1)} %bitcast.78), channel_id=1, source_target_pairs={{1,0},{2,1},{3,2},{4,3},{5,4},{6,5},{7,6},{8,7},{9,8},{10,9},{11,1... | collective-permute-start | bytes 1572872 | tf_op jit(solution)/shard_map/ppermute | solution.py:14
  (56 other events, 125.8 us)
Sparse Core Ops, SparseCore 0:
  319.0 261.6 all-reduce.1
where the time goes:
time: 595 us; the launch traced here: 590 us
  waiting for transfers between devices  247 us (42%)
  matrix products  218 us (37%)
  local copies, waits for them, and re-layouts  58.6 us (10%)
  other arithmetic  29.5 us (5%)
  starting transfers between devices  21.4 us (4%)
  between operations  14.2 us (2%)
    psum x1, waiting for transfers between devices, on_device(): grand_total = lax.psum(grad_sum, ('space', 'sub'))  235 us
    dot_general x16, matrix products, advance(): jnp.einsum('gk,gsc->ksc', block_pick.astype(jnp.float32), returned, preci...  62.8 us
    dot_general x16, matrix products, advance(): jnp.einsum('gt,gbd->tbd', target_pick, product, precision=highest)  45.6 us
    dot_general x16, matrix products, advance(): jnp.einsum('gk,gcd->kcd', off_pick.astype(jnp.float32), pair_grad, precis...  41.4 us
    while x160, local copies, waits for them, and re-layouts  41.2 us
    ppermute x4, starting transfers between devices, passed_along(): lax.ppermute(value, axis, [(source, source + steps) for source in range(l...  21.4 us
    dot_general x16, matrix products, advance(): jnp.einsum('gsd,gcd->gsc', moved, chosen, preferred_element_type=jnp.floa...  18.5 us
    dot_general x16, matrix products, advance(): jnp.einsum('grs,gsc->grc', perm, rows_in, preferred_element_type=jnp.floa...  14.6 us
  transfers between devices with their start and end apart: 5, of which 3 were waited for; matrix products, arithmetic and copies ran while one was open for 1% of the time, Pallas kernels for 0%

commit v1 on v0

--- a/solution.py
+++ b/solution.py
@@ -12,6 +12,26 @@
     count = lax.axis_size(axis)
     leading, last = (max(0, -steps), min(count, count - steps))
     return lax.ppermute(value, axis, [(source, source + steps) for source in range(leading, last)])
+
+
+def summed_everywhere(value, axis):
+    count = lax.axis_size(axis)
+    if count & (count - 1) or value.size % count:
+        return lax.psum(value, axis)
+    me = lax.axis_index(axis)
+    flat = value.reshape(-1)
+    masks = [1 << step for step in range(count.bit_length() - 1)]
+    for mask in masks:
+        half = flat.shape[0] // 2
+        upper = (me & mask) != 0
+        send = jnp.where(upper, flat[:half], flat[half:])
+        keep = jnp.where(upper, flat[half:], flat[:half])
+        flat = keep + lax.ppermute(send, axis, [(i, i ^ mask) for i in range(count)])
+    for mask in reversed(masks):
+        upper = (me & mask) != 0
+        other = lax.ppermute(flat, axis, [(i, i ^ mask) for i in range(count)])
+        flat = jnp.where(upper, jnp.concatenate([other, flat]), jnp.concatenate([flat, other]))
+    return flat.reshape(value.shape)
 
 
 def grouped(array_in, group_size):
@@ -119,7 +139,7 @@
     grad_features = (middle + from_next + from_prev).astype(jnp.bfloat16)
     output = out_sum.reshape(local_rows, channels).astype(jnp.bfloat16)
     grad_sum = grad_sum * (1.0 / math.sqrt(axis_count * local_rows))
-    grand_total = lax.psum(grad_sum, ("space", "sub"))
+    grand_total = summed_everywhere(grad_sum, ("space", "sub"))
     return (output, grad_features, grand_total)
 
 

time: 595 us -> 435 us (0.73)
  waiting for transfers between devices: 247 us -> 80.7 us
  starting transfers between devices: 21.4 us -> 46 us
  between operations: 14.2 us -> 0.97 us
    psum x1 -> x0, waiting for transfers between devices: 235 us -> none  [on_device(): grand_total = lax.psum(grad_sum, ('space', 'sub'))]
    ppermute x0 -> x16, waiting for transfers between devices: none -> 68.6 us  [the longest x8 39.9 us: summed_everywhere(): lax.ppermute(send, axis, [(i, i ^ mask) for i in range(count)])]
    ppermute x0 -> x16, starting transfers between devices: none -> 25.5 us  [the longest x8 22.3 us: summed_everywhere(): other = lax.ppermute(flat, axis, [(i, i ^ mask) for i in range(count)])]
  transfers between devices with their start and end apart: 5 -> 20, of which waited for: 3 -> 17; matrix products, arithmetic and copies ran while one was open for 1% -> 2% of each run, Pallas kernels for 0% -> 0%
where the time goes in v1:
time: 435 us; the launch traced here: 432 us
  matrix products  218 us (50%)
  waiting for transfers between devices  80.7 us (19%)
  local copies, waits for them, and re-layouts  54.6 us (13%)
  starting transfers between devices  46 us (11%)
  other arithmetic  30.6 us (7%)
    dot_general x16, matrix products, advance(): jnp.einsum('gk,gsc->ksc', block_pick.astype(jnp.float32), returned, preci...  62.5 us
    dot_general x16, matrix products, advance(): jnp.einsum('gt,gbd->tbd', target_pick, product, precision=highest)  45.6 us
    while x160, local copies, waits for them, and re-layouts  41.5 us
    dot_general x16, matrix products, advance(): jnp.einsum('gk,gcd->kcd', off_pick.astype(jnp.float32), pair_grad, precis...  41.3 us
    ppermute x8, waiting for transfers between devices, summed_everywhere(): lax.ppermute(send, axis, [(i, i ^ mask) for i in range(count)])  39.9 us
    ppermute x8, waiting for transfers between devices, summed_everywhere(): other = lax.ppermute(flat, axis, [(i, i ^ mask) for i in range(count)])  28.7 us
    ppermute x8, starting transfers between devices, summed_everywhere(): other = lax.ppermute(flat, axis, [(i, i ^ mask) for i in range(count)])  22.3 us
    ppermute x4, starting transfers between devices, passed_along(): lax.ppermute(value, axis, [(source, source + steps) for source in range(l...  20.5 us
  transfers between devices with their start and end apart: 20, of which 17 were waited for; matrix products, arithmetic and copies ran while one was open for 2% of the time, Pallas kernels for 0%

profile of v1, /device:TPU:127, one launch (start us, length us, event | category | flops | bytes accessed | tf_op | source)
XLA Modules:
  0.0 432.1 jit_solution(13427138735752040057)
XLA Ops:
  3.4 8.4 %collective-permute-start = (bf16[1024,128]{1,0:T(8,128)(2,1)}, bf16[1024,128]{1,0:T(8,128)(2,1)S(1)}, u32[]{:S(2)}, u32[]{:S(2)}) collective-permute-start(bf16[1024,128]{1,0:T(8,128)(2,1)} %param.10), channel_id=1, source_target_pairs={{0,1},{1,2},{2,3},{3,4},{4,5},{5,6},{6,7},{7,8},{8,9},{9,10},{10,1... | collective-permute-start | bytes 786440 | tf_op jit(solution)/shard_map/ppermute | solution.py:14
  16.9 291.5 %while.15 = (s32[]{:T(128)}, f32[8,128,128]{2,0,1:T(8,128)}, f32[24,128,128]{2,0,1:T(8,128)}, f32[27,128,128]{2,0,1:T(8,128)}, s32[16,16]{1,0:T(8,128)S(1)}, /*i...) while((s32[]{:T(128)}, f32[8,128,128]{2,0,1:T(8,128)}, ...), condition=%wide.region_1.2_spmd.clone, body=%wide.region_0.1_spmd.clone.sunk | while | flops 556112000 | bytes 45096096 | solution.py:114
  37.2 2.9 convolution_add_fusion.2
  41.6 4.0 select_add_fusion.12
  60.0 4.0 select_add_fusion.12
  78.4 4.0 select_add_fusion.12
  96.7 4.0 select_add_fusion.12
  115.1 4.0 select_add_fusion.12
  133.5 4.0 select_add_fusion.12
  151.8 4.0 select_add_fusion.12
  170.2 4.0 select_add_fusion.12
  188.6 4.0 select_add_fusion.12
  206.9 4.0 select_add_fusion.12
  225.3 4.0 select_add_fusion.12
  243.7 4.0 select_add_fusion.12
  262.0 4.0 select_add_fusion.12
  280.4 4.0 select_add_fusion.12
  298.8 4.0 select_add_fusion.12
  314.1 11.6 %collective-permute-done.5 = f32[110592]{0:T(1024)S(1)} collective-permute-done((f32[110592]{0:T(1024)S(1)}, f32[110592]{0:T(1024)S(1)}, u32[]{:S(2)}, u32[]{:S(2)}) %collective-permute-start.5) | collective-permute-done | bytes 442400 | tf_op jit(solution)/shard_map/ppermute | solution.py:29
  325.9 7.5 %collective-permute-done.6 = f32[55296]{0:T(1024)S(1)} collective-permute-done((f32[55296]{0:T(1024)S(1)}, f32[55296]{0:T(1024)S(1)}, u32[]{:S(2)}, u32[]{:S(2)}) %collective-permute-start.6) | collective-permute-done | bytes 221216 | tf_op jit(solution)/shard_map/ppermute | solution.py:29
  333.6 3.6 collective-permute-done.7
  337.3 4.5 %collective-permute-done.8 = f32[13824]{0:T(1024)S(1)} collective-permute-done((f32[13824]{0:T(1024)S(1)}, f32[13824]{0:T(1024)S(1)}, u32[]{:S(2)}, u32[]{:S(2)}) %collective-permute-start.8) | collective-permute-done | bytes 55328 | tf_op jit(solution)/shard_map/ppermute | solution.py:29
  344.8 3.5 collective-permute-done.10
  350.6 4.1 collective-permute-done.11
  357.1 4.1 collective-permute-done.12
  361.4 3.5 collective-permute-done.13
  368.3 4.2 collective-permute-done.15
  377.1 5.4 %collective-permute-done.17 = f32[55296]{0:T(1024)S(1)} collective-permute-done((f32[55296]{0:T(1024)S(1)}, f32[55296]{0:T(1024)S(1)}, u32[]{:S(2)}, u32[]{:S(2)}) %collective-permute-start.17) | collective-permute-done | bytes 221216 | tf_op jit(solution)/shard_map/ppermute | solution.py:32
  383.8 6.0 %collective-permute-done.18 = f32[110592]{0:T(1024)S(1)} collective-permute-done((f32[110592]{0:T(1024)S(1)}, f32[110592]{0:T(1024)S(1)}, u32[]{:S(2)}, u32[]{:S(2)}) %collective-permute-start.18) | collective-permute-done | bytes 442400 | tf_op jit(solution)/shard_map/ppermute | solution.py:32
  389.9 16.3 %collective-permute-start.19 = (f32[221184]{0:T(1024)S(1)}, f32[221184]{0:T(1024)S(1)}, u32[]{:S(2)}, u32[]{:S(2)}) collective-permute-start(f32[221184]{0:T(1024)S(1)} %maximum_select_fusion.1), channel_id=1, source_target_pairs={{0,1},{1,0},{2,3},{3,2},{4,5},{5,4},{6,7},{7,6},{8,9},{9,8},{10,11... | collective-permute-start | bytes 2654216 | tf_op jit(solution)/shard_map/ppermute | solution.py:32
  406.4 7.5 %collective-permute-start.3 = (f32[1024,128]{1,0:T(8,128)S(1)}, f32[1024,128]{1,0:T(8,128)S(1)}, u32[]{:S(2)}, u32[]{:S(2)}) collective-permute-start(f32[1024,128]{1,0:T(8,128)S(1)} %bitcast.82), channel_id=1, source_target_pairs={{0,1},{1,2},{2,3},{3,4},{4,5},{5,6},{6,7},{7,8},{8,9},{9,10},{10,1... | collective-permute-start | bytes 1572872 | tf_op jit(solution)/shard_map/ppermute | solution.py:14
  420.0 9.9 %collective-permute-done.2 = f32[1024,128]{1,0:T(8,128)S(1)} collective-permute-done((f32[1024,128]{1,0:T(8,128)S(1)}, f32[1024,128]{1,0:T(8,128)S(1)}, u32[]{:S(2)}, u32[]{:S(2)}) %collective-permute-start.2) | collective-permute-done | bytes 524320 | tf_op jit(solution)/shard_map/ppermute | solution.py:14
  (458 shorter events, 266.6 us)
Async XLA Ops:
  0.6 16.2 %copy-start.7 = (bf16[1024,128]{1,0:T(8,128)(2,1)S(1)}, bf16[1024,128]{1,0:T(8,128)(2,1)}, u32[]{:S(2)}) copy-start(bf16[1024,128]{1,0:T(8,128)(2,1)} %param.10) | copy-start | bytes 786436
  0.6 15.2 %copy-start.6 = (bf16[1024,128]{1,0:T(8,128)(2,1)S(1)}, bf16[1024,128]{1,0:T(8,128)(2,1)}, u32[]{:S(2)}) copy-start(bf16[1024,128]{1,0:T(8,128)(2,1)} %param.12) | copy-start | bytes 786436
  0.6 16.1 %collective-permute-start.1 = (bf16[1024,128]{1,0:T(8,128)(2,1)}, bf16[1024,128]{1,0:T(8,128)(2,1)S(1)}, u32[]{:S(2)}, u32[]{:S(2)}) collective-permute-start(bf16[1024,128]{1,0:T(8,128)(2,1)} %param.10), channel_id=1, source_target_pairs={{1,0},{2,1},{3,2},{4,3},{5,4},{6,5},{7,6},{8,7},{9,8},{10,9},{11,1... | collective-permute-start | bytes 786440 | tf_op jit(solution)/shard_map/ppermute | solution.py:14
  3.4 13.4 %collective-permute-start = (bf16[1024,128]{1,0:T(8,128)(2,1)}, bf16[1024,128]{1,0:T(8,128)(2,1)S(1)}, u32[]{:S(2)}, u32[]{:S(2)}) collective-permute-start(bf16[1024,128]{1,0:T(8,128)(2,1)} %param.10), channel_id=1, source_target_pairs={{0,1},{1,2},{2,3},{3,4},{4,5},{5,6},{6,7},{7,8},{8,9},{9,10},{10,1... | collective-permute-start | bytes 786440 | tf_op jit(solution)/shard_map/ppermute | solution.py:14
  28.9 3.9 copy-start.4
  47.2 3.9 copy-start.4
  65.6 3.9 copy-start.4
  120.7 3.9 copy-start.4
  139.1 3.9 copy-start.4
  212.5 3.9 copy-start.4
  230.9 3.9 copy-start.4
  286.0 3.9 copy-start.4
  304.4 3.9 copy-start.4
  311.1 2.5 collective-permute-start.4
  313.8 11.9 %collective-permute-start.5 = (f32[110592]{0:T(1024)S(1)}, f32[110592]{0:T(1024)S(1)}, u32[]{:S(2)}, u32[]{:S(2)}) collective-permute-start(f32[110592]{0:T(1024)S(1)} %slice_select_fusion.1), channel_id=1, source_target_pairs={{0,2},{1,3},{2,0},{3,1},{4,6},{5,7},{6,4},{7,5},{8,10},{9,11},{10,... | collective-permute-start | bytes 1327112 | tf_op jit(solution)/shard_map/ppermute | solution.py:29
  325.8 7.6 %collective-permute-start.6 = (f32[55296]{0:T(1024)S(1)}, f32[55296]{0:T(1024)S(1)}, u32[]{:S(2)}, u32[]{:S(2)}) collective-permute-start(f32[55296]{0:T(1024)S(1)} %slice_select_fusion.2), channel_id=1, source_target_pairs={{0,4},{1,5},{2,6},{3,7},{4,0},{5,1},{6,2},{7,3},{8,12},{9,13},{10,... | collective-permute-start | bytes 663560 | tf_op jit(solution)/shard_map/ppermute | solution.py:29
  333.5 3.7 collective-permute-start.7
  337.2 4.6 %collective-permute-start.8 = (f32[13824]{0:T(1024)S(1)}, f32[13824]{0:T(1024)S(1)}, u32[]{:S(2)}, u32[]{:S(2)}) collective-permute-start(f32[13824]{0:T(1024)S(1)} %slice_select_fusion.4), channel_id=1, source_target_pairs={{0,16},{1,17},{2,18},{3,19},{4,20},{5,21},{6,22},{7,23},{8,24},{9,... | collective-permute-start | bytes 165896 | tf_op jit(solution)/shard_map/ppermute | solution.py:29
  341.8 2.8 collective-permute-start.9
  344.7 3.6 collective-permute-start.10
  348.3 6.4 %collective-permute-start.11 = (f32[1728]{0:T(1024)S(1)}, f32[1728]{0:T(1024)S(1)}, u32[]{:S(2)}, u32[]{:S(2)}) collective-permute-start(f32[1728]{0:T(1024)S(1)} %slice_select_fusion.7), channel_id=1, source_target_pairs={{0,128},{1,129},{2,130},{3,131},{4,132},{5,133},{6,134},{7,135},{8... | collective-permute-start | bytes 20744 | tf_op jit(solution)/shard_map/ppermute | solution.py:29
  354.8 51.4 %copy-start.2 = (f32[24,128,128]{2,0,1:T(8,128)S(1)}, f32[24,128,128]{2,0,1:T(8,128)}, u32[]{:S(2)}) copy-start(f32[24,128,128]{2,0,1:T(8,128)} %get-tuple-element.73) | copy-start | bytes 4718596
  354.8 6.4 %collective-permute-start.12 = (f32[1728]{0:T(1024)S(1)}, f32[1728]{0:T(1024)S(1)}, u32[]{:S(2)}, u32[]{:S(2)}) collective-permute-start(f32[1728]{0:T(1024)S(1)} %select_add_fusion.9), channel_id=1, source_target_pairs={{0,128},{1,129},{2,130},{3,131},{4,132},{5,133},{6,134},{7,135},{8... | collective-permute-start | bytes 20744 | tf_op jit(solution)/shard_map/ppermute | solution.py:32
  361.4 3.5 collective-permute-start.13
  364.9 2.9 collective-permute-start.14
  367.8 4.6 %collective-permute-start.15 = (f32[13824]{0:T(1024)S(1)}, f32[13824]{0:T(1024)S(1)}, u32[]{:S(2)}, u32[]{:S(2)}) collective-permute-start(f32[13824]{0:T(1024)S(1)} %maximum_select_fusion.5), channel_id=1, source_target_pairs={{0,16},{1,17},{2,18},{3,19},{4,20},{5,21},{6,22},{7,23},{8,24},{9,... | collective-permute-start | bytes 165896 | tf_op jit(solution)/shard_map/ppermute | solution.py:32
  372.4 3.7 collective-permute-start.16
  376.1 6.4 %collective-permute-start.17 = (f32[55296]{0:T(1024)S(1)}, f32[55296]{0:T(1024)S(1)}, u32[]{:S(2)}, u32[]{:S(2)}) collective-permute-start(f32[55296]{0:T(1024)S(1)} %maximum_select_fusion.3), channel_id=1, source_target_pairs={{0,4},{1,5},{2,6},{3,7},{4,0},{5,1},{6,2},{7,3},{8,12},{9,13},{10,... | collective-permute-start | bytes 663560 | tf_op jit(solution)/shard_map/ppermute | solution.py:32
  382.5 7.2 %collective-permute-start.18 = (f32[110592]{0:T(1024)S(1)}, f32[110592]{0:T(1024)S(1)}, u32[]{:S(2)}, u32[]{:S(2)}) collective-permute-start(f32[110592]{0:T(1024)S(1)} %maximum_select_fusion.2), channel_id=1, source_target_pairs={{0,2},{1,3},{2,0},{3,1},{4,6},{5,7},{6,4},{7,5},{8,10},{9,11},{10,... | collective-permute-start | bytes 1327112 | tf_op jit(solution)/shard_map/ppermute | solution.py:32
  389.9 40.9 %collective-permute-start.19 = (f32[221184]{0:T(1024)S(1)}, f32[221184]{0:T(1024)S(1)}, u32[]{:S(2)}, u32[]{:S(2)}) collective-permute-start(f32[221184]{0:T(1024)S(1)} %maximum_select_fusion.1), channel_id=1, source_target_pairs={{0,1},{1,0},{2,3},{3,2},{4,5},{5,4},{6,7},{7,6},{8,9},{9,8},{10,11... | collective-permute-start | bytes 2654216 | tf_op jit(solution)/shard_map/ppermute | solution.py:32
  406.4 13.6 %collective-permute-start.3 = (f32[1024,128]{1,0:T(8,128)S(1)}, f32[1024,128]{1,0:T(8,128)S(1)}, u32[]{:S(2)}, u32[]{:S(2)}) collective-permute-start(f32[1024,128]{1,0:T(8,128)S(1)} %bitcast.82), channel_id=1, source_target_pairs={{0,1},{1,2},{2,3},{3,4},{4,5},{5,6},{6,7},{7,8},{8,9},{9,10},{10,1... | collective-permute-start | bytes 1572872 | tf_op jit(solution)/shard_map/ppermute | solution.py:14
  414.0 15.9 %collective-permute-start.2 = (f32[1024,128]{1,0:T(8,128)S(1)}, f32[1024,128]{1,0:T(8,128)S(1)}, u32[]{:S(2)}, u32[]{:S(2)}) collective-permute-start(f32[1024,128]{1,0:T(8,128)S(1)} %bitcast.83), channel_id=1, source_target_pairs={{1,0},{2,1},{3,2},{4,3},{5,4},{6,5},{7,6},{8,7},{9,8},{10,9},{11,1... | collective-permute-start | bytes 1572872 | tf_op jit(solution)/shard_map/ppermute | solution.py:14
  (71 other events, 183.1 us)

commit v2 on v1

--- a/solution.py
+++ b/solution.py
@@ -3,6 +3,8 @@
 import jax
 import jax.numpy as jnp
 from jax import lax
+from jax.experimental import pallas as pl
+from jax.experimental.pallas import tpu as pltpu
 from jax.sharding import PartitionSpec as P
 
 BLK = 128
@@ -47,72 +49,62 @@
     return ((row_map[..., None] == columns[None, None, :]) & usable[..., None]).astype(dtype)
 
 
+def sweep_kernel(offsets, blocks_at, targets, live, window_ref, weights_ref, cot_ref, rows_ref,
+                 out_ref, ret_ref, grad_ref):
+    out_ref[...] = jnp.zeros(out_ref.shape, out_ref.dtype)
+    ret_ref[...] = jnp.zeros(ret_ref.shape, ret_ref.dtype)
+    grad_ref[...] = jnp.zeros(grad_ref.shape, grad_ref.dtype)
+    source_rows = lax.broadcasted_iota(jnp.int32, (BLK, BLK), 0)
+    lhs_rows = (((0,), (0,)), ((), ()))
+    rhs_rows = (((1,), (1,)), ((), ()))
+
+    def advance(p, carry):
+        kernel_at = offsets[p]
+        block_at = blocks_at[p]
+        target_at = targets[p]
+        picks = (rows_ref[p] == source_rows).astype(jnp.bfloat16)
+        chosen = weights_ref[kernel_at]
+        grad_out = cot_ref[target_at]
+        gathered = lax.dot_general(
+            picks, window_ref[block_at], lhs_rows, preferred_element_type=jnp.float32
+        ).astype(jnp.bfloat16)
+        moved = jnp.dot(picks, grad_out, preferred_element_type=jnp.float32).astype(jnp.bfloat16)
+        out_ref[target_at] += jnp.dot(gathered, chosen, preferred_element_type=jnp.float32)
+        ret_ref[block_at] += lax.dot_general(
+            moved, chosen, rhs_rows, preferred_element_type=jnp.float32
+        )
+        grad_ref[kernel_at] += lax.dot_general(
+            gathered, grad_out, lhs_rows, preferred_element_type=jnp.float32
+        )
+        return carry
+
+    lax.fori_loop(0, live[0], advance, 0)
+
+
 def forward_sweep(window, weights, grad_blocks, rulebook, myself, blocks):
     g_off_all, source_all, target_all, row_map_all, live_count = rulebook
     channels = window.shape[1]
     kernel_count = weights.shape[0]
+    pair_slots = g_off_all.shape[0]
     window_blocks = window.reshape(3 * blocks, BLK, channels)
-    group_size = 16
-    positions = jnp.arange(g_off_all.shape[0], dtype=jnp.int32)
     relative = source_all // blocks - myself
-    window_block = (relative + 1) * blocks + source_all % blocks
-    pieces = (
-        grouped(g_off_all, group_size),
-        grouped(window_block, group_size),
-        grouped(target_all, group_size),
-        grouped(row_map_all, group_size),
-        grouped(positions, group_size),
-    )
-    highest = lax.Precision.HIGHEST
-
-    def advance(state_in, item_now):
-        out_sum, returned_sum, grad_sum = state_in
-        g_off, g_block, g_target, row_map, g_pos = item_now
-        usable = (row_map >= 0) & (g_pos < live_count[0])[:, None]
-        perm = permuter(row_map, usable, jnp.bfloat16)
-        block_pick = picker(g_block, 3 * blocks, jnp.bfloat16)
-        rows_in = jnp.einsum(
-            "gk,kbc->gbc", block_pick, window_blocks, preferred_element_type=jnp.float32
-        ).astype(jnp.bfloat16)
-        gathered = jnp.einsum(
-            "grs,gsc->grc", perm, rows_in, preferred_element_type=jnp.float32
-        ).astype(jnp.bfloat16)
-        off_pick = picker(g_off, kernel_count, jnp.bfloat16)
-        chosen = jnp.einsum(
-            "gk,kcd->gcd", off_pick, weights, preferred_element_type=jnp.float32
-        ).astype(jnp.bfloat16)
-        product = jnp.einsum("gbc,gcd->gbd", gathered, chosen, preferred_element_type=jnp.float32)
-        target_pick = picker(g_target, blocks, jnp.float32)
-        out_sum = out_sum + jnp.einsum("gt,gbd->tbd", target_pick, product, precision=highest)
-        grad_out = jnp.einsum(
-            "gt,tbd->gbd",
-            target_pick.astype(jnp.bfloat16),
-            grad_blocks,
-            preferred_element_type=jnp.float32,
-        ).astype(jnp.bfloat16)
-        pair_grad = jnp.einsum(
-            "gbc,gbd->gcd", gathered, grad_out, preferred_element_type=jnp.float32
-        )
-        grad_sum = grad_sum + jnp.einsum(
-            "gk,gcd->kcd", off_pick.astype(jnp.float32), pair_grad, precision=highest
-        )
-        moved = jnp.einsum(
-            "grs,grd->gsd", perm, grad_out, preferred_element_type=jnp.float32
-        ).astype(jnp.bfloat16)
-        returned = jnp.einsum("gsd,gcd->gsc", moved, chosen, preferred_element_type=jnp.float32)
-        returned_sum = returned_sum + jnp.einsum(
-            "gk,gsc->ksc", block_pick.astype(jnp.float32), returned, precision=highest
-        )
-        return ((out_sum, returned_sum, grad_sum), None)
-
-    back_blocks = 3 * blocks
-    start = (
-        jnp.zeros((blocks, BLK, channels), jnp.float32),
-        jnp.zeros((back_blocks, BLK, channels), jnp.float32),
-        jnp.zeros((kernel_count, channels, channels), jnp.float32),
-    )
-    (out_sum, returned_sum, grad_sum), _ = lax.scan(advance, start, pieces)
-    return (out_sum, returned_sum, grad_sum)
+    window_block = jnp.clip((relative + 1) * blocks + source_all % blocks, 0, 3 * blocks - 1)
+    offsets = jnp.clip(g_off_all, 0, kernel_count - 1)
+    targets = jnp.clip(target_all, 0, blocks - 1)
+    live = jnp.clip(live_count, 0, pair_slots)
+    smem = pl.BlockSpec(memory_space=pltpu.SMEM)
+    vmem = pl.BlockSpec(memory_space=pltpu.VMEM)
+    return pl.pallas_call(
+        sweep_kernel,
+        out_shape=(
+            jax.ShapeDtypeStruct((blocks, BLK, channels), jnp.float32),
+            jax.ShapeDtypeStruct((3 * blocks, BLK, channels), jnp.float32),
+            jax.ShapeDtypeStruct((kernel_count, channels, channels), jnp.float32),
+        ),
+        in_specs=[smem, smem, smem, smem, vmem, vmem, vmem, vmem],
+        out_specs=(vmem, vmem, vmem),
+    )(offsets, window_block, targets, live, window_blocks, weights, grad_blocks,
+      row_map_all.reshape(pair_slots, 1, BLK))
 
 
 def on_device(

time: 435 us -> 226 us (0.52)
  matrix products: 218 us -> 0 us
  Pallas kernels: 0 us -> 73.2 us
  local copies, waits for them, and re-layouts: 54.6 us -> 0.15 us
  starting transfers between devices: 46 us -> 67.4 us
  other arithmetic: 30.6 us -> 9.81 us
  waiting for transfers between devices: 80.7 us -> 73.5 us
    dot_general x160 -> x0, matrix products: 218 us -> none  [the longest x16 62.5 us: advance(): jnp.einsum('gk,gsc->ksc', block_pick.astype(jnp.float32), returned, preci...]
    pallas_call x0 -> x1, Pallas kernels: none -> 73.2 us  [forward_sweep(): pl.pallas_call(sweep_kernel, out_shape=(jax.ShapeDtypeStruct((blocks, BLK...]
    while x160 -> x0, local copies, waits for them, and re-layouts: 41.5 us -> none
    ppermute x8, starting transfers between devices: 3.12 us -> 18.8 us  [summed_everywhere(): lax.ppermute(send, axis, [(i, i ^ mask) for i in range(count)])]
    and x16 -> x0, other arithmetic: 12.4 us -> none  [advance(): usable = (row_map >= 0) & (g_pos < live_count[0])[:, None]]
    lt x16 -> x0, other arithmetic: 10.6 us -> none  [advance(): usable = (row_map >= 0) & (g_pos < live_count[0])[:, None]]
    convert_element_type x17 -> x0, local copies, waits for them, and re-layouts: 8.22 us -> none  [the longest x16 7.47 us: advance(): chosen = jnp.einsum('gk,kcd->gcd', off_pick, weights, preferred_element_t...]
    ppermute x8, waiting for transfers between devices: 28.7 us -> 23 us  [summed_everywhere(): other = lax.ppermute(flat, axis, [(i, i ^ mask) for i in range(count)])]
  transfers between devices with their start and end apart: 20 -> 20, of which waited for: 17 -> 18; matrix products, arithmetic and copies ran while one was open for 2% -> 2% of each run, Pallas kernels for 0% -> 0%
where the time goes in v2:
time: 226 us
  waiting for transfers between devices  73.5 us (33%)
  Pallas kernels  73.2 us (32%)
  starting transfers between devices  67.4 us (30%)
  other arithmetic  9.81 us (4%)
    pallas_call x1, Pallas kernels, forward_sweep(): pl.pallas_call(sweep_kernel, out_shape=(jax.ShapeDtypeStruct((blocks, BLK...  73.2 us
    ppermute x8, waiting for transfers between devices, summed_everywhere(): lax.ppermute(send, axis, [(i, i ^ mask) for i in range(count)])  36.8 us
    ppermute x8, starting transfers between devices, summed_everywhere(): other = lax.ppermute(flat, axis, [(i, i ^ mask) for i in range(count)])  26.6 us
    ppermute x8, waiting for transfers between devices, summed_everywhere(): other = lax.ppermute(flat, axis, [(i, i ^ mask) for i in range(count)])  23 us
    ppermute x4, starting transfers between devices, passed_along(): lax.ppermute(value, axis, [(source, source + steps) for source in range(l...  22 us
    ppermute x8, starting transfers between devices, summed_everywhere(): lax.ppermute(send, axis, [(i, i ^ mask) for i in range(count)])  18.8 us
    ppermute x4, waiting for transfers between devices, passed_along(): lax.ppermute(value, axis, [(source, source + steps) for source in range(l...  13.7 us
  transfers between devices with their start and end apart: 20, of which 18 were waited for; matrix products, arithmetic and copies ran while one was open for 2% of the time, Pallas kernels for 0%

profile of v2, /device:TPU:127, one launch (start us, length us, event | category | flops | bytes accessed | tf_op | source)
XLA Modules:
  0.0 225.6 jit_solution(17751693234982796073)
XLA Ops:
  0.6 2.6 %collective-permute-start.1 = (bf16[1024,128]{1,0:T(8,128)(2,1)}, bf16[1024,128]{1,0:T(8,128)(2,1)S(1)}, u32[]{:S(2)}, u32[]{:S(2)}) collective-permute-start(bf16[1024,128]{1,0:T(8,128)(2,1)} %param.8), channel_id=1, source_target_pairs={{1,0},{2,1},{3,2},{4,3},{5,4},{6,5},{7,6},{8,7},{9,8},{10,9},{11,1... | collective-permute-start | bytes 786440 | tf_op jit(solution)/shard_map/ppermute | solution.py:16
  3.2 8.4 %collective-permute-start = (bf16[1024,128]{1,0:T(8,128)(2,1)}, bf16[1024,128]{1,0:T(8,128)(2,1)S(1)}, u32[]{:S(2)}, u32[]{:S(2)}) collective-permute-start(bf16[1024,128]{1,0:T(8,128)(2,1)} %param.8), channel_id=1, source_target_pairs={{0,1},{1,2},{2,3},{3,4},{4,5},{5,6},{6,7},{7,8},{8,9},{9,10},{10,1... | collective-permute-start | bytes 786440 | tf_op jit(solution)/shard_map/ppermute | solution.py:16
  11.6 1.2 broadcast_clamp_fusion.1.offsets
  13.5 1.3 fusion.3
  15.3 1.9 pad_maximum_fusion
  17.1 73.2 %shard_map.103 = (f32[8,128,128]{2,1,0:T(8,128)}, f32[24,128,128]{2,1,0:T(8,128)}, f32[27,128,128]{2,1,0:T(8,128)}) custom-call(s32[256]{0:T(256)} %broadcast_clamp_fusion.1.offsets, s32[256]{0:T(256)} %get-tuple-element.12.blocks_at, s32[256]{0:T(256)} %get-tuple-element.13.targets, s32[1]{0:T(128)S(6)} %min.29.live, bf16[24,128,128]{2,1,0:T(8,128)(2,1)} %bitcast.16, ...), custom_call_target="tpu_custom_call" | custom-call | tf_op jit(solution)/shard_map/pallas_call | solution.py:97
  90.3 1.6 broadcast_multiply_fusion
  92.1 2.4 %collective-permute-done.4 = f32[221184]{0:T(1024)S(1)} collective-permute-done((f32[221184]{0:T(1024)S(1)}, f32[221184]{0:T(1024)S(1)}, u32[]{:S(2)}, u32[]{:S(2)}) %collective-permute-start.4) | collective-permute-done | bytes 884768 | tf_op jit(solution)/shard_map/ppermute | solution.py:31
  94.8 11.6 %collective-permute-done.5 = f32[110592]{0:T(1024)S(1)} collective-permute-done((f32[110592]{0:T(1024)S(1)}, f32[110592]{0:T(1024)S(1)}, u32[]{:S(2)}, u32[]{:S(2)}) %collective-permute-start.5) | collective-permute-done | bytes 442400 | tf_op jit(solution)/shard_map/ppermute | solution.py:31
  106.6 7.5 %collective-permute-done.6 = f32[55296]{0:T(1024)S(1)} collective-permute-done((f32[55296]{0:T(1024)S(1)}, f32[55296]{0:T(1024)S(1)}, u32[]{:S(2)}, u32[]{:S(2)}) %collective-permute-start.6) | collective-permute-done | bytes 221216 | tf_op jit(solution)/shard_map/ppermute | solution.py:31
  114.3 3.6 %collective-permute-done.7 = f32[27648]{0:T(1024)S(1)} collective-permute-done((f32[27648]{0:T(1024)S(1)}, f32[27648]{0:T(1024)S(1)}, u32[]{:S(2)}, u32[]{:S(2)}) %collective-permute-start.7) | collective-permute-done | bytes 110624 | tf_op jit(solution)/shard_map/ppermute | solution.py:31
  118.0 4.5 %collective-permute-done.8 = f32[13824]{0:T(1024)S(1)} collective-permute-done((f32[13824]{0:T(1024)S(1)}, f32[13824]{0:T(1024)S(1)}, u32[]{:S(2)}, u32[]{:S(2)}) %collective-permute-start.8) | collective-permute-done | bytes 55328 | tf_op jit(solution)/shard_map/ppermute | solution.py:31
  122.6 2.7 %collective-permute-done.9 = f32[6912]{0:T(1024)S(1)} collective-permute-done((f32[6912]{0:T(1024)S(1)}, f32[6912]{0:T(1024)S(1)}, u32[]{:S(2)}, u32[]{:S(2)}) %collective-permute-start.9) | collective-permute-done | bytes 27680 | tf_op jit(solution)/shard_map/ppermute | solution.py:31
  125.5 3.5 %collective-permute-done.10 = f32[3456]{0:T(1024)S(1)} collective-permute-done((f32[3456]{0:T(1024)S(1)}, f32[3456]{0:T(1024)S(1)}, u32[]{:S(2)}, u32[]{:S(2)}) %collective-permute-start.10) | collective-permute-done | bytes 13856 | tf_op jit(solution)/shard_map/ppermute | solution.py:31
  129.0 18.2 %collective-permute-start.11 = (f32[1728]{0:T(1024)S(1)}, f32[1728]{0:T(1024)S(1)}, u32[]{:S(2)}, u32[]{:S(2)}) collective-permute-start(f32[1728]{0:T(1024)S(1)} %slice_select_fusion.7), channel_id=1, source_target_pairs={{0,128},{1,129},{2,130},{3,131},{4,132},{5,133},{6,134},{7,135},{8... | collective-permute-start | bytes 20744 | tf_op jit(solution)/shard_map/ppermute | solution.py:31
  148.3 5.4 %collective-permute-start.12 = (f32[1728]{0:T(1024)S(1)}, f32[1728]{0:T(1024)S(1)}, u32[]{:S(2)}, u32[]{:S(2)}) collective-permute-start(f32[1728]{0:T(1024)S(1)} %select_add_fusion.7), channel_id=1, source_target_pairs={{0,128},{1,129},{2,130},{3,131},{4,132},{5,133},{6,134},{7,135},{8... | collective-permute-start | bytes 20744 | tf_op jit(solution)/shard_map/ppermute | solution.py:34
  153.7 1.0 collective-permute-done.12
  154.9 3.5 %collective-permute-done.13 = f32[3456]{0:T(1024)S(1)} collective-permute-done((f32[3456]{0:T(1024)S(1)}, f32[3456]{0:T(1024)S(1)}, u32[]{:S(2)}, u32[]{:S(2)}) %collective-permute-start.13) | collective-permute-done | bytes 13856 | tf_op jit(solution)/shard_map/ppermute | solution.py:34
  158.4 1.7 collective-permute-start.14
  160.1 1.6 collective-permute-done.14
  161.9 4.4 %collective-permute-done.15 = f32[13824]{0:T(1024)S(1)} collective-permute-done((f32[13824]{0:T(1024)S(1)}, f32[13824]{0:T(1024)S(1)}, u32[]{:S(2)}, u32[]{:S(2)}) %collective-permute-start.15) | collective-permute-done | bytes 55328 | tf_op jit(solution)/shard_map/ppermute | solution.py:34
  166.3 1.5 collective-permute-start.16
  167.8 2.2 collective-permute-done.16
  170.0 2.9 %collective-permute-start.17 = (f32[55296]{0:T(1024)S(1)}, f32[55296]{0:T(1024)S(1)}, u32[]{:S(2)}, u32[]{:S(2)}) collective-permute-start(f32[55296]{0:T(1024)S(1)} %maximum_select_fusion.3), channel_id=1, source_target_pairs={{0,4},{1,5},{2,6},{3,7},{4,0},{5,1},{6,2},{7,3},{8,12},{9,13},{10,... | collective-permute-start | bytes 663560 | tf_op jit(solution)/shard_map/ppermute | solution.py:34
  172.9 3.6 %collective-permute-done.17 = f32[55296]{0:T(1024)S(1)} collective-permute-done((f32[55296]{0:T(1024)S(1)}, f32[55296]{0:T(1024)S(1)}, u32[]{:S(2)}, u32[]{:S(2)}) %collective-permute-start.17) | collective-permute-done | bytes 221216 | tf_op jit(solution)/shard_map/ppermute | solution.py:34
  177.0 6.8 %collective-permute-done.18 = f32[110592]{0:T(1024)S(1)} collective-permute-done((f32[110592]{0:T(1024)S(1)}, f32[110592]{0:T(1024)S(1)}, u32[]{:S(2)}, u32[]{:S(2)}) %collective-permute-start.18) | collective-permute-done | bytes 442400 | tf_op jit(solution)/shard_map/ppermute | solution.py:34
  183.8 14.4 %collective-permute-start.19 = (f32[221184]{0:T(1024)S(1)}, f32[221184]{0:T(1024)S(1)}, u32[]{:S(2)}, u32[]{:S(2)}) collective-permute-start(f32[221184]{0:T(1024)S(1)} %maximum_select_fusion.1), channel_id=1, source_target_pairs={{0,1},{1,0},{2,3},{3,2},{4,5},{5,4},{6,7},{7,6},{8,9},{9,8},{10,11... | collective-permute-start | bytes 2654216 | tf_op jit(solution)/shard_map/ppermute | solution.py:34
  198.4 9.1 %collective-permute-start.3 = (f32[1024,128]{1,0:T(8,128)S(1)}, f32[1024,128]{1,0:T(8,128)S(1)}, u32[]{:S(2)}, u32[]{:S(2)}) collective-permute-start(f32[1024,128]{1,0:T(8,128)S(1)} %bitcast.19), channel_id=1, source_target_pairs={{0,1},{1,2},{2,3},{3,4},{4,5},{5,6},{6,7},{7,8},{8,9},{9,10},{10,1... | collective-permute-start | bytes 1572872 | tf_op jit(solution)/shard_map/ppermute | solution.py:16
  207.5 1.9 collective-permute-start.2
  210.1 3.4 %collective-permute-done.3 = f32[1024,128]{1,0:T(8,128)S(1)} collective-permute-done((f32[1024,128]{1,0:T(8,128)S(1)}, f32[1024,128]{1,0:T(8,128)S(1)}, u32[]{:S(2)}, u32[]{:S(2)}) %collective-permute-start.3) | collective-permute-done | bytes 524320 | tf_op jit(solution)/shard_map/ppermute | solution.py:16
  213.6 9.8 %collective-permute-done.2 = f32[1024,128]{1,0:T(8,128)S(1)} collective-permute-done((f32[1024,128]{1,0:T(8,128)S(1)}, f32[1024,128]{1,0:T(8,128)S(1)}, u32[]{:S(2)}, u32[]{:S(2)}) %collective-permute-start.2) | collective-permute-done | bytes 524320 | tf_op jit(solution)/shard_map/ppermute | solution.py:16
  224.2 1.4 maximum_select_fusion
  (44 shorter events, 5.4 us)
Async XLA Ops:
  0.6 14.2 %collective-permute-start.1 = (bf16[1024,128]{1,0:T(8,128)(2,1)}, bf16[1024,128]{1,0:T(8,128)(2,1)S(1)}, u32[]{:S(2)}, u32[]{:S(2)}) collective-permute-start(bf16[1024,128]{1,0:T(8,128)(2,1)} %param.8), channel_id=1, source_target_pairs={{1,0},{2,1},{3,2},{4,3},{5,4},{6,5},{7,6},{8,7},{9,8},{10,9},{11,1... | collective-permute-start | bytes 786440 | tf_op jit(solution)/shard_map/ppermute | solution.py:16
  3.2 12.0 %collective-permute-start = (bf16[1024,128]{1,0:T(8,128)(2,1)}, bf16[1024,128]{1,0:T(8,128)(2,1)S(1)}, u32[]{:S(2)}, u32[]{:S(2)}) collective-permute-start(bf16[1024,128]{1,0:T(8,128)(2,1)} %param.8), channel_id=1, source_target_pairs={{0,1},{1,2},{2,3},{3,4},{4,5},{5,6},{6,7},{7,8},{8,9},{9,10},{10,1... | collective-permute-start | bytes 786440 | tf_op jit(solution)/shard_map/ppermute | solution.py:16
  92.0 2.5 %collective-permute-start.4 = (f32[221184]{0:T(1024)S(1)}, f32[221184]{0:T(1024)S(1)}, u32[]{:S(2)}, u32[]{:S(2)}) collective-permute-start(f32[221184]{0:T(1024)S(1)} %slice_select_fusion), channel_id=1, source_target_pairs={{0,1},{1,0},{2,3},{3,2},{4,5},{5,4},{6,7},{7,6},{8,9},{9,8},{10,11... | collective-permute-start | bytes 2654216 | tf_op jit(solution)/shard_map/ppermute | solution.py:31
  94.7 11.7 %collective-permute-start.5 = (f32[110592]{0:T(1024)S(1)}, f32[110592]{0:T(1024)S(1)}, u32[]{:S(2)}, u32[]{:S(2)}) collective-permute-start(f32[110592]{0:T(1024)S(1)} %slice_select_fusion.1), channel_id=1, source_target_pairs={{0,2},{1,3},{2,0},{3,1},{4,6},{5,7},{6,4},{7,5},{8,10},{9,11},{10,... | collective-permute-start | bytes 1327112 | tf_op jit(solution)/shard_map/ppermute | solution.py:31
  106.5 7.6 %collective-permute-start.6 = (f32[55296]{0:T(1024)S(1)}, f32[55296]{0:T(1024)S(1)}, u32[]{:S(2)}, u32[]{:S(2)}) collective-permute-start(f32[55296]{0:T(1024)S(1)} %slice_select_fusion.2), channel_id=1, source_target_pairs={{0,4},{1,5},{2,6},{3,7},{4,0},{5,1},{6,2},{7,3},{8,12},{9,13},{10,... | collective-permute-start | bytes 663560 | tf_op jit(solution)/shard_map/ppermute | solution.py:31
  114.2 3.7 %collective-permute-start.7 = (f32[27648]{0:T(1024)S(1)}, f32[27648]{0:T(1024)S(1)}, u32[]{:S(2)}, u32[]{:S(2)}) collective-permute-start(f32[27648]{0:T(1024)S(1)} %slice_select_fusion.3), channel_id=1, source_target_pairs={{0,8},{1,9},{2,10},{3,11},{4,12},{5,13},{6,14},{7,15},{8,0},{9,1},... | collective-permute-start | bytes 331784 | tf_op jit(solution)/shard_map/ppermute | solution.py:31
  117.9 4.6 %collective-permute-start.8 = (f32[13824]{0:T(1024)S(1)}, f32[13824]{0:T(1024)S(1)}, u32[]{:S(2)}, u32[]{:S(2)}) collective-permute-start(f32[13824]{0:T(1024)S(1)} %slice_select_fusion.4), channel_id=1, source_target_pairs={{0,16},{1,17},{2,18},{3,19},{4,20},{5,21},{6,22},{7,23},{8,24},{9,... | collective-permute-start | bytes 165896 | tf_op jit(solution)/shard_map/ppermute | solution.py:31
  122.5 2.8 %collective-permute-start.9 = (f32[6912]{0:T(1024)S(1)}, f32[6912]{0:T(1024)S(1)}, u32[]{:S(2)}, u32[]{:S(2)}) collective-permute-start(f32[6912]{0:T(1024)S(1)} %slice_select_fusion.5), channel_id=1, source_target_pairs={{0,32},{1,33},{2,34},{3,35},{4,36},{5,37},{6,38},{7,39},{8,40},{9,... | collective-permute-start | bytes 82952 | tf_op jit(solution)/shard_map/ppermute | solution.py:31
  125.4 3.6 %collective-permute-start.10 = (f32[3456]{0:T(1024)S(1)}, f32[3456]{0:T(1024)S(1)}, u32[]{:S(2)}, u32[]{:S(2)}) collective-permute-start(f32[3456]{0:T(1024)S(1)} %slice_select_fusion.6), channel_id=1, source_target_pairs={{0,64},{1,65},{2,66},{3,67},{4,68},{5,69},{6,70},{7,71},{8,72},{9,... | collective-permute-start | bytes 41480 | tf_op jit(solution)/shard_map/ppermute | solution.py:31
  129.0 19.2 %collective-permute-start.11 = (f32[1728]{0:T(1024)S(1)}, f32[1728]{0:T(1024)S(1)}, u32[]{:S(2)}, u32[]{:S(2)}) collective-permute-start(f32[1728]{0:T(1024)S(1)} %slice_select_fusion.7), channel_id=1, source_target_pairs={{0,128},{1,129},{2,130},{3,131},{4,132},{5,133},{6,134},{7,135},{8... | collective-permute-start | bytes 20744 | tf_op jit(solution)/shard_map/ppermute | solution.py:31
  148.3 49.9 %copy-start = (f32[24,128,128]{2,1,0:T(8,128)S(1)}, f32[24,128,128]{2,1,0:T(8,128)}, u32[]{:S(2)}) copy-start(f32[24,128,128]{2,1,0:T(8,128)} %get-tuple-element.7) | copy-start | bytes 4718596
  148.3 6.4 %collective-permute-start.12 = (f32[1728]{0:T(1024)S(1)}, f32[1728]{0:T(1024)S(1)}, u32[]{:S(2)}, u32[]{:S(2)}) collective-permute-start(f32[1728]{0:T(1024)S(1)} %select_add_fusion.7), channel_id=1, source_target_pairs={{0,128},{1,129},{2,130},{3,131},{4,132},{5,133},{6,134},{7,135},{8... | collective-permute-start | bytes 20744 | tf_op jit(solution)/shard_map/ppermute | solution.py:34
  154.9 3.5 %collective-permute-start.13 = (f32[3456]{0:T(1024)S(1)}, f32[3456]{0:T(1024)S(1)}, u32[]{:S(2)}, u32[]{:S(2)}) collective-permute-start(f32[3456]{0:T(1024)S(1)} %maximum_select_fusion.7), channel_id=1, source_target_pairs={{0,64},{1,65},{2,66},{3,67},{4,68},{5,69},{6,70},{7,71},{8,72},{9,... | collective-permute-start | bytes 41480 | tf_op jit(solution)/shard_map/ppermute | solution.py:34
  158.4 3.3 %collective-permute-start.14 = (f32[6912]{0:T(1024)S(1)}, f32[6912]{0:T(1024)S(1)}, u32[]{:S(2)}, u32[]{:S(2)}) collective-permute-start(f32[6912]{0:T(1024)S(1)} %maximum_select_fusion.6), channel_id=1, source_target_pairs={{0,32},{1,33},{2,34},{3,35},{4,36},{5,37},{6,38},{7,39},{8,40},{9,... | collective-permute-start | bytes 82952 | tf_op jit(solution)/shard_map/ppermute | solution.py:34
  161.7 4.6 %collective-permute-start.15 = (f32[13824]{0:T(1024)S(1)}, f32[13824]{0:T(1024)S(1)}, u32[]{:S(2)}, u32[]{:S(2)}) collective-permute-start(f32[13824]{0:T(1024)S(1)} %maximum_select_fusion.5), channel_id=1, source_target_pairs={{0,16},{1,17},{2,18},{3,19},{4,20},{5,21},{6,22},{7,23},{8,24},{9,... | collective-permute-start | bytes 165896 | tf_op jit(solution)/shard_map/ppermute | solution.py:34
  166.3 3.7 %collective-permute-start.16 = (f32[27648]{0:T(1024)S(1)}, f32[27648]{0:T(1024)S(1)}, u32[]{:S(2)}, u32[]{:S(2)}) collective-permute-start(f32[27648]{0:T(1024)S(1)} %maximum_select_fusion.4), channel_id=1, source_target_pairs={{0,8},{1,9},{2,10},{3,11},{4,12},{5,13},{6,14},{7,15},{8,0},{9,1},... | collective-permute-start | bytes 331784 | tf_op jit(solution)/shard_map/ppermute | solution.py:34
  170.0 6.5 %collective-permute-start.17 = (f32[55296]{0:T(1024)S(1)}, f32[55296]{0:T(1024)S(1)}, u32[]{:S(2)}, u32[]{:S(2)}) collective-permute-start(f32[55296]{0:T(1024)S(1)} %maximum_select_fusion.3), channel_id=1, source_target_pairs={{0,4},{1,5},{2,6},{3,7},{4,0},{5,1},{6,2},{7,3},{8,12},{9,13},{10,... | collective-permute-start | bytes 663560 | tf_op jit(solution)/shard_map/ppermute | solution.py:34
  176.5 7.2 %collective-permute-start.18 = (f32[110592]{0:T(1024)S(1)}, f32[110592]{0:T(1024)S(1)}, u32[]{:S(2)}, u32[]{:S(2)}) collective-permute-start(f32[110592]{0:T(1024)S(1)} %maximum_select_fusion.2), channel_id=1, source_target_pairs={{0,2},{1,3},{2,0},{3,1},{4,6},{5,7},{6,4},{7,5},{8,10},{9,11},{10,... | collective-permute-start | bytes 1327112 | tf_op jit(solution)/shard_map/ppermute | solution.py:34
  183.8 25.6 %copy-start.1 = (f32[8,128,128]{2,1,0:T(8,128)S(1)}, f32[8,128,128]{2,1,0:T(8,128)}, u32[]{:S(2)}) copy-start(f32[8,128,128]{2,1,0:T(8,128)} %get-tuple-element.6) | copy-start | bytes 1572868
  183.8 40.3 %collective-permute-start.19 = (f32[221184]{0:T(1024)S(1)}, f32[221184]{0:T(1024)S(1)}, u32[]{:S(2)}, u32[]{:S(2)}) collective-permute-start(f32[221184]{0:T(1024)S(1)} %maximum_select_fusion.1), channel_id=1, source_target_pairs={{0,1},{1,0},{2,3},{3,2},{4,5},{5,4},{6,7},{7,6},{8,9},{9,8},{10,11... | collective-permute-start | bytes 2654216 | tf_op jit(solution)/shard_map/ppermute | solution.py:34
  198.4 15.2 %collective-permute-start.3 = (f32[1024,128]{1,0:T(8,128)S(1)}, f32[1024,128]{1,0:T(8,128)S(1)}, u32[]{:S(2)}, u32[]{:S(2)}) collective-permute-start(f32[1024,128]{1,0:T(8,128)S(1)} %bitcast.19), channel_id=1, source_target_pairs={{0,1},{1,2},{2,3},{3,4},{4,5},{5,6},{6,7},{7,8},{8,9},{9,10},{10,1... | collective-permute-start | bytes 1572872 | tf_op jit(solution)/shard_map/ppermute | solution.py:16
  207.5 15.9 %collective-permute-start.2 = (f32[1024,128]{1,0:T(8,128)S(1)}, f32[1024,128]{1,0:T(8,128)S(1)}, u32[]{:S(2)}, u32[]{:S(2)}) collective-permute-start(f32[1024,128]{1,0:T(8,128)S(1)} %bitcast.18), channel_id=1, source_target_pairs={{1,0},{2,1},{3,2},{4,3},{5,4},{6,5},{7,6},{8,7},{9,8},{10,9},{11,1... | collective-permute-start | bytes 1572872 | tf_op jit(solution)/shard_map/ppermute | solution.py:16

commit v3 on v2

--- a/solution.py
+++ b/solution.py
@@ -49,36 +49,36 @@
     return ((row_map[..., None] == columns[None, None, :]) & usable[..., None]).astype(dtype)
 
 
-def sweep_kernel(offsets, blocks_at, targets, live, window_ref, weights_ref, cot_ref, rows_ref,
-                 out_ref, ret_ref, grad_ref):
+def sweep_kernel(offsets, blocks_at, targets, live, window_ref, weights_ref, weights_t_ref, cot_ref,
+                 rows_ref, out_ref, ret_ref, grad_ref):
     out_ref[...] = jnp.zeros(out_ref.shape, out_ref.dtype)
     ret_ref[...] = jnp.zeros(ret_ref.shape, ret_ref.dtype)
     grad_ref[...] = jnp.zeros(grad_ref.shape, grad_ref.dtype)
     source_rows = lax.broadcasted_iota(jnp.int32, (BLK, BLK), 0)
-    lhs_rows = (((0,), (0,)), ((), ()))
-    rhs_rows = (((1,), (1,)), ((), ()))
 
     def advance(p, carry):
         kernel_at = offsets[p]
         block_at = blocks_at[p]
         target_at = targets[p]
-        picks = (rows_ref[p] == source_rows).astype(jnp.bfloat16)
-        chosen = weights_ref[kernel_at]
+        picks = ((rows_ref[p] == source_rows) & (p < live[0])).astype(jnp.bfloat16)
         grad_out = cot_ref[target_at]
-        gathered = lax.dot_general(
-            picks, window_ref[block_at], lhs_rows, preferred_element_type=jnp.float32
+        gathered_t = jnp.dot(
+            window_ref[block_at], picks, preferred_element_type=jnp.float32
         ).astype(jnp.bfloat16)
         moved = jnp.dot(picks, grad_out, preferred_element_type=jnp.float32).astype(jnp.bfloat16)
-        out_ref[target_at] += jnp.dot(gathered, chosen, preferred_element_type=jnp.float32)
-        ret_ref[block_at] += lax.dot_general(
-            moved, chosen, rhs_rows, preferred_element_type=jnp.float32
+        out_ref[target_at] += jnp.dot(
+            weights_t_ref[kernel_at], gathered_t, preferred_element_type=jnp.float32
         )
-        grad_ref[kernel_at] += lax.dot_general(
-            gathered, grad_out, lhs_rows, preferred_element_type=jnp.float32
+        ret_ref[block_at] += jnp.dot(
+            moved, weights_t_ref[kernel_at], preferred_element_type=jnp.float32
         )
+        grad_ref[kernel_at] += jnp.dot(gathered_t, grad_out, preferred_element_type=jnp.float32)
         return carry
 
-    lax.fori_loop(0, live[0], advance, 0)
+    lax.fori_loop(0, rows_ref.shape[0], advance, 0, unroll=UNROLL)
+
+
+UNROLL = 4
 
 
 def forward_sweep(window, weights, grad_blocks, rulebook, myself, blocks):
@@ -86,7 +86,8 @@
     channels = window.shape[1]
     kernel_count = weights.shape[0]
     pair_slots = g_off_all.shape[0]
-    window_blocks = window.reshape(3 * blocks, BLK, channels)
+    window_t = window.reshape(3 * blocks, BLK, channels).transpose(0, 2, 1)
+    weights_t = weights.transpose(0, 2, 1)
     relative = source_all // blocks - myself
     window_block = jnp.clip((relative + 1) * blocks + source_all % blocks, 0, 3 * blocks - 1)
     offsets = jnp.clip(g_off_all, 0, kernel_count - 1)
@@ -94,17 +95,18 @@
     live = jnp.clip(live_count, 0, pair_slots)
     smem = pl.BlockSpec(memory_space=pltpu.SMEM)
     vmem = pl.BlockSpec(memory_space=pltpu.VMEM)
-    return pl.pallas_call(
+    out_t, returned, grad = pl.pallas_call(
         sweep_kernel,
         out_shape=(
-            jax.ShapeDtypeStruct((blocks, BLK, channels), jnp.float32),
+            jax.ShapeDtypeStruct((blocks, channels, BLK), jnp.float32),
             jax.ShapeDtypeStruct((3 * blocks, BLK, channels), jnp.float32),
             jax.ShapeDtypeStruct((kernel_count, channels, channels), jnp.float32),
         ),
-        in_specs=[smem, smem, smem, smem, vmem, vmem, vmem, vmem],
+        in_specs=[smem, smem, smem, smem, vmem, vmem, vmem, vmem, vmem],
         out_specs=(vmem, vmem, vmem),
-    )(offsets, window_block, targets, live, window_blocks, weights, grad_blocks,
+    )(offsets, window_block, targets, live, window_t, weights, weights_t, grad_blocks,
       row_map_all.reshape(pair_slots, 1, BLK))
+    return out_t.transpose(0, 2, 1), returned, grad
 
 
 def on_device(

time: 226 us -> 197 us (0.87)
  the two profiles are of different devices: /device:TPU:127 before, /device:TPU:128 now
where the time goes in v3:
time: 197 us
  waiting for transfers between devices  103 us (52%)
  Pallas kernels  53.4 us (27%)
  starting transfers between devices  24.7 us (13%)
  other arithmetic  9.95 us (5%)
  local copies, waits for them, and re-layouts  4.24 us (2%)
    pallas_call x1, Pallas kernels, forward_sweep(): pl.pallas_call(sweep_kernel, out_shape=(jax.ShapeDtypeStruct((blocks, cha...  53.4 us
    ppermute x8, waiting for transfers between devices, summed_everywhere(): lax.ppermute(send, axis, [(i, i ^ mask) for i in range(count)])  49 us
    ppermute x8, waiting for transfers between devices, summed_everywhere(): other = lax.ppermute(flat, axis, [(i, i ^ mask) for i in range(count)])  40.5 us
    ppermute x4, starting transfers between devices, passed_along(): lax.ppermute(value, axis, [(source, source + steps) for source in range(l...  21.5 us
    ppermute x4, waiting for transfers between devices, passed_along(): lax.ppermute(value, axis, [(source, source + steps) for source in range(l...  13.3 us
  transfers between devices with their start and end apart: 20, of which 17 were waited for; matrix products, arithmetic and copies ran while one was open for 5% of the time, Pallas kernels for 0%

profile of v3, /device:TPU:128, one launch (start us, length us, event | category | flops | bytes accessed | tf_op | source)
XLA Modules:
  0.0 196.6 jit_solution(12450974674218469445)
XLA Ops:
  0.7 2.1 %collective-permute-start = (bf16[1024,128]{1,0:T(8,128)(2,1)}, bf16[1024,128]{1,0:T(8,128)(2,1)S(1)}, u32[]{:S(2)}, u32[]{:S(2)}) collective-permute-start(bf16[1024,128]{1,0:T(8,128)(2,1)} %param.8), channel_id=1, source_target_pairs={{0,1},{1,2},{2,3},{3,4},{4,5},{5,6},{6,7},{7,8},{8,9},{9,10},{10,1... | collective-permute-start | bytes 786440 | tf_op jit(solution)/shard_map/ppermute | solution.py:16
  2.7 9.1 %collective-permute-start.1 = (bf16[1024,128]{1,0:T(8,128)(2,1)}, bf16[1024,128]{1,0:T(8,128)(2,1)S(1)}, u32[]{:S(2)}, u32[]{:S(2)}) collective-permute-start(bf16[1024,128]{1,0:T(8,128)(2,1)} %param.8), channel_id=1, source_target_pairs={{1,0},{2,1},{3,2},{4,3},{5,4},{6,5},{7,6},{8,7},{9,8},{10,9},{11,1... | collective-permute-start | bytes 786440 | tf_op jit(solution)/shard_map/ppermute | solution.py:16
  11.8 1.2 broadcast_clamp_fusion.targets
  13.0 1.3 fusion.3.blocks_at
  14.3 2.2 %copy.13 = bf16[27,128,128]{1,2,0:T(8,128)(2,1)} copy(bf16[27,128,128]{2,1,0:T(8,128)(2,1)} %weights_ref.1) | data formatting | bytes 1769472 | tf_op args[1]
  17.8 1.2 copy.12
  19.0 53.4 %shard_map.103 = (f32[8,128,128]{2,1,0:T(8,128)}, f32[24,128,128]{2,1,0:T(8,128)}, f32[27,128,128]{2,1,0:T(8,128)}) custom-call(s32[256]{0:T(256)} %broadcast_clamp_fusion.1.offsets, s32[256]{0:T(256)} %fusion.3.blocks_at, s32[256]{0:T(256)} %broadcast_clamp_fusion.targets, s32[1]{0:T(128)S(6)} %min.29.live, bf16[24,128,128]{2,1,0:T(8,128)(2,1)} %bitcast.22, ...), custom_call_target="tpu_custom_call" | custom-call | tf_op jit(solution)/shard_map/pallas_call | solution.py:98
  72.3 1.6 broadcast_multiply_fusion
  74.2 2.4 %collective-permute-done.4 = f32[221184]{0:T(1024)S(1)} collective-permute-done((f32[221184]{0:T(1024)S(1)}, f32[221184]{0:T(1024)S(1)}, u32[]{:S(2)}, u32[]{:S(2)}) %collective-permute-start.4) | collective-permute-done | bytes 884768 | tf_op jit(solution)/shard_map/ppermute | solution.py:31
  76.9 12.2 %collective-permute-done.5 = f32[110592]{0:T(1024)S(1)} collective-permute-done((f32[110592]{0:T(1024)S(1)}, f32[110592]{0:T(1024)S(1)}, u32[]{:S(2)}, u32[]{:S(2)}) %collective-permute-start.5) | collective-permute-done | bytes 442400 | tf_op jit(solution)/shard_map/ppermute | solution.py:31
  89.3 8.1 %collective-permute-done.6 = f32[55296]{0:T(1024)S(1)} collective-permute-done((f32[55296]{0:T(1024)S(1)}, f32[55296]{0:T(1024)S(1)}, u32[]{:S(2)}, u32[]{:S(2)}) %collective-permute-start.6) | collective-permute-done | bytes 221216 | tf_op jit(solution)/shard_map/ppermute | solution.py:31
  97.5 4.8 %collective-permute-done.7 = f32[27648]{0:T(1024)S(1)} collective-permute-done((f32[27648]{0:T(1024)S(1)}, f32[27648]{0:T(1024)S(1)}, u32[]{:S(2)}, u32[]{:S(2)}) %collective-permute-start.7) | collective-permute-done | bytes 110624 | tf_op jit(solution)/shard_map/ppermute | solution.py:31
  102.5 5.7 %collective-permute-done.8 = f32[13824]{0:T(1024)S(1)} collective-permute-done((f32[13824]{0:T(1024)S(1)}, f32[13824]{0:T(1024)S(1)}, u32[]{:S(2)}, u32[]{:S(2)}) %collective-permute-start.8) | collective-permute-done | bytes 55328 | tf_op jit(solution)/shard_map/ppermute | solution.py:31
  108.3 3.9 %collective-permute-done.9 = f32[6912]{0:T(1024)S(1)} collective-permute-done((f32[6912]{0:T(1024)S(1)}, f32[6912]{0:T(1024)S(1)}, u32[]{:S(2)}, u32[]{:S(2)}) %collective-permute-start.9) | collective-permute-done | bytes 27680 | tf_op jit(solution)/shard_map/ppermute | solution.py:31
  112.4 4.4 %collective-permute-done.10 = f32[3456]{0:T(1024)S(1)} collective-permute-done((f32[3456]{0:T(1024)S(1)}, f32[3456]{0:T(1024)S(1)}, u32[]{:S(2)}, u32[]{:S(2)}) %collective-permute-start.10) | collective-permute-done | bytes 13856 | tf_op jit(solution)/shard_map/ppermute | solution.py:31
  117.0 7.5 %collective-permute-done.11 = f32[1728]{0:T(1024)S(1)} collective-permute-done((f32[1728]{0:T(1024)S(1)}, f32[1728]{0:T(1024)S(1)}, u32[]{:S(2)}, u32[]{:S(2)}) %collective-permute-start.11) | collective-permute-done | bytes 6944 | tf_op jit(solution)/shard_map/ppermute | solution.py:31
  124.7 7.5 %collective-permute-done.12 = f32[1728]{0:T(1024)S(1)} collective-permute-done((f32[1728]{0:T(1024)S(1)}, f32[1728]{0:T(1024)S(1)}, u32[]{:S(2)}, u32[]{:S(2)}) %collective-permute-start.12) | collective-permute-done | bytes 6944 | tf_op jit(solution)/shard_map/ppermute | solution.py:34
  132.5 4.4 %collective-permute-done.13 = f32[3456]{0:T(1024)S(1)} collective-permute-done((f32[3456]{0:T(1024)S(1)}, f32[3456]{0:T(1024)S(1)}, u32[]{:S(2)}, u32[]{:S(2)}) %collective-permute-start.13) | collective-permute-done | bytes 13856 | tf_op jit(solution)/shard_map/ppermute | solution.py:34
  137.2 3.7 %collective-permute-done.14 = f32[6912]{0:T(1024)S(1)} collective-permute-done((f32[6912]{0:T(1024)S(1)}, f32[6912]{0:T(1024)S(1)}, u32[]{:S(2)}, u32[]{:S(2)}) %collective-permute-start.14) | collective-permute-done | bytes 27680 | tf_op jit(solution)/shard_map/ppermute | solution.py:34
  141.2 5.5 %collective-permute-done.15 = f32[13824]{0:T(1024)S(1)} collective-permute-done((f32[13824]{0:T(1024)S(1)}, f32[13824]{0:T(1024)S(1)}, u32[]{:S(2)}, u32[]{:S(2)}) %collective-permute-start.15) | collective-permute-done | bytes 55328 | tf_op jit(solution)/shard_map/ppermute | solution.py:34
  147.0 4.6 %collective-permute-done.16 = f32[27648]{0:T(1024)S(1)} collective-permute-done((f32[27648]{0:T(1024)S(1)}, f32[27648]{0:T(1024)S(1)}, u32[]{:S(2)}, u32[]{:S(2)}) %collective-permute-start.16) | collective-permute-done | bytes 110624 | tf_op jit(solution)/shard_map/ppermute | solution.py:34
  152.2 6.9 %collective-permute-done.17 = f32[55296]{0:T(1024)S(1)} collective-permute-done((f32[55296]{0:T(1024)S(1)}, f32[55296]{0:T(1024)S(1)}, u32[]{:S(2)}, u32[]{:S(2)}) %collective-permute-start.17) | collective-permute-done | bytes 221216 | tf_op jit(solution)/shard_map/ppermute | solution.py:34
  159.2 0.6 collective-permute-start.18
  159.8 7.7 %collective-permute-done.18 = f32[110592]{0:T(1024)S(1)} collective-permute-done((f32[110592]{0:T(1024)S(1)}, f32[110592]{0:T(1024)S(1)}, u32[]{:S(2)}, u32[]{:S(2)}) %collective-permute-start.18) | collective-permute-done | bytes 442400 | tf_op jit(solution)/shard_map/ppermute | solution.py:34
  167.8 1.0 fusion.4
  168.7 8.5 %collective-permute-start.2 = (f32[1024,128]{1,0:T(8,128)}, f32[1024,128]{1,0:T(8,128)}, u32[]{:S(2)}, u32[]{:S(2)}) collective-permute-start(f32[1024,128]{1,0:T(8,128)} %bitcast.8), channel_id=1, source_target_pairs={{1,0},{2,1},{3,2},{4,3},{5,4},{6,5},{7,6},{8,7},{9,8},{10,9},{11,1... | collective-permute-start | bytes 1572872 | tf_op jit(solution)/shard_map/ppermute | solution.py:16
  177.2 1.9 collective-permute-start.3
  179.2 0.9 copy.14
  180.0 4.2 %collective-permute-done.2 = f32[1024,128]{1,0:T(8,128)} collective-permute-done((f32[1024,128]{1,0:T(8,128)}, f32[1024,128]{1,0:T(8,128)}, u32[]{:S(2)}, u32[]{:S(2)}) %collective-permute-start.2) | collective-permute-done | bytes 524320 | tf_op jit(solution)/shard_map/ppermute | solution.py:16
  184.2 9.0 %collective-permute-done.3 = f32[1024,128]{1,0:T(8,128)} collective-permute-done((f32[1024,128]{1,0:T(8,128)S(1)}, f32[1024,128]{1,0:T(8,128)}, u32[]{:S(2)}, u32[]{:S(2)}) %collective-permute-start.3) | collective-permute-done | bytes 524320 | tf_op jit(solution)/shard_map/ppermute | solution.py:16
  193.3 2.0 %fusion.1 = bf16[1024,128]{1,0:T(8,128)(2,1)} fusion(f32[1024,128]{1,0:T(8,128)} %collective-permute-done.3, f32[1024,128]{1,0:T(8,128)} %collective-permute-done.2, f32[8,128,128]{2,1,0:T(8,128)S(1)} %get-tuple-element.9), kind=kLoop, calls=%fused_computation.8 | loop fusion | flops 393216 | bytes 1835008 | tf_op jit(solution)/shard_map/convert_element_type | solution.py:133
  195.3 1.4 maximum_select_fusion
  (51 shorter events, 4.1 us)
Async XLA Ops:
  0.6 17.1 %copy-start.2 = (bf16[1024,128]{1,0:T(8,128)(2,1)S(1)}, bf16[1024,128]{1,0:T(8,128)(2,1)}, u32[]{:S(2)}) copy-start(bf16[1024,128]{1,0:T(8,128)(2,1)} %param.8) | copy-start | bytes 786436
  0.6 16.5 %copy-start.3 = (s32[256]{0:T(256)S(1)}, s32[256]{0:T(256)}, u32[]{:S(2)}) copy-start(s32[256]{0:T(256)} %param.11) | copy-start | bytes 3076
  0.7 17.1 %collective-permute-start = (bf16[1024,128]{1,0:T(8,128)(2,1)}, bf16[1024,128]{1,0:T(8,128)(2,1)S(1)}, u32[]{:S(2)}, u32[]{:S(2)}) collective-permute-start(bf16[1024,128]{1,0:T(8,128)(2,1)} %param.8), channel_id=1, source_target_pairs={{0,1},{1,2},{2,3},{3,4},{4,5},{5,6},{6,7},{7,8},{8,9},{9,10},{10,1... | collective-permute-start | bytes 786440 | tf_op jit(solution)/shard_map/ppermute | solution.py:16
  2.7 15.0 %collective-permute-start.1 = (bf16[1024,128]{1,0:T(8,128)(2,1)}, bf16[1024,128]{1,0:T(8,128)(2,1)S(1)}, u32[]{:S(2)}, u32[]{:S(2)}) collective-permute-start(bf16[1024,128]{1,0:T(8,128)(2,1)} %param.8), channel_id=1, source_target_pairs={{1,0},{2,1},{3,2},{4,3},{5,4},{6,5},{7,6},{8,7},{9,8},{10,9},{11,1... | collective-permute-start | bytes 786440 | tf_op jit(solution)/shard_map/ppermute | solution.py:16
  74.1 2.5 %collective-permute-start.4 = (f32[221184]{0:T(1024)S(1)}, f32[221184]{0:T(1024)S(1)}, u32[]{:S(2)}, u32[]{:S(2)}) collective-permute-start(f32[221184]{0:T(1024)S(1)} %slice_select_fusion), channel_id=1, source_target_pairs={{0,1},{1,0},{2,3},{3,2},{4,5},{5,4},{6,7},{7,6},{8,9},{9,8},{10,11... | collective-permute-start | bytes 2654216 | tf_op jit(solution)/shard_map/ppermute | solution.py:31
  76.8 12.3 %collective-permute-start.5 = (f32[110592]{0:T(1024)S(1)}, f32[110592]{0:T(1024)S(1)}, u32[]{:S(2)}, u32[]{:S(2)}) collective-permute-start(f32[110592]{0:T(1024)S(1)} %slice_select_fusion.1), channel_id=1, source_target_pairs={{0,2},{1,3},{2,0},{3,1},{4,6},{5,7},{6,4},{7,5},{8,10},{9,11},{10,... | collective-permute-start | bytes 1327112 | tf_op jit(solution)/shard_map/ppermute | solution.py:31
  89.2 8.2 %collective-permute-start.6 = (f32[55296]{0:T(1024)S(1)}, f32[55296]{0:T(1024)S(1)}, u32[]{:S(2)}, u32[]{:S(2)}) collective-permute-start(f32[55296]{0:T(1024)S(1)} %slice_select_fusion.2), channel_id=1, source_target_pairs={{0,4},{1,5},{2,6},{3,7},{4,0},{5,1},{6,2},{7,3},{8,12},{9,13},{10,... | collective-permute-start | bytes 663560 | tf_op jit(solution)/shard_map/ppermute | solution.py:31
  97.4 4.9 %collective-permute-start.7 = (f32[27648]{0:T(1024)S(1)}, f32[27648]{0:T(1024)S(1)}, u32[]{:S(2)}, u32[]{:S(2)}) collective-permute-start(f32[27648]{0:T(1024)S(1)} %slice_select_fusion.3), channel_id=1, source_target_pairs={{0,8},{1,9},{2,10},{3,11},{4,12},{5,13},{6,14},{7,15},{8,0},{9,1},... | collective-permute-start | bytes 331784 | tf_op jit(solution)/shard_map/ppermute | solution.py:31
  102.4 5.8 %collective-permute-start.8 = (f32[13824]{0:T(1024)S(1)}, f32[13824]{0:T(1024)S(1)}, u32[]{:S(2)}, u32[]{:S(2)}) collective-permute-start(f32[13824]{0:T(1024)S(1)} %slice_select_fusion.4), channel_id=1, source_target_pairs={{0,16},{1,17},{2,18},{3,19},{4,20},{5,21},{6,22},{7,23},{8,24},{9,... | collective-permute-start | bytes 165896 | tf_op jit(solution)/shard_map/ppermute | solution.py:31
  108.2 4.0 %collective-permute-start.9 = (f32[6912]{0:T(1024)S(1)}, f32[6912]{0:T(1024)S(1)}, u32[]{:S(2)}, u32[]{:S(2)}) collective-permute-start(f32[6912]{0:T(1024)S(1)} %slice_select_fusion.5), channel_id=1, source_target_pairs={{0,32},{1,33},{2,34},{3,35},{4,36},{5,37},{6,38},{7,39},{8,40},{9,... | collective-permute-start | bytes 82952 | tf_op jit(solution)/shard_map/ppermute | solution.py:31
  112.2 4.7 %collective-permute-start.10 = (f32[3456]{0:T(1024)S(1)}, f32[3456]{0:T(1024)S(1)}, u32[]{:S(2)}, u32[]{:S(2)}) collective-permute-start(f32[3456]{0:T(1024)S(1)} %slice_select_fusion.6), channel_id=1, source_target_pairs={{0,64},{1,65},{2,66},{3,67},{4,68},{5,69},{6,70},{7,71},{8,72},{9,... | collective-permute-start | bytes 41480 | tf_op jit(solution)/shard_map/ppermute | solution.py:31
  117.0 7.6 %collective-permute-start.11 = (f32[1728]{0:T(1024)S(1)}, f32[1728]{0:T(1024)S(1)}, u32[]{:S(2)}, u32[]{:S(2)}) collective-permute-start(f32[1728]{0:T(1024)S(1)} %slice_select_fusion.7), channel_id=1, source_target_pairs={{0,128},{1,129},{2,130},{3,131},{4,132},{5,133},{6,134},{7,135},{8... | collective-permute-start | bytes 20744 | tf_op jit(solution)/shard_map/ppermute | solution.py:31
  124.6 43.1 %copy-start = (f32[24,128,128]{2,1,0:T(8,128)S(1)}, f32[24,128,128]{2,1,0:T(8,128)}, u32[]{:S(2)}) copy-start(f32[24,128,128]{2,1,0:T(8,128)} %get-tuple-element.7) | copy-start | bytes 4718596
  124.6 43.1 %copy-start.1 = (f32[8,128,128]{2,1,0:T(8,128)S(1)}, f32[8,128,128]{2,1,0:T(8,128)}, u32[]{:S(2)}) copy-start(f32[8,128,128]{2,1,0:T(8,128)} %get-tuple-element.6) | copy-start | bytes 1572868
  124.6 7.6 %collective-permute-start.12 = (f32[1728]{0:T(1024)S(1)}, f32[1728]{0:T(1024)S(1)}, u32[]{:S(2)}, u32[]{:S(2)}) collective-permute-start(f32[1728]{0:T(1024)S(1)} %select_add_fusion.7), channel_id=1, source_target_pairs={{0,128},{1,129},{2,130},{3,131},{4,132},{5,133},{6,134},{7,135},{8... | collective-permute-start | bytes 20744 | tf_op jit(solution)/shard_map/ppermute | solution.py:34
  132.3 4.7 %collective-permute-start.13 = (f32[3456]{0:T(1024)S(1)}, f32[3456]{0:T(1024)S(1)}, u32[]{:S(2)}, u32[]{:S(2)}) collective-permute-start(f32[3456]{0:T(1024)S(1)} %maximum_select_fusion.7), channel_id=1, source_target_pairs={{0,64},{1,65},{2,66},{3,67},{4,68},{5,69},{6,70},{7,71},{8,72},{9,... | collective-permute-start | bytes 41480 | tf_op jit(solution)/shard_map/ppermute | solution.py:34
  137.0 4.0 %collective-permute-start.14 = (f32[6912]{0:T(1024)S(1)}, f32[6912]{0:T(1024)S(1)}, u32[]{:S(2)}, u32[]{:S(2)}) collective-permute-start(f32[6912]{0:T(1024)S(1)} %maximum_select_fusion.6), channel_id=1, source_target_pairs={{0,32},{1,33},{2,34},{3,35},{4,36},{5,37},{6,38},{7,39},{8,40},{9,... | collective-permute-start | bytes 82952 | tf_op jit(solution)/shard_map/ppermute | solution.py:34
  141.0 5.8 %collective-permute-start.15 = (f32[13824]{0:T(1024)S(1)}, f32[13824]{0:T(1024)S(1)}, u32[]{:S(2)}, u32[]{:S(2)}) collective-permute-start(f32[13824]{0:T(1024)S(1)} %maximum_select_fusion.5), channel_id=1, source_target_pairs={{0,16},{1,17},{2,18},{3,19},{4,20},{5,21},{6,22},{7,23},{8,24},{9,... | collective-permute-start | bytes 165896 | tf_op jit(solution)/shard_map/ppermute | solution.py:34
  146.8 4.8 %collective-permute-start.16 = (f32[27648]{0:T(1024)S(1)}, f32[27648]{0:T(1024)S(1)}, u32[]{:S(2)}, u32[]{:S(2)}) collective-permute-start(f32[27648]{0:T(1024)S(1)} %maximum_select_fusion.4), channel_id=1, source_target_pairs={{0,8},{1,9},{2,10},{3,11},{4,12},{5,13},{6,14},{7,15},{8,0},{9,1},... | collective-permute-start | bytes 331784 | tf_op jit(solution)/shard_map/ppermute | solution.py:34
  151.6 7.5 %collective-permute-start.17 = (f32[55296]{0:T(1024)S(1)}, f32[55296]{0:T(1024)S(1)}, u32[]{:S(2)}, u32[]{:S(2)}) collective-permute-start(f32[55296]{0:T(1024)S(1)} %maximum_select_fusion.3), channel_id=1, source_target_pairs={{0,4},{1,5},{2,6},{3,7},{4,0},{5,1},{6,2},{7,3},{8,12},{9,13},{10,... | collective-permute-start | bytes 663560 | tf_op jit(solution)/shard_map/ppermute | solution.py:34
  159.2 8.4 %collective-permute-start.18 = (f32[110592]{0:T(1024)S(1)}, f32[110592]{0:T(1024)S(1)}, u32[]{:S(2)}, u32[]{:S(2)}) collective-permute-start(f32[110592]{0:T(1024)S(1)} %maximum_select_fusion.2), channel_id=1, source_target_pairs={{0,2},{1,3},{2,0},{3,1},{4,6},{5,7},{6,4},{7,5},{8,10},{9,11},{10,... | collective-permute-start | bytes 1327112 | tf_op jit(solution)/shard_map/ppermute | solution.py:34
  167.6 27.6 %collective-permute-start.19 = (f32[221184]{0:T(1024)S(1)}, f32[221184]{0:T(1024)S(1)}, u32[]{:S(2)}, u32[]{:S(2)}) collective-permute-start(f32[221184]{0:T(1024)S(1)} %maximum_select_fusion.1), channel_id=1, source_target_pairs={{0,1},{1,0},{2,3},{3,2},{4,5},{5,4},{6,7},{7,6},{8,9},{9,8},{10,11... | collective-permute-start | bytes 2654216 | tf_op jit(solution)/shard_map/ppermute | solution.py:34
  168.7 15.5 %collective-permute-start.2 = (f32[1024,128]{1,0:T(8,128)}, f32[1024,128]{1,0:T(8,128)}, u32[]{:S(2)}, u32[]{:S(2)}) collective-permute-start(f32[1024,128]{1,0:T(8,128)} %bitcast.8), channel_id=1, source_target_pairs={{1,0},{2,1},{3,2},{4,3},{5,4},{6,5},{7,6},{8,7},{9,8},{10,9},{11,1... | collective-permute-start | bytes 1572872 | tf_op jit(solution)/shard_map/ppermute | solution.py:16
  177.2 16.0 %collective-permute-start.3 = (f32[1024,128]{1,0:T(8,128)S(1)}, f32[1024,128]{1,0:T(8,128)}, u32[]{:S(2)}, u32[]{:S(2)}) collective-permute-start(f32[1024,128]{1,0:T(8,128)S(1)} %bitcast.24), channel_id=1, source_target_pairs={{0,1},{1,2},{2,3},{3,4},{4,5},{5,6},{6,7},{7,8},{8,9},{9,10},{10,1... | collective-permute-start | bytes 1572872 | tf_op jit(solution)/shard_map/ppermute | solution.py:16

commit v4 on v3

v4 whole, which is shorter than its diff:
```python
import functools
import math

import jax
import jax.numpy as jnp
from jax import lax
from jax.experimental import pallas as pl
from jax.experimental.pallas import tpu as pltpu
from jax.sharding import PartitionSpec as P

BLK = 128


def passed_along(value, axis, steps):
    count = lax.axis_size(axis)
    leading, last = (max(0, -steps), min(count, count - steps))
    return lax.ppermute(value, axis, [(source, source + steps) for source in range(leading, last)])


def summed_everywhere(value, axis, work, state):
    count = lax.axis_size(axis)
    me = lax.axis_index(axis)
    flat = value.reshape(-1)
    masks = [1 << step for step in range(count.bit_length() - 1)]
    step = 0
    for mask in masks:
        half = flat.shape[0] // 2
        upper = (me & mask) != 0
        send = jnp.where(upper, flat[:half], flat[half:])
        keep = jnp.where(upper, flat[half:], flat[:half])
        received = lax.ppermute(send, axis, [(i, i ^ mask) for i in range(count)])
        state = work(step, state)
        flat, state = lax.optimization_barrier((keep + received, state))
        step += 1
    for mask in reversed(masks):
        upper = (me & mask) != 0
        other = lax.ppermute(flat, axis, [(i, i ^ mask) for i in range(count)])
        state = work(step, state)
        flat = jnp.where(upper, jnp.concatenate([other, flat]), jnp.concatenate([flat, other]))
        flat, state = lax.optimization_barrier((flat, state))
        step += 1
    return flat.reshape(value.shape), state


def grouped(array_in, group_size):
    return array_in.reshape((array_in.shape[0] // group_size, group_size) + array_in.shape[1:])


def picker(index, count, dtype):
    return (index[:, None] == jnp.arange(count, dtype=jnp.int32)[None, :]).astype(dtype)


def permuter(row_map, usable, dtype):
    columns = jnp.arange(row_map.shape[1], dtype=jnp.int32)
    return ((row_map[..., None] == columns[None, None, :]) & usable[..., None]).astype(dtype)


def grad_kernel(offsets, blocks_at, targets, live, window_ref, cot_ref, rows_ref, grad_ref,
                gathered_ref):
    grad_ref[...] = jnp.zeros(grad_ref.shape, grad_ref.dtype)
    source_rows = lax.broadcasted_iota(jnp.int32, (BLK, BLK), 0)

    def advance(p, carry):
        kernel_at = offsets[p]
        picks = ((rows_ref[p] == source_rows) & (p < live[0])).astype(jnp.bfloat16)
        gathered_t = jnp.dot(
            window_ref[blocks_at[p]], picks, preferred_element_type=jnp.float32
        ).astype(jnp.bfloat16)
        gathered_ref[p] = gathered_t
        grad_ref[kernel_at] += jnp.dot(
            gathered_t, cot_ref[targets[p]], preferred_element_type=jnp.float32
        )
        return carry

    lax.fori_loop(0, rows_ref.shape[0], advance, 0, unroll=UNROLL)


def sweep_kernel(first, offsets, blocks_at, targets, live, weights_t_ref, cot_ref, rows_ref,
                 gathered_ref, out_in, ret_in, out_ref, ret_ref):
    out_ref[...] = out_in[...]
    ret_ref[...] = ret_in[...]
    source_rows = lax.broadcasted_iota(jnp.int32, (BLK, BLK), 0)

    def advance(p, carry):
        pair = first + p
        kernel_at = offsets[pair]
        target_at = targets[pair]
        picks = ((rows_ref[p] == source_rows) & (pair < live[0])).astype(jnp.bfloat16)
        moved = jnp.dot(
            picks, cot_ref[target_at], preferred_element_type=jnp.float32
        ).astype(jnp.bfloat16)
        out_ref[target_at] += jnp.dot(
            weights_t_ref[kernel_at], gathered_ref[p], preferred_element_type=jnp.float32
        )
        ret_ref[blocks_at[pair]] += jnp.dot(
            moved, weights_t_ref[kernel_at], preferred_element_type=jnp.float32
        )
        return carry

    lax.fori_loop(0, rows_ref.shape[0], advance, 0, unroll=UNROLL)


UNROLL = 4
CHUNKS = 8
FIRST_STEP = 1


def rulebook_scalars(rulebook, myself, blocks, kernel_count):
    g_off_all, source_all, target_all, row_map_all, live_count = rulebook
    pair_slots = g_off_all.shape[0]
    relative = source_all // blocks - myself
    window_block = jnp.clip((relative + 1) * blocks + source_all % blocks, 0, 3 * blocks - 1)
    offsets = jnp.clip(g_off_all, 0, kernel_count - 1)
    targets = jnp.clip(target_all, 0, blocks - 1)
    live = jnp.clip(live_count, 0, pair_slots)
    return offsets, window_block, targets, live, row_map_all.reshape(pair_slots, 1, BLK)


def grad_sweep(window, grad_blocks, scalars, kernel_count):
    channels = window.shape[1]
    rows = scalars[-1]
    window_t = window.reshape(-1, BLK, channels).transpose(0, 2, 1)
    smem = pl.BlockSpec(memory_space=pltpu.SMEM)
    vmem = pl.BlockSpec(memory_space=pltpu.VMEM)
    return pl.pallas_call(
        grad_kernel,
        out_shape=(
            jax.ShapeDtypeStruct((kernel_count, channels, channels), jnp.float32),
            jax.ShapeDtypeStruct((rows.shape[0], channels, BLK), jnp.bfloat16),
        ),
        in_specs=[smem, smem, smem, smem, vmem, vmem, vmem],
        out_specs=(vmem, vmem),
    )(*scalars[:4], window_t, grad_blocks, rows)


def forward_chunk(weights_t, grad_blocks, scalars, gathered, sums, chunk, chunk_size):
    out_sum, returned_sum = sums
    smem = pl.BlockSpec(memory_space=pltpu.SMEM)

    def whole(array):
        return pl.BlockSpec(array.shape, lambda i: (0,) * array.ndim)

    def part(array):
        return pl.BlockSpec((chunk_size,) + array.shape[1:], lambda i: (chunk,) + (0,) * (array.ndim - 1))

    rows = scalars[4]
    return pl.pallas_call(
        functools.partial(sweep_kernel, chunk * chunk_size),
        grid=(1,),
        out_shape=(
            jax.ShapeDtypeStruct(out_sum.shape, jnp.float32),
            jax.ShapeDtypeStruct(returned_sum.shape, jnp.float32),
        ),
        in_specs=[smem, smem, smem, smem, whole(weights_t), whole(grad_blocks), part(rows),
                  part(gathered), whole(out_sum), whole(returned_sum)],
        out_specs=(whole(out_sum), whole(returned_sum)),
        input_output_aliases={8: 0, 9: 1},
    )(*scalars[:4], weights_t, grad_blocks, rows, gathered, out_sum, returned_sum)


def on_device(
    features, weights, cotangent, pair_offset, pair_source, pair_target, pair_rows, pair_count
):
    axis_count = lax.axis_size(("space", "sub"))
    myself = lax.axis_index(("space", "sub"))
    local_rows = features.shape[0]
    blocks = local_rows // BLK
    channels = features.shape[1]
    before = passed_along(features, ("space", "sub"), 1)
    next_side = passed_along(features, ("space", "sub"), -1)
    window = jnp.concatenate([before, features, next_side], axis=0)
    grad_blocks = cotangent.reshape(blocks, BLK, channels)
    rulebook = (pair_offset, pair_source, pair_target, pair_rows, pair_count)
    kernel_count = weights.shape[0]
    scalars = rulebook_scalars(rulebook, myself, blocks, kernel_count)
    grad_sum, gathered = grad_sweep(window, grad_blocks, scalars, kernel_count)
    grad_sum = grad_sum * (1.0 / math.sqrt(axis_count * local_rows))
    weights_t = weights.transpose(0, 2, 1)
    pair_slots = pair_offset.shape[0]
    chunk_count = CHUNKS if pair_slots % CHUNKS == 0 else 1
    chunk_size = pair_slots // chunk_count
    first_step = FIRST_STEP if axis_count & (axis_count - 1) == 0 else 0

    def work(step, sums):
        chunk = step - first_step
        if 0 <= chunk < chunk_count:
            return forward_chunk(weights_t, grad_blocks, scalars, gathered, sums, chunk, chunk_size)
        return sums

    sums = (
        jnp.zeros((blocks, channels, BLK), jnp.float32),
        jnp.zeros((3 * blocks, BLK, channels), jnp.float32),
    )
    if axis_count & (axis_count - 1) or grad_sum.size % axis_count:
        grand_total = lax.psum(grad_sum, ("space", "sub"))
        for chunk in range(chunk_count):
            sums = work(chunk + first_step, sums)
    else:
        grand_total, sums = summed_everywhere(grad_sum, ("space", "sub"), work, sums)
    out_t, returned_sum = sums
    out_sum = out_t.transpose(0, 2, 1)
    low_part = returned_sum[:blocks].reshape(local_rows, channels)
    middle = returned_sum[blocks : 2 * blocks].reshape(local_rows, channels)
    high_part = returned_sum[2 * blocks :].reshape(local_rows, channels)
    from_next = passed_along(low_part, ("space", "sub"), -1)
    from_prev = passed_along(high_part, ("space", "sub"), 1)
    grad_features = (middle + from_next + from_prev).astype(jnp.bfloat16)
    output = out_sum.reshape(local_rows, channels).astype(jnp.bfloat16)
    return (output, grad_features, grand_total)


def solution(mesh):
    placed = (
        P(("space", "sub"), None),
        P(),
        P(("space", "sub"), None),
        P(("space", "sub")),
        P(("space", "sub")),
        P(("space", "sub")),
        P(("space", "sub"), None),
        P(("space", "sub")),
    )
    return jax.shard_map(
        on_device,
        mesh=mesh,
        in_specs=placed,
        out_specs=(P(("space", "sub"), None), P(("space", "sub"), None), P()),
        check_vma=False,
    )
```

time: 197 us -> 193 us (0.980)
  the two profiles are of different devices: /device:TPU:128 before, /device:TPU:127 now
where the time goes in v4:
time: 193 us; the launch traced here: 192 us
  Pallas kernels  85.9 us (45%)
  waiting for transfers between devices  47.1 us (24%)
  starting transfers between devices  42.1 us (22%)
  other arithmetic  9.38 us (5%)
  local copies, waits for them, and re-layouts  6.08 us (3%)
    pallas_call x8, Pallas kernels, forward_chunk(): pl.pallas_call(functools.partial(sweep_kernel, chunk * chunk_size), grid=...  59.8 us
    ppermute x8, waiting for transfers between devices, summed_everywhere(): other = lax.ppermute(flat, axis, [(i, i ^ mask) for i in range(count)])  30.8 us
    pallas_call x1, Pallas kernels, grad_sweep(): pl.pallas_call(grad_kernel, out_shape=(jax.ShapeDtypeStruct((kernel_count...  26.1 us
    ppermute x4, starting transfers between devices, passed_along(): lax.ppermute(value, axis, [(source, source + steps) for source in range(l...  17.5 us
    ppermute x8, starting transfers between devices, summed_everywhere(): received = lax.ppermute(send, axis, [(i, i ^ mask) for i in range(count)])  14.1 us
    ppermute x4, waiting for transfers between devices, passed_along(): lax.ppermute(value, axis, [(source, source + steps) for source in range(l...  13.5 us
    ppermute x8, starting transfers between devices, summed_everywhere(): other = lax.ppermute(flat, axis, [(i, i ^ mask) for i in range(count)])  10.5 us
  transfers between devices with their start and end apart: 20, of which 12 were waited for; matrix products, arithmetic and copies ran while one was open for 4% of the time, Pallas kernels for 31%

profile of v4, /device:TPU:127, one launch (start us, length us, event | category | flops | bytes accessed | tf_op | source)
XLA Modules:
  0.0 192.1 jit_solution(1772509620534813054)
XLA Ops:
  0.6 2.6 %collective-permute-start.1 = (bf16[1024,128]{1,0:T(8,128)(2,1)}, bf16[1024,128]{1,0:T(8,128)(2,1)S(1)}, u32[]{:S(2)}, u32[]{:S(2)}) collective-permute-start(bf16[1024,128]{1,0:T(8,128)(2,1)} %param.8), channel_id=1, source_target_pairs={{1,0},{2,1},{3,2},{4,3},{5,4},{6,5},{7,6},{8,7},{9,8},{10,9},{11,1... | collective-permute-start | bytes 786440 | tf_op jit(solution)/shard_map/ppermute | solution.py:17
  3.2 8.4 %collective-permute-start = (bf16[1024,128]{1,0:T(8,128)(2,1)}, bf16[1024,128]{1,0:T(8,128)(2,1)S(1)}, u32[]{:S(2)}, u32[]{:S(2)}) collective-permute-start(bf16[1024,128]{1,0:T(8,128)(2,1)} %param.8), channel_id=1, source_target_pairs={{0,1},{1,2},{2,3},{3,4},{4,5},{5,6},{6,7},{7,8},{8,9},{9,10},{10,1... | collective-permute-start | bytes 786440 | tf_op jit(solution)/shard_map/ppermute | solution.py:17
  13.5 1.3 fusion.3
  17.5 26.1 %shard_map.103 = (f32[27,128,128]{2,1,0:T(8,128)}, bf16[256,128,128]{2,1,0:T(8,128)(2,1)}) custom-call(s32[256]{0:T(256)} %broadcast_clamp_fusion.1.offsets, s32[256]{0:T(256)} %get-tuple-element.138.blocks_at, s32[256]{0:T(256)} %get-tuple-element.139.targets, s32[1]{0:T(128)S(6)} %min.29.live, bf16[24,128,128]{2,1,0:T(8,128)(2,1)} %bitcast.46, ...), custom_call_target="tpu_custom_call" | custom-call | tf_op jit(solution)/shard_map/pallas_call | solution.py:125
  43.5 1.6 broadcast_multiply_fusion
  45.4 2.5 %collective-permute-done.2 = f32[221184]{0:T(1024)} collective-permute-done((f32[221184]{0:T(1024)S(1)}, f32[221184]{0:T(1024)}, u32[]{:S(2)}, u32[]{:S(2)}) %collective-permute-start.2) | collective-permute-done | bytes 884768 | tf_op jit(solution)/shard_map/ppermute | solution.py:31
  47.9 1.3 select_add_fusion
  49.4 1.6 copy.29
  51.9 1.4 broadcast_in_dim.7.ret_in
  53.2 7.5 %shard_map.104 = (f32[8,128,128]{2,1,0:T(8,128)}, f32[24,128,128]{2,1,0:T(8,128)}) custom-call(s32[256]{0:T(256)} %broadcast_clamp_fusion.1.offsets, s32[256]{0:T(256)} %get-tuple-element.138.blocks_at, s32[256]{0:T(256)} %get-tuple-element.139.targets, s32[1]{0:T(128)S(6)} %min.29.live, ...), custom_call_target="tpu_custom_call", output_to_operand_aliasing={{0}: (8, {}), {1}: (9, {})} | custom-call | tf_op jit(solution)/shard_map/pallas_call | solution.py:147
  62.2 7.5 %shard_map.105 = (f32[8,128,128]{2,1,0:T(8,128)}, f32[24,128,128]{2,1,0:T(8,128)}) custom-call(s32[256]{0:T(256)} %broadcast_clamp_fusion.1.offsets, s32[256]{0:T(256)} %get-tuple-element.138.blocks_at, s32[256]{0:T(256)} %get-tuple-element.139.targets, s32[1]{0:T(128)S(6)} %min.29.live, ...), custom_call_target="tpu_custom_call", output_to_operand_aliasing={{0}: (8, {}), {1}: (9, {})} | custom-call | tf_op jit(solution)/shard_map/pallas_call | solution.py:147
  70.0 7.5 %shard_map.106 = (f32[8,128,128]{2,1,0:T(8,128)}, f32[24,128,128]{2,1,0:T(8,128)}) custom-call(s32[256]{0:T(256)} %broadcast_clamp_fusion.1.offsets, s32[256]{0:T(256)} %get-tuple-element.138.blocks_at, s32[256]{0:T(256)} %get-tuple-element.139.targets, s32[1]{0:T(128)S(6)} %min.29.live, ...), custom_call_target="tpu_custom_call", output_to_operand_aliasing={{0}: (8, {}), {1}: (9, {})} | custom-call | tf_op jit(solution)/shard_map/pallas_call | solution.py:147
  77.6 5.0 %collective-permute-start.6 = (f32[13824]{0:T(1024)S(1)}, f32[13824]{0:T(1024)S(1)}, u32[]{:S(2)}, u32[]{:S(2)}) collective-permute-start(f32[13824]{0:T(1024)S(1)} %slice_select_fusion.4), channel_id=1, source_target_pairs={{0,16},{1,17},{2,18},{3,19},{4,20},{5,21},{6,22},{7,23},{8,24},{9,... | collective-permute-start | bytes 165896 | tf_op jit(solution)/shard_map/ppermute | solution.py:31
  82.5 7.5 %shard_map.107 = (f32[8,128,128]{2,1,0:T(8,128)}, f32[24,128,128]{2,1,0:T(8,128)}) custom-call(s32[256]{0:T(256)} %broadcast_clamp_fusion.1.offsets, s32[256]{0:T(256)} %get-tuple-element.138.blocks_at, s32[256]{0:T(256)} %get-tuple-element.139.targets, s32[1]{0:T(128)S(6)} %min.29.live, ...), custom_call_target="tpu_custom_call", output_to_operand_aliasing={{0}: (8, {}), {1}: (9, {})} | custom-call | tf_op jit(solution)/shard_map/pallas_call | solution.py:147
  90.1 7.5 %shard_map.108 = (f32[8,128,128]{2,1,0:T(8,128)}, f32[24,128,128]{2,1,0:T(8,128)}) custom-call(s32[256]{0:T(256)} %broadcast_clamp_fusion.1.offsets, s32[256]{0:T(256)} %get-tuple-element.138.blocks_at, s32[256]{0:T(256)} %get-tuple-element.139.targets, s32[1]{0:T(128)S(6)} %min.29.live, ...), custom_call_target="tpu_custom_call", output_to_operand_aliasing={{0}: (8, {}), {1}: (9, {})} | custom-call | tf_op jit(solution)/shard_map/pallas_call | solution.py:147
  97.8 7.5 %shard_map.109 = (f32[8,128,128]{2,1,0:T(8,128)}, f32[24,128,128]{2,1,0:T(8,128)}) custom-call(s32[256]{0:T(256)} %broadcast_clamp_fusion.1.offsets, s32[256]{0:T(256)} %get-tuple-element.138.blocks_at, s32[256]{0:T(256)} %get-tuple-element.139.targets, s32[1]{0:T(128)S(6)} %min.29.live, ...), custom_call_target="tpu_custom_call", output_to_operand_aliasing={{0}: (8, {}), {1}: (9, {})} | custom-call | tf_op jit(solution)/shard_map/pallas_call | solution.py:147
  105.3 7.3 %collective-permute-start.9 = (f32[1728]{0:T(1024)S(1)}, f32[1728]{0:T(1024)S(1)}, u32[]{:S(2)}, u32[]{:S(2)}) collective-permute-start(f32[1728]{0:T(1024)S(1)} %slice_select_fusion.7), channel_id=1, source_target_pairs={{0,128},{1,129},{2,130},{3,131},{4,132},{5,133},{6,134},{7,135},{8... | collective-permute-start | bytes 20744 | tf_op jit(solution)/shard_map/ppermute | solution.py:31
  112.6 7.5 %shard_map.110 = (f32[8,128,128]{2,1,0:T(8,128)}, f32[24,128,128]{2,1,0:T(8,128)}) custom-call(s32[256]{0:T(256)} %broadcast_clamp_fusion.1.offsets, s32[256]{0:T(256)} %get-tuple-element.138.blocks_at, s32[256]{0:T(256)} %get-tuple-element.139.targets, s32[1]{0:T(128)S(6)} %min.29.live, ...), custom_call_target="tpu_custom_call", output_to_operand_aliasing={{0}: (8, {}), {1}: (9, {})} | custom-call | tf_op jit(solution)/shard_map/pallas_call | solution.py:147
  120.2 7.5 %shard_map.111 = (f32[8,128,128]{2,1,0:T(8,128)}, f32[24,128,128]{2,1,0:T(8,128)}) custom-call(s32[256]{0:T(256)} %broadcast_clamp_fusion.1.offsets, s32[256]{0:T(256)} %get-tuple-element.138.blocks_at, s32[256]{0:T(256)} %get-tuple-element.139.targets, s32[1]{0:T(128)S(6)} %min.29.live, ...), custom_call_target="tpu_custom_call", output_to_operand_aliasing={{0}: (8, {}), {1}: (9, {})} | custom-call | tf_op jit(solution)/shard_map/pallas_call | solution.py:147
  128.7 2.6 %collective-permute-done.11 = f32[3456]{0:T(1024)S(1)} collective-permute-done((f32[3456]{0:T(1024)S(1)}, f32[3456]{0:T(1024)S(1)}, u32[]{:S(2)}, u32[]{:S(2)}) %collective-permute-start.11) | collective-permute-done | bytes 13856 | tf_op jit(solution)/shard_map/ppermute | solution.py:37
  131.9 2.6 %collective-permute-done.12 = f32[6912]{0:T(1024)S(1)} collective-permute-done((f32[6912]{0:T(1024)S(1)}, f32[6912]{0:T(1024)S(1)}, u32[]{:S(2)}, u32[]{:S(2)}) %collective-permute-start.12) | collective-permute-done | bytes 27680 | tf_op jit(solution)/shard_map/ppermute | solution.py:37
  134.6 4.5 %collective-permute-done.13 = f32[13824]{0:T(1024)S(1)} collective-permute-done((f32[13824]{0:T(1024)S(1)}, f32[13824]{0:T(1024)S(1)}, u32[]{:S(2)}, u32[]{:S(2)}) %collective-permute-start.13) | collective-permute-done | bytes 55328 | tf_op jit(solution)/shard_map/ppermute | solution.py:37
  139.4 3.9 %collective-permute-done.14 = f32[27648]{0:T(1024)S(1)} collective-permute-done((f32[27648]{0:T(1024)S(1)}, f32[27648]{0:T(1024)S(1)}, u32[]{:S(2)}, u32[]{:S(2)}) %collective-permute-start.14) | collective-permute-done | bytes 110624 | tf_op jit(solution)/shard_map/ppermute | solution.py:37
  143.4 6.3 %collective-permute-done.15 = f32[55296]{0:T(1024)S(1)} collective-permute-done((f32[55296]{0:T(1024)S(1)}, f32[55296]{0:T(1024)S(1)}, u32[]{:S(2)}, u32[]{:S(2)}) %collective-permute-start.15) | collective-permute-done | bytes 221216 | tf_op jit(solution)/shard_map/ppermute | solution.py:37
  149.8 8.8 %collective-permute-done.16 = f32[110592]{0:T(1024)S(1)} collective-permute-done((f32[110592]{0:T(1024)S(1)}, f32[110592]{0:T(1024)S(1)}, u32[]{:S(2)}, u32[]{:S(2)}) %collective-permute-start.16) | collective-permute-done | bytes 442400 | tf_op jit(solution)/shard_map/ppermute | solution.py:37
  158.7 8.4 %collective-permute-start.17 = (f32[221184]{0:T(1024)S(1)}, f32[221184]{0:T(1024)S(1)}, u32[]{:S(2)}, u32[]{:S(2)}) collective-permute-start(f32[221184]{0:T(1024)S(1)} %maximum_select_fusion.1), channel_id=1, source_target_pairs={{0,1},{1,0},{2,3},{3,2},{4,5},{5,4},{6,7},{7,6},{8,9},{9,8},{10,11... | collective-permute-start | bytes 2654216 | tf_op jit(solution)/shard_map/ppermute | solution.py:37
  167.2 2.1 %collective-permute-done.17 = f32[221184]{0:T(1024)S(1)} collective-permute-done((f32[221184]{0:T(1024)S(1)}, f32[221184]{0:T(1024)S(1)}, u32[]{:S(2)}, u32[]{:S(2)}) %collective-permute-start.17) | collective-permute-done | bytes 884768 | tf_op jit(solution)/shard_map/ppermute | solution.py:37
  169.2 1.4 maximum_select_fusion
  170.8 4.6 %collective-permute-start.19 = (f32[1024,128]{1,0:T(8,128)S(1)}, f32[1024,128]{1,0:T(8,128)S(1)}, u32[]{:S(2)}, u32[]{:S(2)}) collective-permute-start(f32[1024,128]{1,0:T(8,128)S(1)} %bitcast.50), channel_id=1, source_target_pairs={{0,1},{1,2},{2,3},{3,4},{4,5},{5,6},{6,7},{7,8},{8,9},{9,10},{10,1... | collective-permute-start | bytes 1572872 | tf_op jit(solution)/shard_map/ppermute | solution.py:17
  175.4 1.9 collective-permute-start.18
  178.2 3.3 %collective-permute-done.19 = f32[1024,128]{1,0:T(8,128)S(1)} collective-permute-done((f32[1024,128]{1,0:T(8,128)S(1)}, f32[1024,128]{1,0:T(8,128)S(1)}, u32[]{:S(2)}, u32[]{:S(2)}) %collective-permute-start.19) | collective-permute-done | bytes 524320 | tf_op jit(solution)/shard_map/ppermute | solution.py:17
  181.5 9.8 %collective-permute-done.18 = f32[1024,128]{1,0:T(8,128)S(1)} collective-permute-done((f32[1024,128]{1,0:T(8,128)S(1)}, f32[1024,128]{1,0:T(8,128)S(1)}, u32[]{:S(2)}, u32[]{:S(2)}) %collective-permute-start.18) | collective-permute-done | bytes 524320 | tf_op jit(solution)/shard_map/ppermute | solution.py:17
  (59 shorter events, 11.4 us)
Async XLA Ops:
  0.6 14.2 %collective-permute-start.1 = (bf16[1024,128]{1,0:T(8,128)(2,1)}, bf16[1024,128]{1,0:T(8,128)(2,1)S(1)}, u32[]{:S(2)}, u32[]{:S(2)}) collective-permute-start(bf16[1024,128]{1,0:T(8,128)(2,1)} %param.8), channel_id=1, source_target_pairs={{1,0},{2,1},{3,2},{4,3},{5,4},{6,5},{7,6},{8,7},{9,8},{10,9},{11,1... | collective-permute-start | bytes 786440 | tf_op jit(solution)/shard_map/ppermute | solution.py:17
  3.2 12.0 %collective-permute-start = (bf16[1024,128]{1,0:T(8,128)(2,1)}, bf16[1024,128]{1,0:T(8,128)(2,1)S(1)}, u32[]{:S(2)}, u32[]{:S(2)}) collective-permute-start(bf16[1024,128]{1,0:T(8,128)(2,1)} %param.8), channel_id=1, source_target_pairs={{0,1},{1,2},{2,3},{3,4},{4,5},{5,6},{6,7},{7,8},{8,9},{9,10},{10,1... | collective-permute-start | bytes 786440 | tf_op jit(solution)/shard_map/ppermute | solution.py:17
  45.3 2.6 %collective-permute-start.2 = (f32[221184]{0:T(1024)S(1)}, f32[221184]{0:T(1024)}, u32[]{:S(2)}, u32[]{:S(2)}) collective-permute-start(f32[221184]{0:T(1024)S(1)} %slice_select_fusion), channel_id=1, source_target_pairs={{0,1},{1,0},{2,3},{3,2},{4,5},{5,4},{6,7},{7,6},{8,9},{9,8},{10,11... | collective-permute-start | bytes 2654216 | tf_op jit(solution)/shard_map/ppermute | solution.py:31
  45.4 4.0 %copy-start.2 = (bf16[27,128,128]{2,1,0:T(8,128)(2,1)S(1)}, bf16[27,128,128]{2,1,0:T(8,128)(2,1)}, u32[]{:S(2)}) copy-start(bf16[27,128,128]{2,1,0:T(8,128)(2,1)} %param.9) | copy-start | bytes 2654212
  49.3 11.7 %collective-permute-start.3 = (f32[110592]{0:T(1024)S(1)}, f32[110592]{0:T(1024)S(1)}, u32[]{:S(2)}, u32[]{:S(2)}) collective-permute-start(f32[110592]{0:T(1024)S(1)} %slice_select_fusion.1), channel_id=1, source_target_pairs={{0,2},{1,3},{2,0},{3,1},{4,6},{5,7},{6,4},{7,5},{8,10},{9,11},{10,... | collective-permute-start | bytes 1327112 | tf_op jit(solution)/shard_map/ppermute | solution.py:31
  61.0 8.7 %collective-permute-start.4 = (f32[55296]{0:T(1024)S(1)}, f32[55296]{0:T(1024)S(1)}, u32[]{:S(2)}, u32[]{:S(2)}) collective-permute-start(f32[55296]{0:T(1024)S(1)} %slice_select_fusion.2), channel_id=1, source_target_pairs={{0,4},{1,5},{2,6},{3,7},{4,0},{5,1},{6,2},{7,3},{8,12},{9,13},{10,... | collective-permute-start | bytes 663560 | tf_op jit(solution)/shard_map/ppermute | solution.py:31
  69.8 7.7 %collective-permute-start.5 = (f32[27648]{0:T(1024)S(1)}, f32[27648]{0:T(1024)S(1)}, u32[]{:S(2)}, u32[]{:S(2)}) collective-permute-start(f32[27648]{0:T(1024)S(1)} %slice_select_fusion.3), channel_id=1, source_target_pairs={{0,8},{1,9},{2,10},{3,11},{4,12},{5,13},{6,14},{7,15},{8,0},{9,1},... | collective-permute-start | bytes 331784 | tf_op jit(solution)/shard_map/ppermute | solution.py:31
  77.6 12.4 %collective-permute-start.6 = (f32[13824]{0:T(1024)S(1)}, f32[13824]{0:T(1024)S(1)}, u32[]{:S(2)}, u32[]{:S(2)}) collective-permute-start(f32[13824]{0:T(1024)S(1)} %slice_select_fusion.4), channel_id=1, source_target_pairs={{0,16},{1,17},{2,18},{3,19},{4,20},{5,21},{6,22},{7,23},{8,24},{9,... | collective-permute-start | bytes 165896 | tf_op jit(solution)/shard_map/ppermute | solution.py:31
  90.0 7.6 %collective-permute-start.7 = (f32[6912]{0:T(1024)S(1)}, f32[6912]{0:T(1024)S(1)}, u32[]{:S(2)}, u32[]{:S(2)}) collective-permute-start(f32[6912]{0:T(1024)S(1)} %slice_select_fusion.5), channel_id=1, source_target_pairs={{0,32},{1,33},{2,34},{3,35},{4,36},{5,37},{6,38},{7,39},{8,40},{9,... | collective-permute-start | bytes 82952 | tf_op jit(solution)/shard_map/ppermute | solution.py:31
  97.7 7.6 %collective-permute-start.8 = (f32[3456]{0:T(1024)S(1)}, f32[3456]{0:T(1024)S(1)}, u32[]{:S(2)}, u32[]{:S(2)}) collective-permute-start(f32[3456]{0:T(1024)S(1)} %slice_select_fusion.6), channel_id=1, source_target_pairs={{0,64},{1,65},{2,66},{3,67},{4,68},{5,69},{6,70},{7,71},{8,72},{9,... | collective-permute-start | bytes 41480 | tf_op jit(solution)/shard_map/ppermute | solution.py:31
  105.3 14.8 %collective-permute-start.9 = (f32[1728]{0:T(1024)S(1)}, f32[1728]{0:T(1024)S(1)}, u32[]{:S(2)}, u32[]{:S(2)}) collective-permute-start(f32[1728]{0:T(1024)S(1)} %slice_select_fusion.7), channel_id=1, source_target_pairs={{0,128},{1,129},{2,130},{3,131},{4,132},{5,133},{6,134},{7,135},{8... | collective-permute-start | bytes 20744 | tf_op jit(solution)/shard_map/ppermute | solution.py:31
  120.2 7.5 %collective-permute-start.10 = (f32[1728]{0:T(1024)S(1)}, f32[1728]{0:T(1024)S(1)}, u32[]{:S(2)}, u32[]{:S(2)}) collective-permute-start(f32[1728]{0:T(1024)S(1)} %select_add_fusion.7), channel_id=1, source_target_pairs={{0,128},{1,129},{2,130},{3,131},{4,132},{5,133},{6,134},{7,135},{8... | collective-permute-start | bytes 20744 | tf_op jit(solution)/shard_map/ppermute | solution.py:37
  127.8 3.5 %collective-permute-start.11 = (f32[3456]{0:T(1024)S(1)}, f32[3456]{0:T(1024)S(1)}, u32[]{:S(2)}, u32[]{:S(2)}) collective-permute-start(f32[3456]{0:T(1024)S(1)} %maximum_select_fusion.7), channel_id=1, source_target_pairs={{0,64},{1,65},{2,66},{3,67},{4,68},{5,69},{6,70},{7,71},{8,72},{9,... | collective-permute-start | bytes 41480 | tf_op jit(solution)/shard_map/ppermute | solution.py:37
  131.3 3.1 %collective-permute-start.12 = (f32[6912]{0:T(1024)S(1)}, f32[6912]{0:T(1024)S(1)}, u32[]{:S(2)}, u32[]{:S(2)}) collective-permute-start(f32[6912]{0:T(1024)S(1)} %maximum_select_fusion.6), channel_id=1, source_target_pairs={{0,32},{1,33},{2,34},{3,35},{4,36},{5,37},{6,38},{7,39},{8,40},{9,... | collective-permute-start | bytes 82952 | tf_op jit(solution)/shard_map/ppermute | solution.py:37
  134.5 4.6 %collective-permute-start.13 = (f32[13824]{0:T(1024)S(1)}, f32[13824]{0:T(1024)S(1)}, u32[]{:S(2)}, u32[]{:S(2)}) collective-permute-start(f32[13824]{0:T(1024)S(1)} %maximum_select_fusion.5), channel_id=1, source_target_pairs={{0,16},{1,17},{2,18},{3,19},{4,20},{5,21},{6,22},{7,23},{8,24},{9,... | collective-permute-start | bytes 165896 | tf_op jit(solution)/shard_map/ppermute | solution.py:37
  139.1 4.2 %collective-permute-start.14 = (f32[27648]{0:T(1024)S(1)}, f32[27648]{0:T(1024)S(1)}, u32[]{:S(2)}, u32[]{:S(2)}) collective-permute-start(f32[27648]{0:T(1024)S(1)} %maximum_select_fusion.4), channel_id=1, source_target_pairs={{0,8},{1,9},{2,10},{3,11},{4,12},{5,13},{6,14},{7,15},{8,0},{9,1},... | collective-permute-start | bytes 331784 | tf_op jit(solution)/shard_map/ppermute | solution.py:37
  143.3 6.4 %collective-permute-start.15 = (f32[55296]{0:T(1024)S(1)}, f32[55296]{0:T(1024)S(1)}, u32[]{:S(2)}, u32[]{:S(2)}) collective-permute-start(f32[55296]{0:T(1024)S(1)} %maximum_select_fusion.3), channel_id=1, source_target_pairs={{0,4},{1,5},{2,6},{3,7},{4,0},{5,1},{6,2},{7,3},{8,12},{9,13},{10,... | collective-permute-start | bytes 663560 | tf_op jit(solution)/shard_map/ppermute | solution.py:37
  149.7 8.9 %collective-permute-start.16 = (f32[110592]{0:T(1024)S(1)}, f32[110592]{0:T(1024)S(1)}, u32[]{:S(2)}, u32[]{:S(2)}) collective-permute-start(f32[110592]{0:T(1024)S(1)} %maximum_select_fusion.2), channel_id=1, source_target_pairs={{0,2},{1,3},{2,0},{3,1},{4,6},{5,7},{6,4},{7,5},{8,10},{9,11},{10,... | collective-permute-start | bytes 1327112 | tf_op jit(solution)/shard_map/ppermute | solution.py:37
  158.7 11.9 %copy-start = (f32[24,128,128]{2,1,0:T(8,128)S(1)}, f32[24,128,128]{2,1,0:T(8,128)}, u32[]{:S(2)}) copy-start(f32[24,128,128]{2,1,0:T(8,128)} %get-tuple-element.133) | copy-start | bytes 4718596
  158.7 10.5 %collective-permute-start.17 = (f32[221184]{0:T(1024)S(1)}, f32[221184]{0:T(1024)S(1)}, u32[]{:S(2)}, u32[]{:S(2)}) collective-permute-start(f32[221184]{0:T(1024)S(1)} %maximum_select_fusion.1), channel_id=1, source_target_pairs={{0,1},{1,0},{2,3},{3,2},{4,5},{5,4},{6,7},{7,6},{8,9},{9,8},{10,11... | collective-permute-start | bytes 2654216 | tf_op jit(solution)/shard_map/ppermute | solution.py:37
  170.6 6.7 %copy-start.1 = (f32[8,128,128]{2,1,0:T(8,128)S(1)}, f32[8,128,128]{2,1,0:T(8,128)}, u32[]{:S(2)}) copy-start(f32[8,128,128]{2,1,0:T(8,128)} %get-tuple-element.132) | copy-start | bytes 1572868
  170.8 10.7 %collective-permute-start.19 = (f32[1024,128]{1,0:T(8,128)S(1)}, f32[1024,128]{1,0:T(8,128)S(1)}, u32[]{:S(2)}, u32[]{:S(2)}) collective-permute-start(f32[1024,128]{1,0:T(8,128)S(1)} %bitcast.50), channel_id=1, source_target_pairs={{0,1},{1,2},{2,3},{3,4},{4,5},{5,6},{6,7},{7,8},{8,9},{9,10},{10,1... | collective-permute-start | bytes 1572872 | tf_op jit(solution)/shard_map/ppermute | solution.py:17
  175.4 15.9 %collective-permute-start.18 = (f32[1024,128]{1,0:T(8,128)S(1)}, f32[1024,128]{1,0:T(8,128)S(1)}, u32[]{:S(2)}, u32[]{:S(2)}) collective-permute-start(f32[1024,128]{1,0:T(8,128)S(1)} %bitcast.49), channel_id=1, source_target_pairs={{1,0},{2,1},{3,2},{4,3},{5,4},{6,5},{7,6},{8,7},{9,8},{10,9},{11,1... | collective-permute-start | bytes 1572872 | tf_op jit(solution)/shard_map/ppermute | solution.py:17

commit v5 on v4

--- a/solution.py
+++ b/solution.py
@@ -17,11 +17,23 @@
     return lax.ppermute(value, axis, [(source, source + steps) for source in range(leading, last)])
 
 
-def summed_everywhere(value, axis, work, state):
+def summed_everywhere(value, axis, work, state, last_work):
     count = lax.axis_size(axis)
     me = lax.axis_index(axis)
     flat = value.reshape(-1)
-    masks = [1 << step for step in range(count.bit_length() - 1)]
+    bits = count.bit_length() - 1
+    split = max(bits - 2, 0)
+    masks = [1 << step for step in range(split)]
+    group = [0]
+    for step in range(split, bits):
+        group = group + [member | (1 << step) for member in group]
+
+    def tied(flat, state, step):
+        state = work(step, state)
+        if step <= last_work:
+            return lax.optimization_barrier((flat, state))
+        return flat, state
+
     step = 0
     for mask in masks:
         half = flat.shape[0] // 2
@@ -29,15 +41,18 @@
         send = jnp.where(upper, flat[:half], flat[half:])
         keep = jnp.where(upper, flat[half:], flat[:half])
         received = lax.ppermute(send, axis, [(i, i ^ mask) for i in range(count)])
-        state = work(step, state)
-        flat, state = lax.optimization_barrier((keep + received, state))
+        flat, state = tied(keep + received, state, step)
         step += 1
+    others = [lax.ppermute(flat, axis, [(i, i ^ mask) for i in range(count)]) for mask in group[1:]]
+    for other in others:
+        flat = flat + other
+    flat, state = tied(flat, state, step)
+    step += 1
     for mask in reversed(masks):
         upper = (me & mask) != 0
         other = lax.ppermute(flat, axis, [(i, i ^ mask) for i in range(count)])
-        state = work(step, state)
         flat = jnp.where(upper, jnp.concatenate([other, flat]), jnp.concatenate([flat, other]))
-        flat, state = lax.optimization_barrier((flat, state))
+        flat, state = tied(flat, state, step)
         step += 1
     return flat.reshape(value.shape), state
 
@@ -181,10 +196,21 @@
     chunk_size = pair_slots // chunk_count
     first_step = FIRST_STEP if axis_count & (axis_count - 1) == 0 else 0
 
+    def exchanged(sums):
+        out_t, returned_sum = sums
+        low_part = returned_sum[:blocks].reshape(local_rows, channels)
+        middle = returned_sum[blocks : 2 * blocks].reshape(local_rows, channels)
+        high_part = returned_sum[2 * blocks :].reshape(local_rows, channels)
+        from_next = passed_along(low_part, ("space", "sub"), -1)
+        from_prev = passed_along(high_part, ("space", "sub"), 1)
+        return out_t, (middle + from_next + from_prev).astype(jnp.bfloat16)
+
     def work(step, sums):
         chunk = step - first_step
         if 0 <= chunk < chunk_count:
             return forward_chunk(weights_t, grad_blocks, scalars, gathered, sums, chunk, chunk_size)
+        if chunk == chunk_count:
+            return exchanged(sums)
         return sums
 
     sums = (
@@ -193,18 +219,14 @@
     )
     if axis_count & (axis_count - 1) or grad_sum.size % axis_count:
         grand_total = lax.psum(grad_sum, ("space", "sub"))
-        for chunk in range(chunk_count):
+        for chunk in range(chunk_count + 1):
             sums = work(chunk + first_step, sums)
     else:
-        grand_total, sums = summed_everywhere(grad_sum, ("space", "sub"), work, sums)
-    out_t, returned_sum = sums
+        grand_total, sums = summed_everywhere(
+            grad_sum, ("space", "sub"), work, sums, first_step + chunk_count
+        )
+    out_t, grad_features = sums
     out_sum = out_t.transpose(0, 2, 1)
-    low_part = returned_sum[:blocks].reshape(local_rows, channels)
-    middle = returned_sum[blocks : 2 * blocks].reshape(local_rows, channels)
-    high_part = returned_sum[2 * blocks :].reshape(local_rows, channels)
-    from_next = passed_along(low_part, ("space", "sub"), -1)
-    from_prev = passed_along(high_part, ("space", "sub"), 1)
-    grad_features = (middle + from_next + from_prev).astype(jnp.bfloat16)
     output = out_sum.reshape(local_rows, channels).astype(jnp.bfloat16)
     return (output, grad_features, grand_total)
 

time: 193 us -> 179 us (0.927)
  waiting for transfers between devices: 47.1 us -> 34.9 us
  starting transfers between devices: 42.1 us -> 39.2 us
    ppermute x8 -> x6, waiting for transfers between devices: 30.8 us -> 15.1 us  [summed_everywhere(): other = lax.ppermute(flat, axis, [(i, i ^ mask) for i in range(count)])]
    ppermute x8 -> x6, starting transfers between devices: 10.5 us -> 0.91 us  [summed_everywhere(): other = lax.ppermute(flat, axis, [(i, i ^ mask) for i in range(count)])]
    ppermute x0 -> x3, starting transfers between devices: none -> 7.49 us  [summed_everywhere(): lax.ppermute(flat, axis, [(i, i ^ mask) for i in range(count)])]
    ppermute x8 -> x6, starting transfers between devices: 14.1 us -> 6.61 us  [summed_everywhere(): received = lax.ppermute(send, axis, [(i, i ^ mask) for i in range(count)])]
    ppermute x4, starting transfers between devices: 17.5 us -> 24.2 us  [passed_along(): lax.ppermute(value, axis, [(source, source + steps) for source in range(l...]
    ppermute x4, waiting for transfers between devices: 13.5 us -> 17 us  [passed_along(): lax.ppermute(value, axis, [(source, source + steps) for source in range(l...]
  transfers between devices with their start and end apart: 20 -> 19, of which waited for: 12 -> 8; matrix products, arithmetic and copies ran while one was open for 4% -> 5% of each run, Pallas kernels for 31% -> 33%
where the time goes in v5:
time: 179 us; the launch traced here: 178 us
  Pallas kernels  85.5 us (48%)
  starting transfers between devices  39.2 us (22%)
  waiting for transfers between devices  34.9 us (19%)
  other arithmetic  9.15 us (5%)
  local copies, waits for them, and re-layouts  7.4 us (4%)
    pallas_call x8, Pallas kernels, forward_chunk(): pl.pallas_call(functools.partial(sweep_kernel, chunk * chunk_size), grid=...  59.4 us
    pallas_call x1, Pallas kernels, grad_sweep(): pl.pallas_call(grad_kernel, out_shape=(jax.ShapeDtypeStruct((kernel_count...  26.1 us
    ppermute x4, starting transfers between devices, passed_along(): lax.ppermute(value, axis, [(source, source + steps) for source in range(l...  24.2 us
    ppermute x4, waiting for transfers between devices, passed_along(): lax.ppermute(value, axis, [(source, source + steps) for source in range(l...  17 us
    ppermute x6, waiting for transfers between devices, summed_everywhere(): other = lax.ppermute(flat, axis, [(i, i ^ mask) for i in range(count)])  15.1 us
    ppermute x3, starting transfers between devices, summed_everywhere(): lax.ppermute(flat, axis, [(i, i ^ mask) for i in range(count)])  7.49 us
    ppermute x6, starting transfers between devices, summed_everywhere(): received = lax.ppermute(send, axis, [(i, i ^ mask) for i in range(count)])  6.61 us
  transfers between devices with their start and end apart: 19, of which 8 were waited for; matrix products, arithmetic and copies ran while one was open for 5% of the time, Pallas kernels for 33%

profile of v5, /device:TPU:127, one launch (start us, length us, event | category | flops | bytes accessed | tf_op | source)
XLA Modules:
  0.0 177.8 jit_solution(871039570541053170)
XLA Ops:
  0.6 2.6 %collective-permute-start.1 = (bf16[1024,128]{1,0:T(8,128)(2,1)}, bf16[1024,128]{1,0:T(8,128)(2,1)S(1)}, u32[]{:S(2)}, u32[]{:S(2)}) collective-permute-start(bf16[1024,128]{1,0:T(8,128)(2,1)} %param.8), channel_id=1, source_target_pairs={{1,0},{2,1},{3,2},{4,3},{5,4},{6,5},{7,6},{8,7},{9,8},{10,9},{11,1... | collective-permute-start | bytes 786440 | tf_op jit(solution)/shard_map/ppermute | solution.py:17
  3.2 8.4 %collective-permute-start = (bf16[1024,128]{1,0:T(8,128)(2,1)}, bf16[1024,128]{1,0:T(8,128)(2,1)S(1)}, u32[]{:S(2)}, u32[]{:S(2)}) collective-permute-start(bf16[1024,128]{1,0:T(8,128)(2,1)} %param.8), channel_id=1, source_target_pairs={{0,1},{1,2},{2,3},{3,4},{4,5},{5,6},{6,7},{7,8},{8,9},{9,10},{10,1... | collective-permute-start | bytes 786440 | tf_op jit(solution)/shard_map/ppermute | solution.py:17
  11.6 1.2 broadcast_clamp_fusion.1.offsets
  13.5 1.3 fusion.3
  16.3 1.2 copy.28
  17.5 26.1 %shard_map.103 = (f32[27,128,128]{2,1,0:T(8,128)}, bf16[256,128,128]{2,1,0:T(8,128)(2,1)}) custom-call(s32[256]{0:T(256)} %broadcast_clamp_fusion.1.offsets, s32[256]{0:T(256)} %get-tuple-element.102.blocks_at, s32[256]{0:T(256)} %get-tuple-element.103.targets, s32[1]{0:T(128)S(6)} %min.29.live, bf16[24,128,128]{2,1,0:T(8,128)(2,1)} %bitcast.46, ...), custom_call_target="tpu_custom_call" | custom-call | tf_op jit(solution)/shard_map/pallas_call | solution.py:140
  43.6 1.6 broadcast_multiply_fusion
  45.4 2.5 %collective-permute-done.2 = f32[221184]{0:T(1024)} collective-permute-done((f32[221184]{0:T(1024)S(1)}, f32[221184]{0:T(1024)}, u32[]{:S(2)}, u32[]{:S(2)}) %collective-permute-start.2) | collective-permute-done | bytes 884768 | tf_op jit(solution)/shard_map/ppermute | solution.py:43
  47.9 1.3 select_add_fusion
  49.4 1.7 copy.29
  51.9 1.3 broadcast_in_dim.7.ret_in
  53.2 7.4 %shard_map.104 = (f32[8,128,128]{2,1,0:T(8,128)}, f32[24,128,128]{2,1,0:T(8,128)}) custom-call(s32[256]{0:T(256)} %broadcast_clamp_fusion.1.offsets, s32[256]{0:T(256)} %get-tuple-element.102.blocks_at, s32[256]{0:T(256)} %get-tuple-element.103.targets, s32[1]{0:T(128)S(6)} %min.29.live, ...), custom_call_target="tpu_custom_call", output_to_operand_aliasing={{0}: (8, {}), {1}: (9, {})} | custom-call | tf_op jit(solution)/shard_map/pallas_call | solution.py:162
  61.1 1.1 collective-permute-start.4
  62.2 7.4 %shard_map.105 = (f32[8,128,128]{2,1,0:T(8,128)}, f32[24,128,128]{2,1,0:T(8,128)}) custom-call(s32[256]{0:T(256)} %broadcast_clamp_fusion.1.offsets, s32[256]{0:T(256)} %get-tuple-element.102.blocks_at, s32[256]{0:T(256)} %get-tuple-element.103.targets, s32[1]{0:T(128)S(6)} %min.29.live, ...), custom_call_target="tpu_custom_call", output_to_operand_aliasing={{0}: (8, {}), {1}: (9, {})} | custom-call | tf_op jit(solution)/shard_map/pallas_call | solution.py:162
  69.9 7.4 %shard_map.106 = (f32[8,128,128]{2,1,0:T(8,128)}, f32[24,128,128]{2,1,0:T(8,128)}) custom-call(s32[256]{0:T(256)} %broadcast_clamp_fusion.1.offsets, s32[256]{0:T(256)} %get-tuple-element.102.blocks_at, s32[256]{0:T(256)} %get-tuple-element.103.targets, s32[1]{0:T(128)S(6)} %min.29.live, ...), custom_call_target="tpu_custom_call", output_to_operand_aliasing={{0}: (8, {}), {1}: (9, {})} | custom-call | tf_op jit(solution)/shard_map/pallas_call | solution.py:162
  77.4 5.0 %collective-permute-start.6 = (f32[13824]{0:T(1024)S(1)}, f32[13824]{0:T(1024)S(1)}, u32[]{:S(2)}, u32[]{:S(2)}) collective-permute-start(f32[13824]{0:T(1024)S(1)} %slice_select_fusion.4), channel_id=1, source_target_pairs={{0,16},{1,17},{2,18},{3,19},{4,20},{5,21},{6,22},{7,23},{8,24},{9,... | collective-permute-start | bytes 165896 | tf_op jit(solution)/shard_map/ppermute | solution.py:43
  82.4 7.4 %shard_map.107 = (f32[8,128,128]{2,1,0:T(8,128)}, f32[24,128,128]{2,1,0:T(8,128)}) custom-call(s32[256]{0:T(256)} %broadcast_clamp_fusion.1.offsets, s32[256]{0:T(256)} %get-tuple-element.102.blocks_at, s32[256]{0:T(256)} %get-tuple-element.103.targets, s32[1]{0:T(128)S(6)} %min.29.live, ...), custom_call_target="tpu_custom_call", output_to_operand_aliasing={{0}: (8, {}), {1}: (9, {})} | custom-call | tf_op jit(solution)/shard_map/pallas_call | solution.py:162
  89.9 7.4 %shard_map.108 = (f32[8,128,128]{2,1,0:T(8,128)}, f32[24,128,128]{2,1,0:T(8,128)}) custom-call(s32[256]{0:T(256)} %broadcast_clamp_fusion.1.offsets, s32[256]{0:T(256)} %get-tuple-element.102.blocks_at, s32[256]{0:T(256)} %get-tuple-element.103.targets, s32[1]{0:T(128)S(6)} %min.29.live, ...), custom_call_target="tpu_custom_call", output_to_operand_aliasing={{0}: (8, {}), {1}: (9, {})} | custom-call | tf_op jit(solution)/shard_map/pallas_call | solution.py:162
  97.4 5.3 %collective-permute-start.10 = (f32[6912]{0:T(1024)S(1)}, f32[6912]{0:T(1024)S(1)}, u32[]{:S(2)}, u32[]{:S(2)}) collective-permute-start(f32[6912]{0:T(1024)S(1)} %select_add_fusion.5), channel_id=1, source_target_pairs={{0,192},{1,193},{2,194},{3,195},{4,196},{5,197},{6,198},{7,199},{8... | collective-permute-start | bytes 82952 | tf_op jit(solution)/shard_map/ppermute | solution.py:46
  103.4 1.5 collective-permute-start.8
  104.9 7.4 %shard_map.109 = (f32[8,128,128]{2,1,0:T(8,128)}, f32[24,128,128]{2,1,0:T(8,128)}) custom-call(s32[256]{0:T(256)} %broadcast_clamp_fusion.1.offsets, s32[256]{0:T(256)} %get-tuple-element.102.blocks_at, s32[256]{0:T(256)} %get-tuple-element.103.targets, s32[1]{0:T(128)S(6)} %min.29.live, ...), custom_call_target="tpu_custom_call", output_to_operand_aliasing={{0}: (8, {}), {1}: (9, {})} | custom-call | tf_op jit(solution)/shard_map/pallas_call | solution.py:162
  112.8 7.4 %shard_map.110 = (f32[8,128,128]{2,1,0:T(8,128)}, f32[24,128,128]{2,1,0:T(8,128)}) custom-call(s32[256]{0:T(256)} %broadcast_clamp_fusion.1.offsets, s32[256]{0:T(256)} %get-tuple-element.102.blocks_at, s32[256]{0:T(256)} %get-tuple-element.103.targets, s32[1]{0:T(128)S(6)} %min.29.live, ...), custom_call_target="tpu_custom_call", output_to_operand_aliasing={{0}: (8, {}), {1}: (9, {})} | custom-call | tf_op jit(solution)/shard_map/pallas_call | solution.py:162
  120.4 7.4 %shard_map.111 = (f32[8,128,128]{2,1,0:T(8,128)}, f32[24,128,128]{2,1,0:T(8,128)}) custom-call(s32[256]{0:T(256)} %broadcast_clamp_fusion.1.offsets, s32[256]{0:T(256)} %get-tuple-element.102.blocks_at, s32[256]{0:T(256)} %get-tuple-element.103.targets, s32[1]{0:T(128)S(6)} %min.29.live, ...), custom_call_target="tpu_custom_call", output_to_operand_aliasing={{0}: (8, {}), {1}: (9, {})} | custom-call | tf_op jit(solution)/shard_map/pallas_call | solution.py:162
  128.0 1.5 fusion.4
  129.4 11.3 %collective-permute-start.15 = (f32[1024,128]{1,0:T(8,128)S(1)}, f32[1024,128]{1,0:T(8,128)S(1)}, u32[]{:S(2)}, u32[]{:S(2)}) collective-permute-start(f32[1024,128]{1,0:T(8,128)S(1)} %bitcast.50), channel_id=1, source_target_pairs={{0,1},{1,2},{2,3},{3,4},{4,5},{5,6},{6,7},{7,8},{8,9},{9,10},{10,1... | collective-permute-start | bytes 1572872 | tf_op jit(solution)/shard_map/ppermute | solution.py:17
  140.8 1.9 %collective-permute-start.14 = (f32[1024,128]{1,0:T(8,128)S(1)}, f32[1024,128]{1,0:T(8,128)S(1)}, u32[]{:S(2)}, u32[]{:S(2)}) collective-permute-start(f32[1024,128]{1,0:T(8,128)S(1)} %bitcast.49), channel_id=1, source_target_pairs={{1,0},{2,1},{3,2},{4,3},{5,4},{6,5},{7,6},{8,7},{9,8},{10,9},{11,1... | collective-permute-start | bytes 1572872 | tf_op jit(solution)/shard_map/ppermute | solution.py:17
  142.7 4.0 %collective-permute-done.15 = f32[1024,128]{1,0:T(8,128)S(1)} collective-permute-done((f32[1024,128]{1,0:T(8,128)S(1)}, f32[1024,128]{1,0:T(8,128)S(1)}, u32[]{:S(2)}, u32[]{:S(2)}) %collective-permute-start.15) | collective-permute-done | bytes 524320 | tf_op jit(solution)/shard_map/ppermute | solution.py:17
  146.7 12.6 %collective-permute-done.14 = f32[1024,128]{1,0:T(8,128)S(1)} collective-permute-done((f32[1024,128]{1,0:T(8,128)S(1)}, f32[1024,128]{1,0:T(8,128)S(1)}, u32[]{:S(2)}, u32[]{:S(2)}) %collective-permute-start.14) | collective-permute-done | bytes 524320 | tf_op jit(solution)/shard_map/ppermute | solution.py:17
  160.0 6.5 %collective-permute-done.16 = f32[55296]{0:T(1024)S(1)} collective-permute-done((f32[55296]{0:T(1024)S(1)}, f32[55296]{0:T(1024)S(1)}, u32[]{:S(2)}, u32[]{:S(2)}) %collective-permute-start.16) | collective-permute-done | bytes 221216 | tf_op jit(solution)/shard_map/ppermute | solution.py:53
  166.6 7.1 %collective-permute-done.17 = f32[110592]{0:T(1024)S(1)} collective-permute-done((f32[110592]{0:T(1024)S(1)}, f32[110592]{0:T(1024)S(1)}, u32[]{:S(2)}, u32[]{:S(2)}) %collective-permute-start.17) | collective-permute-done | bytes 442400 | tf_op jit(solution)/shard_map/ppermute | solution.py:53
  174.9 1.5 collective-permute-done.18
  176.4 1.4 maximum_select_fusion
  (50 shorter events, 6.9 us)
Async XLA Ops:
  0.6 14.2 %collective-permute-start.1 = (bf16[1024,128]{1,0:T(8,128)(2,1)}, bf16[1024,128]{1,0:T(8,128)(2,1)S(1)}, u32[]{:S(2)}, u32[]{:S(2)}) collective-permute-start(bf16[1024,128]{1,0:T(8,128)(2,1)} %param.8), channel_id=1, source_target_pairs={{1,0},{2,1},{3,2},{4,3},{5,4},{6,5},{7,6},{8,7},{9,8},{10,9},{11,1... | collective-permute-start | bytes 786440 | tf_op jit(solution)/shard_map/ppermute | solution.py:17
  3.2 12.0 %collective-permute-start = (bf16[1024,128]{1,0:T(8,128)(2,1)}, bf16[1024,128]{1,0:T(8,128)(2,1)S(1)}, u32[]{:S(2)}, u32[]{:S(2)}) collective-permute-start(bf16[1024,128]{1,0:T(8,128)(2,1)} %param.8), channel_id=1, source_target_pairs={{0,1},{1,2},{2,3},{3,4},{4,5},{5,6},{6,7},{7,8},{8,9},{9,10},{10,1... | collective-permute-start | bytes 786440 | tf_op jit(solution)/shard_map/ppermute | solution.py:17
  45.3 2.6 %collective-permute-start.2 = (f32[221184]{0:T(1024)S(1)}, f32[221184]{0:T(1024)}, u32[]{:S(2)}, u32[]{:S(2)}) collective-permute-start(f32[221184]{0:T(1024)S(1)} %slice_select_fusion), channel_id=1, source_target_pairs={{0,1},{1,0},{2,3},{3,2},{4,5},{5,4},{6,7},{7,6},{8,9},{9,8},{10,11... | collective-permute-start | bytes 2654216 | tf_op jit(solution)/shard_map/ppermute | solution.py:43
  45.4 4.0 %copy-start.1 = (bf16[27,128,128]{2,1,0:T(8,128)(2,1)S(1)}, bf16[27,128,128]{2,1,0:T(8,128)(2,1)}, u32[]{:S(2)}) copy-start(bf16[27,128,128]{2,1,0:T(8,128)(2,1)} %param.9) | copy-start | bytes 2654212
  49.3 11.7 %collective-permute-start.3 = (f32[110592]{0:T(1024)S(1)}, f32[110592]{0:T(1024)S(1)}, u32[]{:S(2)}, u32[]{:S(2)}) collective-permute-start(f32[110592]{0:T(1024)S(1)} %slice_select_fusion.1), channel_id=1, source_target_pairs={{0,2},{1,3},{2,0},{3,1},{4,6},{5,7},{6,4},{7,5},{8,10},{9,11},{10,... | collective-permute-start | bytes 1327112 | tf_op jit(solution)/shard_map/ppermute | solution.py:43
  61.1 8.5 %collective-permute-start.4 = (f32[55296]{0:T(1024)S(1)}, f32[55296]{0:T(1024)S(1)}, u32[]{:S(2)}, u32[]{:S(2)}) collective-permute-start(f32[55296]{0:T(1024)S(1)} %slice_select_fusion.2), channel_id=1, source_target_pairs={{0,4},{1,5},{2,6},{3,7},{4,0},{5,1},{6,2},{7,3},{8,12},{9,13},{10,... | collective-permute-start | bytes 663560 | tf_op jit(solution)/shard_map/ppermute | solution.py:43
  69.7 7.7 %collective-permute-start.5 = (f32[27648]{0:T(1024)S(1)}, f32[27648]{0:T(1024)S(1)}, u32[]{:S(2)}, u32[]{:S(2)}) collective-permute-start(f32[27648]{0:T(1024)S(1)} %slice_select_fusion.3), channel_id=1, source_target_pairs={{0,8},{1,9},{2,10},{3,11},{4,12},{5,13},{6,14},{7,15},{8,0},{9,1},... | collective-permute-start | bytes 331784 | tf_op jit(solution)/shard_map/ppermute | solution.py:43
  77.4 12.4 %collective-permute-start.6 = (f32[13824]{0:T(1024)S(1)}, f32[13824]{0:T(1024)S(1)}, u32[]{:S(2)}, u32[]{:S(2)}) collective-permute-start(f32[13824]{0:T(1024)S(1)} %slice_select_fusion.4), channel_id=1, source_target_pairs={{0,16},{1,17},{2,18},{3,19},{4,20},{5,21},{6,22},{7,23},{8,24},{9,... | collective-permute-start | bytes 165896 | tf_op jit(solution)/shard_map/ppermute | solution.py:43
  89.8 7.5 %collective-permute-start.7 = (f32[6912]{0:T(1024)S(1)}, f32[6912]{0:T(1024)S(1)}, u32[]{:S(2)}, u32[]{:S(2)}) collective-permute-start(f32[6912]{0:T(1024)S(1)} %slice_select_fusion.5), channel_id=1, source_target_pairs={{0,32},{1,33},{2,34},{3,35},{4,36},{5,37},{6,38},{7,39},{8,40},{9,... | collective-permute-start | bytes 82952 | tf_op jit(solution)/shard_map/ppermute | solution.py:43
  97.4 14.9 %collective-permute-start.10 = (f32[6912]{0:T(1024)S(1)}, f32[6912]{0:T(1024)S(1)}, u32[]{:S(2)}, u32[]{:S(2)}) collective-permute-start(f32[6912]{0:T(1024)S(1)} %select_add_fusion.5), channel_id=1, source_target_pairs={{0,192},{1,193},{2,194},{3,195},{4,196},{5,197},{6,198},{7,199},{8... | collective-permute-start | bytes 82952 | tf_op jit(solution)/shard_map/ppermute | solution.py:46
  102.7 9.6 %collective-permute-start.9 = (f32[6912]{0:T(1024)S(1)}, f32[6912]{0:T(1024)S(1)}, u32[]{:S(2)}, u32[]{:S(2)}) collective-permute-start(f32[6912]{0:T(1024)S(1)} %select_add_fusion.5), channel_id=1, source_target_pairs={{0,128},{1,129},{2,130},{3,131},{4,132},{5,133},{6,134},{7,135},{8... | collective-permute-start | bytes 82952 | tf_op jit(solution)/shard_map/ppermute | solution.py:46
  103.4 8.9 %collective-permute-start.8 = (f32[6912]{0:T(1024)S(1)}, f32[6912]{0:T(1024)S(1)}, u32[]{:S(2)}, u32[]{:S(2)}) collective-permute-start(f32[6912]{0:T(1024)S(1)} %select_add_fusion.5), channel_id=1, source_target_pairs={{0,64},{1,65},{2,66},{3,67},{4,68},{5,69},{6,70},{7,71},{8,72},{9,... | collective-permute-start | bytes 82952 | tf_op jit(solution)/shard_map/ppermute | solution.py:46
  112.3 7.9 %collective-permute-start.11 = (f32[6912]{0:T(1024)S(1)}, f32[6912]{0:T(1024)S(1)}, u32[]{:S(2)}, u32[]{:S(2)}) collective-permute-start(f32[6912]{0:T(1024)S(1)} %add_add_fusion), channel_id=1, source_target_pairs={{0,32},{1,33},{2,34},{3,35},{4,36},{5,37},{6,38},{7,39},{8,40},{9,... | collective-permute-start | bytes 82952 | tf_op jit(solution)/shard_map/ppermute | solution.py:53
  120.3 7.5 %collective-permute-start.12 = (f32[13824]{0:T(1024)S(1)}, f32[13824]{0:T(1024)S(1)}, u32[]{:S(2)}, u32[]{:S(2)}) collective-permute-start(f32[13824]{0:T(1024)S(1)} %maximum_select_fusion.5), channel_id=1, source_target_pairs={{0,16},{1,17},{2,18},{3,19},{4,20},{5,21},{6,22},{7,23},{8,24},{9,... | collective-permute-start | bytes 165896 | tf_op jit(solution)/shard_map/ppermute | solution.py:53
  127.9 14.8 %collective-permute-start.13 = (f32[27648]{0:T(1024)S(1)}, f32[27648]{0:T(1024)S(1)}, u32[]{:S(2)}, u32[]{:S(2)}) collective-permute-start(f32[27648]{0:T(1024)S(1)} %maximum_select_fusion.4), channel_id=1, source_target_pairs={{0,8},{1,9},{2,10},{3,11},{4,12},{5,13},{6,14},{7,15},{8,0},{9,1},... | collective-permute-start | bytes 331784 | tf_op jit(solution)/shard_map/ppermute | solution.py:53
  129.4 17.2 %collective-permute-start.15 = (f32[1024,128]{1,0:T(8,128)S(1)}, f32[1024,128]{1,0:T(8,128)S(1)}, u32[]{:S(2)}, u32[]{:S(2)}) collective-permute-start(f32[1024,128]{1,0:T(8,128)S(1)} %bitcast.50), channel_id=1, source_target_pairs={{0,1},{1,2},{2,3},{3,4},{4,5},{5,6},{6,7},{7,8},{8,9},{9,10},{10,1... | collective-permute-start | bytes 1572872 | tf_op jit(solution)/shard_map/ppermute | solution.py:17
  140.8 18.5 %collective-permute-start.14 = (f32[1024,128]{1,0:T(8,128)S(1)}, f32[1024,128]{1,0:T(8,128)S(1)}, u32[]{:S(2)}, u32[]{:S(2)}) collective-permute-start(f32[1024,128]{1,0:T(8,128)S(1)} %bitcast.49), channel_id=1, source_target_pairs={{1,0},{2,1},{3,2},{4,3},{5,4},{6,5},{7,6},{8,7},{9,8},{10,9},{11,1... | collective-permute-start | bytes 1572872 | tf_op jit(solution)/shard_map/ppermute | solution.py:17
  160.0 13.9 %copy-start = (f32[8,128,128]{2,1,0:T(8,128)S(1)}, f32[8,128,128]{2,1,0:T(8,128)}, u32[]{:S(2)}) copy-start(f32[8,128,128]{2,1,0:T(8,128)} %get-tuple-element.96) | copy-start | bytes 1572868
  160.0 6.5 %collective-permute-start.16 = (f32[55296]{0:T(1024)S(1)}, f32[55296]{0:T(1024)S(1)}, u32[]{:S(2)}, u32[]{:S(2)}) collective-permute-start(f32[55296]{0:T(1024)S(1)} %maximum_select_fusion.3), channel_id=1, source_target_pairs={{0,4},{1,5},{2,6},{3,7},{4,0},{5,1},{6,2},{7,3},{8,12},{9,13},{10,... | collective-permute-start | bytes 663560 | tf_op jit(solution)/shard_map/ppermute | solution.py:53
  166.5 7.2 %collective-permute-start.17 = (f32[110592]{0:T(1024)S(1)}, f32[110592]{0:T(1024)S(1)}, u32[]{:S(2)}, u32[]{:S(2)}) collective-permute-start(f32[110592]{0:T(1024)S(1)} %maximum_select_fusion.2), channel_id=1, source_target_pairs={{0,2},{1,3},{2,0},{3,1},{4,6},{5,7},{6,4},{7,5},{8,10},{9,11},{10,... | collective-permute-start | bytes 1327112 | tf_op jit(solution)/shard_map/ppermute | solution.py:53
  173.8 2.5 %collective-permute-start.18 = (f32[221184]{0:T(1024)S(1)}, f32[221184]{0:T(1024)S(1)}, u32[]{:S(2)}, u32[]{:S(2)}) collective-permute-start(f32[221184]{0:T(1024)S(1)} %maximum_select_fusion.1), channel_id=1, source_target_pairs={{0,1},{1,0},{2,3},{3,2},{4,5},{5,4},{6,7},{7,6},{8,9},{9,8},{10,11... | collective-permute-start | bytes 2654216 | tf_op jit(solution)/shard_map/ppermute | solution.py:53

commit v6 on v5

--- a/solution.py
+++ b/solution.py
@@ -91,9 +91,15 @@
 
 
 def sweep_kernel(first, offsets, blocks_at, targets, live, weights_t_ref, cot_ref, rows_ref,
-                 gathered_ref, out_in, ret_in, out_ref, ret_ref):
-    out_ref[...] = out_in[...]
-    ret_ref[...] = ret_in[...]
+                 gathered_ref, *sums):
+    if len(sums) == 4:
+        out_in, ret_in, out_ref, ret_ref = sums
+        out_ref[...] = out_in[...]
+        ret_ref[...] = ret_in[...]
+    else:
+        out_ref, ret_ref = sums
+        out_ref[...] = jnp.zeros(out_ref.shape, out_ref.dtype)
+        ret_ref[...] = jnp.zeros(ret_ref.shape, ret_ref.dtype)
     source_rows = lax.broadcasted_iota(jnp.int32, (BLK, BLK), 0)
 
     def advance(p, carry):
@@ -149,28 +155,34 @@
 
 
 def forward_chunk(weights_t, grad_blocks, scalars, gathered, sums, chunk, chunk_size):
-    out_sum, returned_sum = sums
+    out_shape, returned_shape = sum_shapes(grad_blocks, gathered, scalars)
     smem = pl.BlockSpec(memory_space=pltpu.SMEM)
 
-    def whole(array):
-        return pl.BlockSpec(array.shape, lambda i: (0,) * array.ndim)
+    def whole(shape):
+        return pl.BlockSpec(shape, lambda i: (0,) * len(shape))
 
     def part(array):
         return pl.BlockSpec((chunk_size,) + array.shape[1:], lambda i: (chunk,) + (0,) * (array.ndim - 1))
 
     rows = scalars[4]
+    carried = () if sums is None else tuple(sums)
     return pl.pallas_call(
         functools.partial(sweep_kernel, chunk * chunk_size),
         grid=(1,),
         out_shape=(
-            jax.ShapeDtypeStruct(out_sum.shape, jnp.float32),
-            jax.ShapeDtypeStruct(returned_sum.shape, jnp.float32),
+            jax.ShapeDtypeStruct(out_shape, jnp.float32),
+            jax.ShapeDtypeStruct(returned_shape, jnp.float32),
         ),
-        in_specs=[smem, smem, smem, smem, whole(weights_t), whole(grad_blocks), part(rows),
-                  part(gathered), whole(out_sum), whole(returned_sum)],
-        out_specs=(whole(out_sum), whole(returned_sum)),
-        input_output_aliases={8: 0, 9: 1},
-    )(*scalars[:4], weights_t, grad_blocks, rows, gathered, out_sum, returned_sum)
+        in_specs=[smem, smem, smem, smem, whole(weights_t.shape), whole(grad_blocks.shape), part(rows),
+                  part(gathered)] + [whole(out_shape), whole(returned_shape)][: len(carried)],
+        out_specs=(whole(out_shape), whole(returned_shape)),
+        input_output_aliases={8: 0, 9: 1} if carried else {},
+    )(*scalars[:4], weights_t, grad_blocks, rows, gathered, *carried)
+
+
+def sum_shapes(grad_blocks, gathered, scalars):
+    blocks, rows_per_block, channels = grad_blocks.shape
+    return (blocks, channels, rows_per_block), (3 * blocks, rows_per_block, channels)
 
 
 def on_device(
@@ -213,10 +225,7 @@
             return exchanged(sums)
         return sums
 
-    sums = (
-        jnp.zeros((blocks, channels, BLK), jnp.float32),
-        jnp.zeros((3 * blocks, BLK, channels), jnp.float32),
-    )
+    sums = None
     if axis_count & (axis_count - 1) or grad_sum.size % axis_count:
         grand_total = lax.psum(grad_sum, ("space", "sub"))
         for chunk in range(chunk_count + 1):

time: 179 us -> 178 us (level)
  waiting for transfers between devices: 34.9 us -> 38.1 us
  local copies, waits for them, and re-layouts: 7.4 us -> 5.24 us
    ppermute x6, waiting for transfers between devices: 2.85 us -> 5.71 us  [summed_everywhere(): received = lax.ppermute(send, axis, [(i, i ^ mask) for i in range(count)])]
    broadcast_in_dim x2 -> x0, local copies, waits for them, and re-layouts: 2.15 us -> none  [the longest x1 1.32 us: on_device(): jnp.zeros((3 * blocks, BLK, channels), jnp.float32)]
  transfers between devices with their start and end apart: 19 -> 19, of which waited for: 8 -> 8; matrix products, arithmetic and copies ran while one was open for 5% -> 4% of each run, Pallas kernels for 33% -> 33%
where the time goes in v6:
time: 178 us
  Pallas kernels  84.8 us (48%)
  starting transfers between devices  39 us (22%)
  waiting for transfers between devices  38.1 us (21%)
  other arithmetic  9.15 us (5%)
  local copies, waits for them, and re-layouts  5.24 us (3%)
    pallas_call x8, Pallas kernels, forward_chunk(): pl.pallas_call(functools.partial(sweep_kernel, chunk * chunk_size), grid=...  58.8 us
    pallas_call x1, Pallas kernels, grad_sweep(): pl.pallas_call(grad_kernel, out_shape=(jax.ShapeDtypeStruct((kernel_count...  26.1 us
    ppermute x4, starting transfers between devices, passed_along(): lax.ppermute(value, axis, [(source, source + steps) for source in range(l...  25.1 us
    ppermute x4, waiting for transfers between devices, passed_along(): lax.ppermute(value, axis, [(source, source + steps) for source in range(l...  17.5 us
    ppermute x6, waiting for transfers between devices, summed_everywhere(): other = lax.ppermute(flat, axis, [(i, i ^ mask) for i in range(count)])  14.9 us
    ppermute x3, starting transfers between devices, summed_everywhere(): lax.ppermute(flat, axis, [(i, i ^ mask) for i in range(count)])  7.49 us
    ppermute x6, waiting for transfers between devices, summed_everywhere(): received = lax.ppermute(send, axis, [(i, i ^ mask) for i in range(count)])  5.71 us
    ppermute x6, starting transfers between devices, summed_everywhere(): received = lax.ppermute(send, axis, [(i, i ^ mask) for i in range(count)])  5.48 us
  transfers between devices with their start and end apart: 19, of which 8 were waited for; matrix products, arithmetic and copies ran while one was open for 4% of the time, Pallas kernels for 33%

profile of v6, /device:TPU:127, one launch (start us, length us, event | category | flops | bytes accessed | tf_op | source)
XLA Modules:
  0.0 177.9 jit_solution(12088651274604105717)
XLA Ops:
  0.6 2.6 %collective-permute-start.1 = (bf16[1024,128]{1,0:T(8,128)(2,1)}, bf16[1024,128]{1,0:T(8,128)(2,1)S(1)}, u32[]{:S(2)}, u32[]{:S(2)}) collective-permute-start(bf16[1024,128]{1,0:T(8,128)(2,1)} %param.8), channel_id=1, source_target_pairs={{1,0},{2,1},{3,2},{4,3},{5,4},{6,5},{7,6},{8,7},{9,8},{10,9},{11,1... | collective-permute-start | bytes 786440 | tf_op jit(solution)/shard_map/ppermute | solution.py:17
  3.2 8.4 %collective-permute-start = (bf16[1024,128]{1,0:T(8,128)(2,1)}, bf16[1024,128]{1,0:T(8,128)(2,1)S(1)}, u32[]{:S(2)}, u32[]{:S(2)}) collective-permute-start(bf16[1024,128]{1,0:T(8,128)(2,1)} %param.8), channel_id=1, source_target_pairs={{0,1},{1,2},{2,3},{3,4},{4,5},{5,6},{6,7},{7,8},{8,9},{9,10},{10,1... | collective-permute-start | bytes 786440 | tf_op jit(solution)/shard_map/ppermute | solution.py:17
  11.6 1.2 broadcast_clamp_fusion.1.offsets
  13.5 1.3 fusion.3
  15.3 1.0 pad_maximum_fusion
  16.3 1.2 copy.26
  17.5 26.1 %shard_map.103 = (f32[27,128,128]{2,1,0:T(8,128)}, bf16[256,128,128]{2,1,0:T(8,128)(2,1)}) custom-call(s32[256]{0:T(256)} %broadcast_clamp_fusion.1.offsets, s32[256]{0:T(256)} %get-tuple-element.96.blocks_at, s32[256]{0:T(256)} %get-tuple-element.97.targets, s32[1]{0:T(128)S(6)} %min.29.live, bf16[24,128,128]{2,1,0:T(8,128)(2,1)} %bitcast.46, ...), custom_call_target="tpu_custom_call" | custom-call | tf_op jit(solution)/shard_map/pallas_call | solution.py:146
  43.6 1.6 broadcast_multiply_fusion
  45.4 2.5 %collective-permute-done.2 = f32[221184]{0:T(1024)} collective-permute-done((f32[221184]{0:T(1024)S(1)}, f32[221184]{0:T(1024)}, u32[]{:S(2)}, u32[]{:S(2)}) %collective-permute-start.2) | collective-permute-done | bytes 884768 | tf_op jit(solution)/shard_map/ppermute | solution.py:43
  47.9 1.3 select_add_fusion
  49.4 1.7 copy.27
  51.1 6.8 %shard_map.104 = (f32[8,128,128]{2,1,0:T(8,128)}, f32[24,128,128]{2,1,0:T(8,128)}) custom-call(s32[256]{0:T(256)} %broadcast_clamp_fusion.1.offsets, s32[256]{0:T(256)} %get-tuple-element.96.blocks_at, s32[256]{0:T(256)} %get-tuple-element.97.targets, s32[1]{0:T(128)S(6)} %min.29.live, bf16[27,128,128]{2,1,0:T(8,128)(2,1)} %bitcast.18, ...), custom_call_target="tpu_custom_call" | custom-call | tf_op jit(solution)/shard_map/pallas_call | solution.py:169
  57.8 3.1 %collective-permute-done.3 = f32[110592]{0:T(1024)S(1)} collective-permute-done((f32[110592]{0:T(1024)S(1)}, f32[110592]{0:T(1024)S(1)}, u32[]{:S(2)}, u32[]{:S(2)}) %collective-permute-start.3) | collective-permute-done | bytes 442400 | tf_op jit(solution)/shard_map/ppermute | solution.py:43
  61.2 7.4 %shard_map.105 = (f32[8,128,128]{2,1,0:T(8,128)}, f32[24,128,128]{2,1,0:T(8,128)}) custom-call(s32[256]{0:T(256)} %broadcast_clamp_fusion.1.offsets, s32[256]{0:T(256)} %get-tuple-element.96.blocks_at, s32[256]{0:T(256)} %get-tuple-element.97.targets, s32[1]{0:T(128)S(6)} %min.29.live, ...), custom_call_target="tpu_custom_call", output_to_operand_aliasing={{0}: (8, {}), {1}: (9, {})} | custom-call | tf_op jit(solution)/shard_map/pallas_call | solution.py:169
  68.8 7.4 %shard_map.106 = (f32[8,128,128]{2,1,0:T(8,128)}, f32[24,128,128]{2,1,0:T(8,128)}) custom-call(s32[256]{0:T(256)} %broadcast_clamp_fusion.1.offsets, s32[256]{0:T(256)} %get-tuple-element.96.blocks_at, s32[256]{0:T(256)} %get-tuple-element.97.targets, s32[1]{0:T(128)S(6)} %min.29.live, ...), custom_call_target="tpu_custom_call", output_to_operand_aliasing={{0}: (8, {}), {1}: (9, {})} | custom-call | tf_op jit(solution)/shard_map/pallas_call | solution.py:169
  76.3 5.0 %collective-permute-start.6 = (f32[13824]{0:T(1024)S(1)}, f32[13824]{0:T(1024)S(1)}, u32[]{:S(2)}, u32[]{:S(2)}) collective-permute-start(f32[13824]{0:T(1024)S(1)} %slice_select_fusion.4), channel_id=1, source_target_pairs={{0,16},{1,17},{2,18},{3,19},{4,20},{5,21},{6,22},{7,23},{8,24},{9,... | collective-permute-start | bytes 165896 | tf_op jit(solution)/shard_map/ppermute | solution.py:43
  81.3 7.4 %shard_map.107 = (f32[8,128,128]{2,1,0:T(8,128)}, f32[24,128,128]{2,1,0:T(8,128)}) custom-call(s32[256]{0:T(256)} %broadcast_clamp_fusion.1.offsets, s32[256]{0:T(256)} %get-tuple-element.96.blocks_at, s32[256]{0:T(256)} %get-tuple-element.97.targets, s32[1]{0:T(128)S(6)} %min.29.live, ...), custom_call_target="tpu_custom_call", output_to_operand_aliasing={{0}: (8, {}), {1}: (9, {})} | custom-call | tf_op jit(solution)/shard_map/pallas_call | solution.py:169
  88.9 7.4 %shard_map.108 = (f32[8,128,128]{2,1,0:T(8,128)}, f32[24,128,128]{2,1,0:T(8,128)}) custom-call(s32[256]{0:T(256)} %broadcast_clamp_fusion.1.offsets, s32[256]{0:T(256)} %get-tuple-element.96.blocks_at, s32[256]{0:T(256)} %get-tuple-element.97.targets, s32[1]{0:T(128)S(6)} %min.29.live, ...), custom_call_target="tpu_custom_call", output_to_operand_aliasing={{0}: (8, {}), {1}: (9, {})} | custom-call | tf_op jit(solution)/shard_map/pallas_call | solution.py:169
  96.3 5.3 %collective-permute-start.10 = (f32[6912]{0:T(1024)S(1)}, f32[6912]{0:T(1024)S(1)}, u32[]{:S(2)}, u32[]{:S(2)}) collective-permute-start(f32[6912]{0:T(1024)S(1)} %select_add_fusion.5), channel_id=1, source_target_pairs={{0,192},{1,193},{2,194},{3,195},{4,196},{5,197},{6,198},{7,199},{8... | collective-permute-start | bytes 82952 | tf_op jit(solution)/shard_map/ppermute | solution.py:46
  102.3 1.5 collective-permute-start.8
  103.8 7.4 %shard_map.109 = (f32[8,128,128]{2,1,0:T(8,128)}, f32[24,128,128]{2,1,0:T(8,128)}) custom-call(s32[256]{0:T(256)} %broadcast_clamp_fusion.1.offsets, s32[256]{0:T(256)} %get-tuple-element.96.blocks_at, s32[256]{0:T(256)} %get-tuple-element.97.targets, s32[1]{0:T(128)S(6)} %min.29.live, ...), custom_call_target="tpu_custom_call", output_to_operand_aliasing={{0}: (8, {}), {1}: (9, {})} | custom-call | tf_op jit(solution)/shard_map/pallas_call | solution.py:169
  111.8 7.4 %shard_map.110 = (f32[8,128,128]{2,1,0:T(8,128)}, f32[24,128,128]{2,1,0:T(8,128)}) custom-call(s32[256]{0:T(256)} %broadcast_clamp_fusion.1.offsets, s32[256]{0:T(256)} %get-tuple-element.96.blocks_at, s32[256]{0:T(256)} %get-tuple-element.97.targets, s32[1]{0:T(128)S(6)} %min.29.live, ...), custom_call_target="tpu_custom_call", output_to_operand_aliasing={{0}: (8, {}), {1}: (9, {})} | custom-call | tf_op jit(solution)/shard_map/pallas_call | solution.py:169
  119.3 7.4 %shard_map.111 = (f32[8,128,128]{2,1,0:T(8,128)}, f32[24,128,128]{2,1,0:T(8,128)}) custom-call(s32[256]{0:T(256)} %broadcast_clamp_fusion.1.offsets, s32[256]{0:T(256)} %get-tuple-element.96.blocks_at, s32[256]{0:T(256)} %get-tuple-element.97.targets, s32[1]{0:T(128)S(6)} %min.29.live, ...), custom_call_target="tpu_custom_call", output_to_operand_aliasing={{0}: (8, {}), {1}: (9, {})} | custom-call | tf_op jit(solution)/shard_map/pallas_call | solution.py:169
  126.9 1.5 fusion.4
  128.4 12.2 %collective-permute-start.15 = (f32[1024,128]{1,0:T(8,128)S(1)}, f32[1024,128]{1,0:T(8,128)S(1)}, u32[]{:S(2)}, u32[]{:S(2)}) collective-permute-start(f32[1024,128]{1,0:T(8,128)S(1)} %bitcast.50), channel_id=1, source_target_pairs={{0,1},{1,2},{2,3},{3,4},{4,5},{5,6},{6,7},{7,8},{8,9},{9,10},{10,1... | collective-permute-start | bytes 1572872 | tf_op jit(solution)/shard_map/ppermute | solution.py:17
  140.6 1.9 %collective-permute-start.14 = (f32[1024,128]{1,0:T(8,128)S(1)}, f32[1024,128]{1,0:T(8,128)S(1)}, u32[]{:S(2)}, u32[]{:S(2)}) collective-permute-start(f32[1024,128]{1,0:T(8,128)S(1)} %bitcast.49), channel_id=1, source_target_pairs={{1,0},{2,1},{3,2},{4,3},{5,4},{6,5},{7,6},{8,7},{9,8},{10,9},{11,1... | collective-permute-start | bytes 1572872 | tf_op jit(solution)/shard_map/ppermute | solution.py:17
  142.5 4.1 %collective-permute-done.15 = f32[1024,128]{1,0:T(8,128)S(1)} collective-permute-done((f32[1024,128]{1,0:T(8,128)S(1)}, f32[1024,128]{1,0:T(8,128)S(1)}, u32[]{:S(2)}, u32[]{:S(2)}) %collective-permute-start.15) | collective-permute-done | bytes 524320 | tf_op jit(solution)/shard_map/ppermute | solution.py:17
  146.7 12.9 %collective-permute-done.14 = f32[1024,128]{1,0:T(8,128)S(1)} collective-permute-done((f32[1024,128]{1,0:T(8,128)S(1)}, f32[1024,128]{1,0:T(8,128)S(1)}, u32[]{:S(2)}, u32[]{:S(2)}) %collective-permute-start.14) | collective-permute-done | bytes 524320 | tf_op jit(solution)/shard_map/ppermute | solution.py:17
  160.4 6.3 %collective-permute-done.16 = f32[55296]{0:T(1024)S(1)} collective-permute-done((f32[55296]{0:T(1024)S(1)}, f32[55296]{0:T(1024)S(1)}, u32[]{:S(2)}, u32[]{:S(2)}) %collective-permute-start.16) | collective-permute-done | bytes 221216 | tf_op jit(solution)/shard_map/ppermute | solution.py:53
  166.8 7.1 %collective-permute-done.17 = f32[110592]{0:T(1024)S(1)} collective-permute-done((f32[110592]{0:T(1024)S(1)}, f32[110592]{0:T(1024)S(1)}, u32[]{:S(2)}, u32[]{:S(2)}) %collective-permute-start.17) | collective-permute-done | bytes 442400 | tf_op jit(solution)/shard_map/ppermute | solution.py:53
  175.0 1.5 collective-permute-done.18
  176.5 1.4 maximum_select_fusion
  (48 shorter events, 4.8 us)
Async XLA Ops:
  0.6 14.2 %collective-permute-start.1 = (bf16[1024,128]{1,0:T(8,128)(2,1)}, bf16[1024,128]{1,0:T(8,128)(2,1)S(1)}, u32[]{:S(2)}, u32[]{:S(2)}) collective-permute-start(bf16[1024,128]{1,0:T(8,128)(2,1)} %param.8), channel_id=1, source_target_pairs={{1,0},{2,1},{3,2},{4,3},{5,4},{6,5},{7,6},{8,7},{9,8},{10,9},{11,1... | collective-permute-start | bytes 786440 | tf_op jit(solution)/shard_map/ppermute | solution.py:17
  3.2 12.0 %collective-permute-start = (bf16[1024,128]{1,0:T(8,128)(2,1)}, bf16[1024,128]{1,0:T(8,128)(2,1)S(1)}, u32[]{:S(2)}, u32[]{:S(2)}) collective-permute-start(bf16[1024,128]{1,0:T(8,128)(2,1)} %param.8), channel_id=1, source_target_pairs={{0,1},{1,2},{2,3},{3,4},{4,5},{5,6},{6,7},{7,8},{8,9},{9,10},{10,1... | collective-permute-start | bytes 786440 | tf_op jit(solution)/shard_map/ppermute | solution.py:17
  45.3 2.6 %collective-permute-start.2 = (f32[221184]{0:T(1024)S(1)}, f32[221184]{0:T(1024)}, u32[]{:S(2)}, u32[]{:S(2)}) collective-permute-start(f32[221184]{0:T(1024)S(1)} %slice_select_fusion), channel_id=1, source_target_pairs={{0,1},{1,0},{2,3},{3,2},{4,5},{5,4},{6,7},{7,6},{8,9},{9,8},{10,11... | collective-permute-start | bytes 2654216 | tf_op jit(solution)/shard_map/ppermute | solution.py:43
  45.4 4.0 %copy-start.1 = (bf16[27,128,128]{2,1,0:T(8,128)(2,1)S(1)}, bf16[27,128,128]{2,1,0:T(8,128)(2,1)}, u32[]{:S(2)}) copy-start(bf16[27,128,128]{2,1,0:T(8,128)(2,1)} %param.9) | copy-start | bytes 2654212
  49.3 11.7 %collective-permute-start.3 = (f32[110592]{0:T(1024)S(1)}, f32[110592]{0:T(1024)S(1)}, u32[]{:S(2)}, u32[]{:S(2)}) collective-permute-start(f32[110592]{0:T(1024)S(1)} %slice_select_fusion.1), channel_id=1, source_target_pairs={{0,2},{1,3},{2,0},{3,1},{4,6},{5,7},{6,4},{7,5},{8,10},{9,11},{10,... | collective-permute-start | bytes 1327112 | tf_op jit(solution)/shard_map/ppermute | solution.py:43
  61.1 7.6 %collective-permute-start.4 = (f32[55296]{0:T(1024)S(1)}, f32[55296]{0:T(1024)S(1)}, u32[]{:S(2)}, u32[]{:S(2)}) collective-permute-start(f32[55296]{0:T(1024)S(1)} %slice_select_fusion.2), channel_id=1, source_target_pairs={{0,4},{1,5},{2,6},{3,7},{4,0},{5,1},{6,2},{7,3},{8,12},{9,13},{10,... | collective-permute-start | bytes 663560 | tf_op jit(solution)/shard_map/ppermute | solution.py:43
  68.7 7.6 %collective-permute-start.5 = (f32[27648]{0:T(1024)S(1)}, f32[27648]{0:T(1024)S(1)}, u32[]{:S(2)}, u32[]{:S(2)}) collective-permute-start(f32[27648]{0:T(1024)S(1)} %slice_select_fusion.3), channel_id=1, source_target_pairs={{0,8},{1,9},{2,10},{3,11},{4,12},{5,13},{6,14},{7,15},{8,0},{9,1},... | collective-permute-start | bytes 331784 | tf_op jit(solution)/shard_map/ppermute | solution.py:43
  76.3 12.4 %collective-permute-start.6 = (f32[13824]{0:T(1024)S(1)}, f32[13824]{0:T(1024)S(1)}, u32[]{:S(2)}, u32[]{:S(2)}) collective-permute-start(f32[13824]{0:T(1024)S(1)} %slice_select_fusion.4), channel_id=1, source_target_pairs={{0,16},{1,17},{2,18},{3,19},{4,20},{5,21},{6,22},{7,23},{8,24},{9,... | collective-permute-start | bytes 165896 | tf_op jit(solution)/shard_map/ppermute | solution.py:43
  88.8 7.5 %collective-permute-start.7 = (f32[6912]{0:T(1024)S(1)}, f32[6912]{0:T(1024)S(1)}, u32[]{:S(2)}, u32[]{:S(2)}) collective-permute-start(f32[6912]{0:T(1024)S(1)} %slice_select_fusion.5), channel_id=1, source_target_pairs={{0,32},{1,33},{2,34},{3,35},{4,36},{5,37},{6,38},{7,39},{8,40},{9,... | collective-permute-start | bytes 82952 | tf_op jit(solution)/shard_map/ppermute | solution.py:43
  96.3 14.9 %collective-permute-start.10 = (f32[6912]{0:T(1024)S(1)}, f32[6912]{0:T(1024)S(1)}, u32[]{:S(2)}, u32[]{:S(2)}) collective-permute-start(f32[6912]{0:T(1024)S(1)} %select_add_fusion.5), channel_id=1, source_target_pairs={{0,192},{1,193},{2,194},{3,195},{4,196},{5,197},{6,198},{7,199},{8... | collective-permute-start | bytes 82952 | tf_op jit(solution)/shard_map/ppermute | solution.py:46
  101.6 9.6 %collective-permute-start.9 = (f32[6912]{0:T(1024)S(1)}, f32[6912]{0:T(1024)S(1)}, u32[]{:S(2)}, u32[]{:S(2)}) collective-permute-start(f32[6912]{0:T(1024)S(1)} %select_add_fusion.5), channel_id=1, source_target_pairs={{0,128},{1,129},{2,130},{3,131},{4,132},{5,133},{6,134},{7,135},{8... | collective-permute-start | bytes 82952 | tf_op jit(solution)/shard_map/ppermute | solution.py:46
  102.3 8.9 %collective-permute-start.8 = (f32[6912]{0:T(1024)S(1)}, f32[6912]{0:T(1024)S(1)}, u32[]{:S(2)}, u32[]{:S(2)}) collective-permute-start(f32[6912]{0:T(1024)S(1)} %select_add_fusion.5), channel_id=1, source_target_pairs={{0,64},{1,65},{2,66},{3,67},{4,68},{5,69},{6,70},{7,71},{8,72},{9,... | collective-permute-start | bytes 82952 | tf_op jit(solution)/shard_map/ppermute | solution.py:46
  111.3 7.9 %collective-permute-start.11 = (f32[6912]{0:T(1024)S(1)}, f32[6912]{0:T(1024)S(1)}, u32[]{:S(2)}, u32[]{:S(2)}) collective-permute-start(f32[6912]{0:T(1024)S(1)} %add_add_fusion), channel_id=1, source_target_pairs={{0,32},{1,33},{2,34},{3,35},{4,36},{5,37},{6,38},{7,39},{8,40},{9,... | collective-permute-start | bytes 82952 | tf_op jit(solution)/shard_map/ppermute | solution.py:53
  119.2 7.5 %collective-permute-start.12 = (f32[13824]{0:T(1024)S(1)}, f32[13824]{0:T(1024)S(1)}, u32[]{:S(2)}, u32[]{:S(2)}) collective-permute-start(f32[13824]{0:T(1024)S(1)} %maximum_select_fusion.5), channel_id=1, source_target_pairs={{0,16},{1,17},{2,18},{3,19},{4,20},{5,21},{6,22},{7,23},{8,24},{9,... | collective-permute-start | bytes 165896 | tf_op jit(solution)/shard_map/ppermute | solution.py:53
  126.8 15.7 %collective-permute-start.13 = (f32[27648]{0:T(1024)S(1)}, f32[27648]{0:T(1024)S(1)}, u32[]{:S(2)}, u32[]{:S(2)}) collective-permute-start(f32[27648]{0:T(1024)S(1)} %maximum_select_fusion.4), channel_id=1, source_target_pairs={{0,8},{1,9},{2,10},{3,11},{4,12},{5,13},{6,14},{7,15},{8,0},{9,1},... | collective-permute-start | bytes 331784 | tf_op jit(solution)/shard_map/ppermute | solution.py:53
  128.4 18.3 %collective-permute-start.15 = (f32[1024,128]{1,0:T(8,128)S(1)}, f32[1024,128]{1,0:T(8,128)S(1)}, u32[]{:S(2)}, u32[]{:S(2)}) collective-permute-start(f32[1024,128]{1,0:T(8,128)S(1)} %bitcast.50), channel_id=1, source_target_pairs={{0,1},{1,2},{2,3},{3,4},{4,5},{5,6},{6,7},{7,8},{8,9},{9,10},{10,1... | collective-permute-start | bytes 1572872 | tf_op jit(solution)/shard_map/ppermute | solution.py:17
  140.6 19.0 %collective-permute-start.14 = (f32[1024,128]{1,0:T(8,128)S(1)}, f32[1024,128]{1,0:T(8,128)S(1)}, u32[]{:S(2)}, u32[]{:S(2)}) collective-permute-start(f32[1024,128]{1,0:T(8,128)S(1)} %bitcast.49), channel_id=1, source_target_pairs={{1,0},{2,1},{3,2},{4,3},{5,4},{6,5},{7,6},{8,7},{9,8},{10,9},{11,1... | collective-permute-start | bytes 1572872 | tf_op jit(solution)/shard_map/ppermute | solution.py:17
  160.4 13.7 %copy-start = (f32[8,128,128]{2,1,0:T(8,128)S(1)}, f32[8,128,128]{2,1,0:T(8,128)}, u32[]{:S(2)}) copy-start(f32[8,128,128]{2,1,0:T(8,128)} %get-tuple-element.90) | copy-start | bytes 1572868
  160.4 6.3 %collective-permute-start.16 = (f32[55296]{0:T(1024)S(1)}, f32[55296]{0:T(1024)S(1)}, u32[]{:S(2)}, u32[]{:S(2)}) collective-permute-start(f32[55296]{0:T(1024)S(1)} %maximum_select_fusion.3), channel_id=1, source_target_pairs={{0,4},{1,5},{2,6},{3,7},{4,0},{5,1},{6,2},{7,3},{8,12},{9,13},{10,... | collective-permute-start | bytes 663560 | tf_op jit(solution)/shard_map/ppermute | solution.py:53
  166.7 7.2 %collective-permute-start.17 = (f32[110592]{0:T(1024)S(1)}, f32[110592]{0:T(1024)S(1)}, u32[]{:S(2)}, u32[]{:S(2)}) collective-permute-start(f32[110592]{0:T(1024)S(1)} %maximum_select_fusion.2), channel_id=1, source_target_pairs={{0,2},{1,3},{2,0},{3,1},{4,6},{5,7},{6,4},{7,5},{8,10},{9,11},{10,... | collective-permute-start | bytes 1327112 | tf_op jit(solution)/shard_map/ppermute | solution.py:53
  174.0 2.5 %collective-permute-start.18 = (f32[221184]{0:T(1024)S(1)}, f32[221184]{0:T(1024)S(1)}, u32[]{:S(2)}, u32[]{:S(2)}) collective-permute-start(f32[221184]{0:T(1024)S(1)} %maximum_select_fusion.1), channel_id=1, source_target_pairs={{0,1},{1,0},{2,3},{3,2},{4,5},{5,4},{6,7},{7,6},{8,9},{9,8},{10,11... | collective-permute-start | bytes 2654216 | tf_op jit(solution)/shard_map/ppermute | solution.py:53

commit v7 on v6

--- a/solution.py
+++ b/solution.py
@@ -121,7 +121,7 @@
     lax.fori_loop(0, rows_ref.shape[0], advance, 0, unroll=UNROLL)
 
 
-UNROLL = 4
+UNROLL = 16
 CHUNKS = 8
 FIRST_STEP = 1
 

time: 178 us -> 162 us (0.910)
  Pallas kernels: 84.8 us -> 65.9 us
  waiting for transfers between devices: 38.1 us -> 40.3 us
    pallas_call x1, Pallas kernels: 26.1 us -> 13.7 us  [grad_sweep(): pl.pallas_call(grad_kernel, out_shape=(jax.ShapeDtypeStruct((kernel_count...]
    pallas_call x8, Pallas kernels: 58.8 us -> 52.2 us  [forward_chunk(): pl.pallas_call(functools.partial(sweep_kernel, chunk * chunk_size), grid=...]
  transfers between devices with their start and end apart: 19 -> 19, of which waited for: 8 -> 9; matrix products, arithmetic and copies ran while one was open for 4% -> 4% of each run, Pallas kernels for 33% -> 32%
where the time goes in v7:
time: 162 us; the launch traced here: 161 us
  Pallas kernels  65.9 us (41%)
  waiting for transfers between devices  40.3 us (25%)
  starting transfers between devices  39 us (24%)
  other arithmetic  9.15 us (6%)
  local copies, waits for them, and re-layouts  5.24 us (3%)
    pallas_call x8, Pallas kernels, forward_chunk(): pl.pallas_call(functools.partial(sweep_kernel, chunk * chunk_size), grid=...  52.2 us
    ppermute x4, starting transfers between devices, passed_along(): lax.ppermute(value, axis, [(source, source + steps) for source in range(l...  25.9 us
    ppermute x4, waiting for transfers between devices, passed_along(): lax.ppermute(value, axis, [(source, source + steps) for source in range(l...  18 us
    ppermute x6, waiting for transfers between devices, summed_everywhere(): other = lax.ppermute(flat, axis, [(i, i ^ mask) for i in range(count)])  14.9 us
    pallas_call x1, Pallas kernels, grad_sweep(): pl.pallas_call(grad_kernel, out_shape=(jax.ShapeDtypeStruct((kernel_count...  13.7 us
    ppermute x3, starting transfers between devices, summed_everywhere(): lax.ppermute(flat, axis, [(i, i ^ mask) for i in range(count)])  7.48 us
    ppermute x6, waiting for transfers between devices, summed_everywhere(): received = lax.ppermute(send, axis, [(i, i ^ mask) for i in range(count)])  7.33 us
    ppermute x6, starting transfers between devices, summed_everywhere(): received = lax.ppermute(send, axis, [(i, i ^ mask) for i in range(count)])  4.63 us
  transfers between devices with their start and end apart: 19, of which 9 were waited for; matrix products, arithmetic and copies ran while one was open for 4% of the time, Pallas kernels for 32%

profile of v7, /device:TPU:127, one launch (start us, length us, event | category | flops | bytes accessed | tf_op | source)
XLA Modules:
  0.0 161.1 jit_solution(9369580768390162557)
XLA Ops:
  0.6 2.6 %collective-permute-start.1 = (bf16[1024,128]{1,0:T(8,128)(2,1)}, bf16[1024,128]{1,0:T(8,128)(2,1)S(1)}, u32[]{:S(2)}, u32[]{:S(2)}) collective-permute-start(bf16[1024,128]{1,0:T(8,128)(2,1)} %param.8), channel_id=1, source_target_pairs={{1,0},{2,1},{3,2},{4,3},{5,4},{6,5},{7,6},{8,7},{9,8},{10,9},{11,1... | collective-permute-start | bytes 786440 | tf_op jit(solution)/shard_map/ppermute | solution.py:17
  3.2 8.4 %collective-permute-start = (bf16[1024,128]{1,0:T(8,128)(2,1)}, bf16[1024,128]{1,0:T(8,128)(2,1)S(1)}, u32[]{:S(2)}, u32[]{:S(2)}) collective-permute-start(bf16[1024,128]{1,0:T(8,128)(2,1)} %param.8), channel_id=1, source_target_pairs={{0,1},{1,2},{2,3},{3,4},{4,5},{5,6},{6,7},{7,8},{8,9},{9,10},{10,1... | collective-permute-start | bytes 786440 | tf_op jit(solution)/shard_map/ppermute | solution.py:17
  11.6 1.2 broadcast_clamp_fusion.1.offsets
  13.5 1.3 fusion.3
  15.3 1.0 pad_maximum_fusion
  16.3 1.2 copy.26
  17.5 13.7 %shard_map.103 = (f32[27,128,128]{2,1,0:T(8,128)}, bf16[256,128,128]{2,1,0:T(8,128)(2,1)}) custom-call(s32[256]{0:T(256)} %broadcast_clamp_fusion.1.offsets, s32[256]{0:T(256)} %get-tuple-element.96.blocks_at, s32[256]{0:T(256)} %get-tuple-element.97.targets, s32[1]{0:T(128)S(6)} %min.29.live, bf16[24,128,128]{2,1,0:T(8,128)(2,1)} %bitcast.46, ...), custom_call_target="tpu_custom_call" | custom-call | tf_op jit(solution)/shard_map/pallas_call | solution.py:146
  31.2 1.6 broadcast_multiply_fusion
  33.0 2.5 %collective-permute-done.2 = f32[221184]{0:T(1024)} collective-permute-done((f32[221184]{0:T(1024)S(1)}, f32[221184]{0:T(1024)}, u32[]{:S(2)}, u32[]{:S(2)}) %collective-permute-start.2) | collective-permute-done | bytes 884768 | tf_op jit(solution)/shard_map/ppermute | solution.py:43
  35.6 1.3 select_add_fusion
  37.0 1.7 %copy.27 = bf16[27,128,128]{1,2,0:T(8,128)(2,1)} copy(bf16[27,128,128]{2,1,0:T(8,128)(2,1)S(1)} %copy-done.1) | data formatting | bytes 1769472 | tf_op args[1]
  38.7 6.0 %shard_map.104 = (f32[8,128,128]{2,1,0:T(8,128)}, f32[24,128,128]{2,1,0:T(8,128)}) custom-call(s32[256]{0:T(256)} %broadcast_clamp_fusion.1.offsets, s32[256]{0:T(256)} %get-tuple-element.96.blocks_at, s32[256]{0:T(256)} %get-tuple-element.97.targets, s32[1]{0:T(128)S(6)} %min.29.live, bf16[27,128,128]{2,1,0:T(8,128)(2,1)} %bitcast.18, ...), custom_call_target="tpu_custom_call" | custom-call | tf_op jit(solution)/shard_map/pallas_call | solution.py:169
  44.7 3.9 %collective-permute-done.3 = f32[110592]{0:T(1024)S(1)} collective-permute-done((f32[110592]{0:T(1024)S(1)}, f32[110592]{0:T(1024)S(1)}, u32[]{:S(2)}, u32[]{:S(2)}) %collective-permute-start.3) | collective-permute-done | bytes 442400 | tf_op jit(solution)/shard_map/ppermute | solution.py:43
  48.8 6.6 %shard_map.105 = (f32[8,128,128]{2,1,0:T(8,128)}, f32[24,128,128]{2,1,0:T(8,128)}) custom-call(s32[256]{0:T(256)} %broadcast_clamp_fusion.1.offsets, s32[256]{0:T(256)} %get-tuple-element.96.blocks_at, s32[256]{0:T(256)} %get-tuple-element.97.targets, s32[1]{0:T(128)S(6)} %min.29.live, ...), custom_call_target="tpu_custom_call", output_to_operand_aliasing={{0}: (8, {}), {1}: (9, {})} | custom-call | tf_op jit(solution)/shard_map/pallas_call | solution.py:169
  56.5 6.6 %shard_map.106 = (f32[8,128,128]{2,1,0:T(8,128)}, f32[24,128,128]{2,1,0:T(8,128)}) custom-call(s32[256]{0:T(256)} %broadcast_clamp_fusion.1.offsets, s32[256]{0:T(256)} %get-tuple-element.96.blocks_at, s32[256]{0:T(256)} %get-tuple-element.97.targets, s32[1]{0:T(128)S(6)} %min.29.live, ...), custom_call_target="tpu_custom_call", output_to_operand_aliasing={{0}: (8, {}), {1}: (9, {})} | custom-call | tf_op jit(solution)/shard_map/pallas_call | solution.py:169
  63.1 4.2 %collective-permute-start.6 = (f32[13824]{0:T(1024)S(1)}, f32[13824]{0:T(1024)S(1)}, u32[]{:S(2)}, u32[]{:S(2)}) collective-permute-start(f32[13824]{0:T(1024)S(1)} %slice_select_fusion.4), channel_id=1, source_target_pairs={{0,16},{1,17},{2,18},{3,19},{4,20},{5,21},{6,22},{7,23},{8,24},{9,... | collective-permute-start | bytes 165896 | tf_op jit(solution)/shard_map/ppermute | solution.py:43
  67.3 6.6 %shard_map.107 = (f32[8,128,128]{2,1,0:T(8,128)}, f32[24,128,128]{2,1,0:T(8,128)}) custom-call(s32[256]{0:T(256)} %broadcast_clamp_fusion.1.offsets, s32[256]{0:T(256)} %get-tuple-element.96.blocks_at, s32[256]{0:T(256)} %get-tuple-element.97.targets, s32[1]{0:T(128)S(6)} %min.29.live, ...), custom_call_target="tpu_custom_call", output_to_operand_aliasing={{0}: (8, {}), {1}: (9, {})} | custom-call | tf_op jit(solution)/shard_map/pallas_call | solution.py:169
  74.0 6.6 %shard_map.108 = (f32[8,128,128]{2,1,0:T(8,128)}, f32[24,128,128]{2,1,0:T(8,128)}) custom-call(s32[256]{0:T(256)} %broadcast_clamp_fusion.1.offsets, s32[256]{0:T(256)} %get-tuple-element.96.blocks_at, s32[256]{0:T(256)} %get-tuple-element.97.targets, s32[1]{0:T(128)S(6)} %min.29.live, ...), custom_call_target="tpu_custom_call", output_to_operand_aliasing={{0}: (8, {}), {1}: (9, {})} | custom-call | tf_op jit(solution)/shard_map/pallas_call | solution.py:169
  80.6 5.3 %collective-permute-start.10 = (f32[6912]{0:T(1024)S(1)}, f32[6912]{0:T(1024)S(1)}, u32[]{:S(2)}, u32[]{:S(2)}) collective-permute-start(f32[6912]{0:T(1024)S(1)} %select_add_fusion.5), channel_id=1, source_target_pairs={{0,192},{1,193},{2,194},{3,195},{4,196},{5,197},{6,198},{7,199},{8... | collective-permute-start | bytes 82952 | tf_op jit(solution)/shard_map/ppermute | solution.py:46
  86.7 1.5 collective-permute-start.8
  88.1 6.6 %shard_map.109 = (f32[8,128,128]{2,1,0:T(8,128)}, f32[24,128,128]{2,1,0:T(8,128)}) custom-call(s32[256]{0:T(256)} %broadcast_clamp_fusion.1.offsets, s32[256]{0:T(256)} %get-tuple-element.96.blocks_at, s32[256]{0:T(256)} %get-tuple-element.97.targets, s32[1]{0:T(128)S(6)} %min.29.live, ...), custom_call_target="tpu_custom_call", output_to_operand_aliasing={{0}: (8, {}), {1}: (9, {})} | custom-call | tf_op jit(solution)/shard_map/pallas_call | solution.py:169
  95.3 6.6 %shard_map.110 = (f32[8,128,128]{2,1,0:T(8,128)}, f32[24,128,128]{2,1,0:T(8,128)}) custom-call(s32[256]{0:T(256)} %broadcast_clamp_fusion.1.offsets, s32[256]{0:T(256)} %get-tuple-element.96.blocks_at, s32[256]{0:T(256)} %get-tuple-element.97.targets, s32[1]{0:T(128)S(6)} %min.29.live, ...), custom_call_target="tpu_custom_call", output_to_operand_aliasing={{0}: (8, {}), {1}: (9, {})} | custom-call | tf_op jit(solution)/shard_map/pallas_call | solution.py:169
  102.0 6.6 %shard_map.111 = (f32[8,128,128]{2,1,0:T(8,128)}, f32[24,128,128]{2,1,0:T(8,128)}) custom-call(s32[256]{0:T(256)} %broadcast_clamp_fusion.1.offsets, s32[256]{0:T(256)} %get-tuple-element.96.blocks_at, s32[256]{0:T(256)} %get-tuple-element.97.targets, s32[1]{0:T(128)S(6)} %min.29.live, ...), custom_call_target="tpu_custom_call", output_to_operand_aliasing={{0}: (8, {}), {1}: (9, {})} | custom-call | tf_op jit(solution)/shard_map/pallas_call | solution.py:169
  108.7 1.5 fusion.4
  110.2 13.0 %collective-permute-start.15 = (f32[1024,128]{1,0:T(8,128)S(1)}, f32[1024,128]{1,0:T(8,128)S(1)}, u32[]{:S(2)}, u32[]{:S(2)}) collective-permute-start(f32[1024,128]{1,0:T(8,128)S(1)} %bitcast.50), channel_id=1, source_target_pairs={{0,1},{1,2},{2,3},{3,4},{4,5},{5,6},{6,7},{7,8},{8,9},{9,10},{10,1... | collective-permute-start | bytes 1572872 | tf_op jit(solution)/shard_map/ppermute | solution.py:17
  123.3 1.9 %collective-permute-start.14 = (f32[1024,128]{1,0:T(8,128)S(1)}, f32[1024,128]{1,0:T(8,128)S(1)}, u32[]{:S(2)}, u32[]{:S(2)}) collective-permute-start(f32[1024,128]{1,0:T(8,128)S(1)} %bitcast.49), channel_id=1, source_target_pairs={{1,0},{2,1},{3,2},{4,3},{5,4},{6,5},{7,6},{8,7},{9,8},{10,9},{11,1... | collective-permute-start | bytes 1572872 | tf_op jit(solution)/shard_map/ppermute | solution.py:17
  125.2 4.1 %collective-permute-done.15 = f32[1024,128]{1,0:T(8,128)S(1)} collective-permute-done((f32[1024,128]{1,0:T(8,128)S(1)}, f32[1024,128]{1,0:T(8,128)S(1)}, u32[]{:S(2)}, u32[]{:S(2)}) %collective-permute-start.15) | collective-permute-done | bytes 524320 | tf_op jit(solution)/shard_map/ppermute | solution.py:17
  129.4 13.5 %collective-permute-done.14 = f32[1024,128]{1,0:T(8,128)S(1)} collective-permute-done((f32[1024,128]{1,0:T(8,128)S(1)}, f32[1024,128]{1,0:T(8,128)S(1)}, u32[]{:S(2)}, u32[]{:S(2)}) %collective-permute-start.14) | collective-permute-done | bytes 524320 | tf_op jit(solution)/shard_map/ppermute | solution.py:17
  143.6 6.3 %collective-permute-done.16 = f32[55296]{0:T(1024)S(1)} collective-permute-done((f32[55296]{0:T(1024)S(1)}, f32[55296]{0:T(1024)S(1)}, u32[]{:S(2)}, u32[]{:S(2)}) %collective-permute-start.16) | collective-permute-done | bytes 221216 | tf_op jit(solution)/shard_map/ppermute | solution.py:53
  150.0 7.1 %collective-permute-done.17 = f32[110592]{0:T(1024)S(1)} collective-permute-done((f32[110592]{0:T(1024)S(1)}, f32[110592]{0:T(1024)S(1)}, u32[]{:S(2)}, u32[]{:S(2)}) %collective-permute-start.17) | collective-permute-done | bytes 442400 | tf_op jit(solution)/shard_map/ppermute | solution.py:53
  158.2 1.5 collective-permute-done.18
  159.7 1.4 maximum_select_fusion
  (48 shorter events, 5.6 us)
Async XLA Ops:
  0.6 14.2 %collective-permute-start.1 = (bf16[1024,128]{1,0:T(8,128)(2,1)}, bf16[1024,128]{1,0:T(8,128)(2,1)S(1)}, u32[]{:S(2)}, u32[]{:S(2)}) collective-permute-start(bf16[1024,128]{1,0:T(8,128)(2,1)} %param.8), channel_id=1, source_target_pairs={{1,0},{2,1},{3,2},{4,3},{5,4},{6,5},{7,6},{8,7},{9,8},{10,9},{11,1... | collective-permute-start | bytes 786440 | tf_op jit(solution)/shard_map/ppermute | solution.py:17
  3.2 12.0 %collective-permute-start = (bf16[1024,128]{1,0:T(8,128)(2,1)}, bf16[1024,128]{1,0:T(8,128)(2,1)S(1)}, u32[]{:S(2)}, u32[]{:S(2)}) collective-permute-start(bf16[1024,128]{1,0:T(8,128)(2,1)} %param.8), channel_id=1, source_target_pairs={{0,1},{1,2},{2,3},{3,4},{4,5},{5,6},{6,7},{7,8},{8,9},{9,10},{10,1... | collective-permute-start | bytes 786440 | tf_op jit(solution)/shard_map/ppermute | solution.py:17
  32.9 2.6 %collective-permute-start.2 = (f32[221184]{0:T(1024)S(1)}, f32[221184]{0:T(1024)}, u32[]{:S(2)}, u32[]{:S(2)}) collective-permute-start(f32[221184]{0:T(1024)S(1)} %slice_select_fusion), channel_id=1, source_target_pairs={{0,1},{1,0},{2,3},{3,2},{4,5},{5,4},{6,7},{7,6},{8,9},{9,8},{10,11... | collective-permute-start | bytes 2654216 | tf_op jit(solution)/shard_map/ppermute | solution.py:43
  33.0 4.0 %copy-start.1 = (bf16[27,128,128]{2,1,0:T(8,128)(2,1)S(1)}, bf16[27,128,128]{2,1,0:T(8,128)(2,1)}, u32[]{:S(2)}) copy-start(bf16[27,128,128]{2,1,0:T(8,128)(2,1)} %param.9) | copy-start | bytes 2654212
  36.9 11.7 %collective-permute-start.3 = (f32[110592]{0:T(1024)S(1)}, f32[110592]{0:T(1024)S(1)}, u32[]{:S(2)}, u32[]{:S(2)}) collective-permute-start(f32[110592]{0:T(1024)S(1)} %slice_select_fusion.1), channel_id=1, source_target_pairs={{0,2},{1,3},{2,0},{3,1},{4,6},{5,7},{6,4},{7,5},{8,10},{9,11},{10,... | collective-permute-start | bytes 1327112 | tf_op jit(solution)/shard_map/ppermute | solution.py:43
  48.7 7.6 %collective-permute-start.4 = (f32[55296]{0:T(1024)S(1)}, f32[55296]{0:T(1024)S(1)}, u32[]{:S(2)}, u32[]{:S(2)}) collective-permute-start(f32[55296]{0:T(1024)S(1)} %slice_select_fusion.2), channel_id=1, source_target_pairs={{0,4},{1,5},{2,6},{3,7},{4,0},{5,1},{6,2},{7,3},{8,12},{9,13},{10,... | collective-permute-start | bytes 663560 | tf_op jit(solution)/shard_map/ppermute | solution.py:43
  56.4 6.7 %collective-permute-start.5 = (f32[27648]{0:T(1024)S(1)}, f32[27648]{0:T(1024)S(1)}, u32[]{:S(2)}, u32[]{:S(2)}) collective-permute-start(f32[27648]{0:T(1024)S(1)} %slice_select_fusion.3), channel_id=1, source_target_pairs={{0,8},{1,9},{2,10},{3,11},{4,12},{5,13},{6,14},{7,15},{8,0},{9,1},... | collective-permute-start | bytes 331784 | tf_op jit(solution)/shard_map/ppermute | solution.py:43
  63.1 10.8 %collective-permute-start.6 = (f32[13824]{0:T(1024)S(1)}, f32[13824]{0:T(1024)S(1)}, u32[]{:S(2)}, u32[]{:S(2)}) collective-permute-start(f32[13824]{0:T(1024)S(1)} %slice_select_fusion.4), channel_id=1, source_target_pairs={{0,16},{1,17},{2,18},{3,19},{4,20},{5,21},{6,22},{7,23},{8,24},{9,... | collective-permute-start | bytes 165896 | tf_op jit(solution)/shard_map/ppermute | solution.py:43
  73.9 6.7 %collective-permute-start.7 = (f32[6912]{0:T(1024)S(1)}, f32[6912]{0:T(1024)S(1)}, u32[]{:S(2)}, u32[]{:S(2)}) collective-permute-start(f32[6912]{0:T(1024)S(1)} %slice_select_fusion.5), channel_id=1, source_target_pairs={{0,32},{1,33},{2,34},{3,35},{4,36},{5,37},{6,38},{7,39},{8,40},{9,... | collective-permute-start | bytes 82952 | tf_op jit(solution)/shard_map/ppermute | solution.py:43
  80.6 14.1 %collective-permute-start.10 = (f32[6912]{0:T(1024)S(1)}, f32[6912]{0:T(1024)S(1)}, u32[]{:S(2)}, u32[]{:S(2)}) collective-permute-start(f32[6912]{0:T(1024)S(1)} %select_add_fusion.5), channel_id=1, source_target_pairs={{0,192},{1,193},{2,194},{3,195},{4,196},{5,197},{6,198},{7,199},{8... | collective-permute-start | bytes 82952 | tf_op jit(solution)/shard_map/ppermute | solution.py:46
  85.9 8.8 %collective-permute-start.9 = (f32[6912]{0:T(1024)S(1)}, f32[6912]{0:T(1024)S(1)}, u32[]{:S(2)}, u32[]{:S(2)}) collective-permute-start(f32[6912]{0:T(1024)S(1)} %select_add_fusion.5), channel_id=1, source_target_pairs={{0,128},{1,129},{2,130},{3,131},{4,132},{5,133},{6,134},{7,135},{8... | collective-permute-start | bytes 82952 | tf_op jit(solution)/shard_map/ppermute | solution.py:46
  86.7 8.1 %collective-permute-start.8 = (f32[6912]{0:T(1024)S(1)}, f32[6912]{0:T(1024)S(1)}, u32[]{:S(2)}, u32[]{:S(2)}) collective-permute-start(f32[6912]{0:T(1024)S(1)} %select_add_fusion.5), channel_id=1, source_target_pairs={{0,64},{1,65},{2,66},{3,67},{4,68},{5,69},{6,70},{7,71},{8,72},{9,... | collective-permute-start | bytes 82952 | tf_op jit(solution)/shard_map/ppermute | solution.py:46
  94.8 7.1 %collective-permute-start.11 = (f32[6912]{0:T(1024)S(1)}, f32[6912]{0:T(1024)S(1)}, u32[]{:S(2)}, u32[]{:S(2)}) collective-permute-start(f32[6912]{0:T(1024)S(1)} %add_add_fusion), channel_id=1, source_target_pairs={{0,32},{1,33},{2,34},{3,35},{4,36},{5,37},{6,38},{7,39},{8,40},{9,... | collective-permute-start | bytes 82952 | tf_op jit(solution)/shard_map/ppermute | solution.py:53
  101.9 6.7 %collective-permute-start.12 = (f32[13824]{0:T(1024)S(1)}, f32[13824]{0:T(1024)S(1)}, u32[]{:S(2)}, u32[]{:S(2)}) collective-permute-start(f32[13824]{0:T(1024)S(1)} %maximum_select_fusion.5), channel_id=1, source_target_pairs={{0,16},{1,17},{2,18},{3,19},{4,20},{5,21},{6,22},{7,23},{8,24},{9,... | collective-permute-start | bytes 165896 | tf_op jit(solution)/shard_map/ppermute | solution.py:53
  108.6 16.5 %collective-permute-start.13 = (f32[27648]{0:T(1024)S(1)}, f32[27648]{0:T(1024)S(1)}, u32[]{:S(2)}, u32[]{:S(2)}) collective-permute-start(f32[27648]{0:T(1024)S(1)} %maximum_select_fusion.4), channel_id=1, source_target_pairs={{0,8},{1,9},{2,10},{3,11},{4,12},{5,13},{6,14},{7,15},{8,0},{9,1},... | collective-permute-start | bytes 331784 | tf_op jit(solution)/shard_map/ppermute | solution.py:53
  110.2 19.1 %collective-permute-start.15 = (f32[1024,128]{1,0:T(8,128)S(1)}, f32[1024,128]{1,0:T(8,128)S(1)}, u32[]{:S(2)}, u32[]{:S(2)}) collective-permute-start(f32[1024,128]{1,0:T(8,128)S(1)} %bitcast.50), channel_id=1, source_target_pairs={{0,1},{1,2},{2,3},{3,4},{4,5},{5,6},{6,7},{7,8},{8,9},{9,10},{10,1... | collective-permute-start | bytes 1572872 | tf_op jit(solution)/shard_map/ppermute | solution.py:17
  123.3 19.6 %collective-permute-start.14 = (f32[1024,128]{1,0:T(8,128)S(1)}, f32[1024,128]{1,0:T(8,128)S(1)}, u32[]{:S(2)}, u32[]{:S(2)}) collective-permute-start(f32[1024,128]{1,0:T(8,128)S(1)} %bitcast.49), channel_id=1, source_target_pairs={{1,0},{2,1},{3,2},{4,3},{5,4},{6,5},{7,6},{8,7},{9,8},{10,9},{11,1... | collective-permute-start | bytes 1572872 | tf_op jit(solution)/shard_map/ppermute | solution.py:17
  143.6 13.7 %copy-start = (f32[8,128,128]{2,1,0:T(8,128)S(1)}, f32[8,128,128]{2,1,0:T(8,128)}, u32[]{:S(2)}) copy-start(f32[8,128,128]{2,1,0:T(8,128)} %get-tuple-element.90) | copy-start | bytes 1572868
  143.6 6.3 %collective-permute-start.16 = (f32[55296]{0:T(1024)S(1)}, f32[55296]{0:T(1024)S(1)}, u32[]{:S(2)}, u32[]{:S(2)}) collective-permute-start(f32[55296]{0:T(1024)S(1)} %maximum_select_fusion.3), channel_id=1, source_target_pairs={{0,4},{1,5},{2,6},{3,7},{4,0},{5,1},{6,2},{7,3},{8,12},{9,13},{10,... | collective-permute-start | bytes 663560 | tf_op jit(solution)/shard_map/ppermute | solution.py:53
  149.9 7.2 %collective-permute-start.17 = (f32[110592]{0:T(1024)S(1)}, f32[110592]{0:T(1024)S(1)}, u32[]{:S(2)}, u32[]{:S(2)}) collective-permute-start(f32[110592]{0:T(1024)S(1)} %maximum_select_fusion.2), channel_id=1, source_target_pairs={{0,2},{1,3},{2,0},{3,1},{4,6},{5,7},{6,4},{7,5},{8,10},{9,11},{10,... | collective-permute-start | bytes 1327112 | tf_op jit(solution)/shard_map/ppermute | solution.py:53
  157.2 2.5 %collective-permute-start.18 = (f32[221184]{0:T(1024)S(1)}, f32[221184]{0:T(1024)S(1)}, u32[]{:S(2)}, u32[]{:S(2)}) collective-permute-start(f32[221184]{0:T(1024)S(1)} %maximum_select_fusion.1), channel_id=1, source_target_pairs={{0,1},{1,0},{2,3},{3,2},{4,5},{5,4},{6,7},{7,6},{8,9},{9,8},{10,11... | collective-permute-start | bytes 2654216 | tf_op jit(solution)/shard_map/ppermute | solution.py:53

commit v8 on v7

--- a/solution.py
+++ b/solution.py
@@ -121,7 +121,7 @@
     lax.fori_loop(0, rows_ref.shape[0], advance, 0, unroll=UNROLL)
 
 
-UNROLL = 16
+UNROLL = 32
 CHUNKS = 8
 FIRST_STEP = 1
 

time: 162 us -> 159 us (0.981)
  Pallas kernels: 65.9 us -> 61.9 us
    pallas_call x1, Pallas kernels: 13.7 us -> 11.6 us  [grad_sweep(): pl.pallas_call(grad_kernel, out_shape=(jax.ShapeDtypeStruct((kernel_count...]
    pallas_call x8, Pallas kernels: 52.2 us -> 50.3 us  [forward_chunk(): pl.pallas_call(functools.partial(sweep_kernel, chunk * chunk_size), grid=...]
where the time goes in v8:
time: 159 us; the launch traced here: 158 us
  Pallas kernels  61.9 us (39%)
  waiting for transfers between devices  40.9 us (26%)
  starting transfers between devices  39.3 us (25%)
  other arithmetic  9.15 us (6%)
  local copies, waits for them, and re-layouts  5.24 us (3%)
    pallas_call x8, Pallas kernels, forward_chunk(): pl.pallas_call(functools.partial(sweep_kernel, chunk * chunk_size), grid=...  50.3 us
    ppermute x4, starting transfers between devices, passed_along(): lax.ppermute(value, axis, [(source, source + steps) for source in range(l...  26.2 us
    ppermute x4, waiting for transfers between devices, passed_along(): lax.ppermute(value, axis, [(source, source + steps) for source in range(l...  18.2 us
    ppermute x6, waiting for transfers between devices, summed_everywhere(): other = lax.ppermute(flat, axis, [(i, i ^ mask) for i in range(count)])  14.9 us
    pallas_call x1, Pallas kernels, grad_sweep(): pl.pallas_call(grad_kernel, out_shape=(jax.ShapeDtypeStruct((kernel_count...  11.6 us
    ppermute x6, waiting for transfers between devices, summed_everywhere(): received = lax.ppermute(send, axis, [(i, i ^ mask) for i in range(count)])  7.78 us
    ppermute x3, starting transfers between devices, summed_everywhere(): lax.ppermute(flat, axis, [(i, i ^ mask) for i in range(count)])  7.47 us
    ppermute x6, starting transfers between devices, summed_everywhere(): received = lax.ppermute(send, axis, [(i, i ^ mask) for i in range(count)])  4.56 us
  transfers between devices with their start and end apart: 19, of which 9 were waited for; matrix products, arithmetic and copies ran while one was open for 4% of the time, Pallas kernels for 32%

profile of v8, /device:TPU:127, one launch (start us, length us, event | category | flops | bytes accessed | tf_op | source)
XLA Modules:
  0.0 158.1 jit_solution(52848912030537166)
XLA Ops:
  0.6 2.6 %collective-permute-start.1 = (bf16[1024,128]{1,0:T(8,128)(2,1)}, bf16[1024,128]{1,0:T(8,128)(2,1)S(1)}, u32[]{:S(2)}, u32[]{:S(2)}) collective-permute-start(bf16[1024,128]{1,0:T(8,128)(2,1)} %param.8), channel_id=1, source_target_pairs={{1,0},{2,1},{3,2},{4,3},{5,4},{6,5},{7,6},{8,7},{9,8},{10,9},{11,1... | collective-permute-start | bytes 786440 | tf_op jit(solution)/shard_map/ppermute | solution.py:17
  3.2 8.4 %collective-permute-start = (bf16[1024,128]{1,0:T(8,128)(2,1)}, bf16[1024,128]{1,0:T(8,128)(2,1)S(1)}, u32[]{:S(2)}, u32[]{:S(2)}) collective-permute-start(bf16[1024,128]{1,0:T(8,128)(2,1)} %param.8), channel_id=1, source_target_pairs={{0,1},{1,2},{2,3},{3,4},{4,5},{5,6},{6,7},{7,8},{8,9},{9,10},{10,1... | collective-permute-start | bytes 786440 | tf_op jit(solution)/shard_map/ppermute | solution.py:17
  11.6 1.2 broadcast_clamp_fusion.1.offsets
  13.5 1.3 fusion.3
  16.3 1.2 copy.26
  17.5 11.6 %shard_map.103 = (f32[27,128,128]{2,1,0:T(8,128)}, bf16[256,128,128]{2,1,0:T(8,128)(2,1)}) custom-call(s32[256]{0:T(256)} %broadcast_clamp_fusion.1.offsets, s32[256]{0:T(256)} %get-tuple-element.96.blocks_at, s32[256]{0:T(256)} %get-tuple-element.97.targets, s32[1]{0:T(128)S(6)} %min.29.live, bf16[24,128,128]{2,1,0:T(8,128)(2,1)} %bitcast.46, ...), custom_call_target="tpu_custom_call" | custom-call | tf_op jit(solution)/shard_map/pallas_call | solution.py:146
  29.1 1.6 %broadcast_multiply_fusion = f32[27,128,128]{2,1,0:T(8,128)S(1)} fusion(f32[27,128,128]{2,1,0:T(8,128)} %get-tuple-element.48), kind=kLoop, calls=%fused_computation.3 | loop fusion | flops 442368 | bytes 3538944 | tf_op jit(solution)/shard_map/mul | solution.py:204
  31.0 2.5 %collective-permute-done.2 = f32[221184]{0:T(1024)} collective-permute-done((f32[221184]{0:T(1024)S(1)}, f32[221184]{0:T(1024)}, u32[]{:S(2)}, u32[]{:S(2)}) %collective-permute-start.2) | collective-permute-done | bytes 884768 | tf_op jit(solution)/shard_map/ppermute | solution.py:43
  33.5 1.3 select_add_fusion
  35.0 1.7 %copy.27 = bf16[27,128,128]{1,2,0:T(8,128)(2,1)} copy(bf16[27,128,128]{2,1,0:T(8,128)(2,1)S(1)} %copy-done.1) | data formatting | bytes 1769472 | tf_op args[1]
  36.6 5.8 %shard_map.104 = (f32[8,128,128]{2,1,0:T(8,128)}, f32[24,128,128]{2,1,0:T(8,128)}) custom-call(s32[256]{0:T(256)} %broadcast_clamp_fusion.1.offsets, s32[256]{0:T(256)} %get-tuple-element.96.blocks_at, s32[256]{0:T(256)} %get-tuple-element.97.targets, s32[1]{0:T(128)S(6)} %min.29.live, bf16[27,128,128]{2,1,0:T(8,128)(2,1)} %bitcast.18, ...), custom_call_target="tpu_custom_call" | custom-call | tf_op jit(solution)/shard_map/pallas_call | solution.py:169
  42.4 4.1 %collective-permute-done.3 = f32[110592]{0:T(1024)S(1)} collective-permute-done((f32[110592]{0:T(1024)S(1)}, f32[110592]{0:T(1024)S(1)}, u32[]{:S(2)}, u32[]{:S(2)}) %collective-permute-start.3) | collective-permute-done | bytes 442400 | tf_op jit(solution)/shard_map/ppermute | solution.py:43
  46.7 6.3 %shard_map.105 = (f32[8,128,128]{2,1,0:T(8,128)}, f32[24,128,128]{2,1,0:T(8,128)}) custom-call(s32[256]{0:T(256)} %broadcast_clamp_fusion.1.offsets, s32[256]{0:T(256)} %get-tuple-element.96.blocks_at, s32[256]{0:T(256)} %get-tuple-element.97.targets, s32[1]{0:T(128)S(6)} %min.29.live, ...), custom_call_target="tpu_custom_call", output_to_operand_aliasing={{0}: (8, {}), {1}: (9, {})} | custom-call | tf_op jit(solution)/shard_map/pallas_call | solution.py:169
  53.1 1.1 collective-permute-done.4
  54.4 6.4 %shard_map.106 = (f32[8,128,128]{2,1,0:T(8,128)}, f32[24,128,128]{2,1,0:T(8,128)}) custom-call(s32[256]{0:T(256)} %broadcast_clamp_fusion.1.offsets, s32[256]{0:T(256)} %get-tuple-element.96.blocks_at, s32[256]{0:T(256)} %get-tuple-element.97.targets, s32[1]{0:T(128)S(6)} %min.29.live, ...), custom_call_target="tpu_custom_call", output_to_operand_aliasing={{0}: (8, {}), {1}: (9, {})} | custom-call | tf_op jit(solution)/shard_map/pallas_call | solution.py:169
  60.8 4.1 %collective-permute-start.6 = (f32[13824]{0:T(1024)S(1)}, f32[13824]{0:T(1024)S(1)}, u32[]{:S(2)}, u32[]{:S(2)}) collective-permute-start(f32[13824]{0:T(1024)S(1)} %slice_select_fusion.4), channel_id=1, source_target_pairs={{0,16},{1,17},{2,18},{3,19},{4,20},{5,21},{6,22},{7,23},{8,24},{9,... | collective-permute-start | bytes 165896 | tf_op jit(solution)/shard_map/ppermute | solution.py:43
  64.9 6.3 %shard_map.107 = (f32[8,128,128]{2,1,0:T(8,128)}, f32[24,128,128]{2,1,0:T(8,128)}) custom-call(s32[256]{0:T(256)} %broadcast_clamp_fusion.1.offsets, s32[256]{0:T(256)} %get-tuple-element.96.blocks_at, s32[256]{0:T(256)} %get-tuple-element.97.targets, s32[1]{0:T(128)S(6)} %min.29.live, ...), custom_call_target="tpu_custom_call", output_to_operand_aliasing={{0}: (8, {}), {1}: (9, {})} | custom-call | tf_op jit(solution)/shard_map/pallas_call | solution.py:169
  71.4 6.4 %shard_map.108 = (f32[8,128,128]{2,1,0:T(8,128)}, f32[24,128,128]{2,1,0:T(8,128)}) custom-call(s32[256]{0:T(256)} %broadcast_clamp_fusion.1.offsets, s32[256]{0:T(256)} %get-tuple-element.96.blocks_at, s32[256]{0:T(256)} %get-tuple-element.97.targets, s32[1]{0:T(128)S(6)} %min.29.live, ...), custom_call_target="tpu_custom_call", output_to_operand_aliasing={{0}: (8, {}), {1}: (9, {})} | custom-call | tf_op jit(solution)/shard_map/pallas_call | solution.py:169
  77.8 5.3 %collective-permute-start.10 = (f32[6912]{0:T(1024)S(1)}, f32[6912]{0:T(1024)S(1)}, u32[]{:S(2)}, u32[]{:S(2)}) collective-permute-start(f32[6912]{0:T(1024)S(1)} %select_add_fusion.5), channel_id=1, source_target_pairs={{0,192},{1,193},{2,194},{3,195},{4,196},{5,197},{6,198},{7,199},{8... | collective-permute-start | bytes 82952 | tf_op jit(solution)/shard_map/ppermute | solution.py:46
  83.7 1.5 collective-permute-start.8
  85.3 6.4 %shard_map.109 = (f32[8,128,128]{2,1,0:T(8,128)}, f32[24,128,128]{2,1,0:T(8,128)}) custom-call(s32[256]{0:T(256)} %broadcast_clamp_fusion.1.offsets, s32[256]{0:T(256)} %get-tuple-element.96.blocks_at, s32[256]{0:T(256)} %get-tuple-element.97.targets, s32[1]{0:T(128)S(6)} %min.29.live, ...), custom_call_target="tpu_custom_call", output_to_operand_aliasing={{0}: (8, {}), {1}: (9, {})} | custom-call | tf_op jit(solution)/shard_map/pallas_call | solution.py:169
  92.1 6.4 %shard_map.110 = (f32[8,128,128]{2,1,0:T(8,128)}, f32[24,128,128]{2,1,0:T(8,128)}) custom-call(s32[256]{0:T(256)} %broadcast_clamp_fusion.1.offsets, s32[256]{0:T(256)} %get-tuple-element.96.blocks_at, s32[256]{0:T(256)} %get-tuple-element.97.targets, s32[1]{0:T(128)S(6)} %min.29.live, ...), custom_call_target="tpu_custom_call", output_to_operand_aliasing={{0}: (8, {}), {1}: (9, {})} | custom-call | tf_op jit(solution)/shard_map/pallas_call | solution.py:169
  98.6 6.3 %shard_map.111 = (f32[8,128,128]{2,1,0:T(8,128)}, f32[24,128,128]{2,1,0:T(8,128)}) custom-call(s32[256]{0:T(256)} %broadcast_clamp_fusion.1.offsets, s32[256]{0:T(256)} %get-tuple-element.96.blocks_at, s32[256]{0:T(256)} %get-tuple-element.97.targets, s32[1]{0:T(128)S(6)} %min.29.live, ...), custom_call_target="tpu_custom_call", output_to_operand_aliasing={{0}: (8, {}), {1}: (9, {})} | custom-call | tf_op jit(solution)/shard_map/pallas_call | solution.py:169
  105.3 1.5 fusion.4
  106.8 13.3 %collective-permute-start.15 = (f32[1024,128]{1,0:T(8,128)S(1)}, f32[1024,128]{1,0:T(8,128)S(1)}, u32[]{:S(2)}, u32[]{:S(2)}) collective-permute-start(f32[1024,128]{1,0:T(8,128)S(1)} %bitcast.50), channel_id=1, source_target_pairs={{0,1},{1,2},{2,3},{3,4},{4,5},{5,6},{6,7},{7,8},{8,9},{9,10},{10,1... | collective-permute-start | bytes 1572872 | tf_op jit(solution)/shard_map/ppermute | solution.py:17
  120.1 1.9 %collective-permute-start.14 = (f32[1024,128]{1,0:T(8,128)S(1)}, f32[1024,128]{1,0:T(8,128)S(1)}, u32[]{:S(2)}, u32[]{:S(2)}) collective-permute-start(f32[1024,128]{1,0:T(8,128)S(1)} %bitcast.49), channel_id=1, source_target_pairs={{1,0},{2,1},{3,2},{4,3},{5,4},{6,5},{7,6},{8,7},{9,8},{10,9},{11,1... | collective-permute-start | bytes 1572872 | tf_op jit(solution)/shard_map/ppermute | solution.py:17
  122.1 4.1 %collective-permute-done.15 = f32[1024,128]{1,0:T(8,128)S(1)} collective-permute-done((f32[1024,128]{1,0:T(8,128)S(1)}, f32[1024,128]{1,0:T(8,128)S(1)}, u32[]{:S(2)}, u32[]{:S(2)}) %collective-permute-start.15) | collective-permute-done | bytes 524320 | tf_op jit(solution)/shard_map/ppermute | solution.py:17
  126.2 13.6 %collective-permute-done.14 = f32[1024,128]{1,0:T(8,128)S(1)} collective-permute-done((f32[1024,128]{1,0:T(8,128)S(1)}, f32[1024,128]{1,0:T(8,128)S(1)}, u32[]{:S(2)}, u32[]{:S(2)}) %collective-permute-start.14) | collective-permute-done | bytes 524320 | tf_op jit(solution)/shard_map/ppermute | solution.py:17
  140.6 6.3 %collective-permute-done.16 = f32[55296]{0:T(1024)S(1)} collective-permute-done((f32[55296]{0:T(1024)S(1)}, f32[55296]{0:T(1024)S(1)}, u32[]{:S(2)}, u32[]{:S(2)}) %collective-permute-start.16) | collective-permute-done | bytes 221216 | tf_op jit(solution)/shard_map/ppermute | solution.py:53
  147.0 7.1 %collective-permute-done.17 = f32[110592]{0:T(1024)S(1)} collective-permute-done((f32[110592]{0:T(1024)S(1)}, f32[110592]{0:T(1024)S(1)}, u32[]{:S(2)}, u32[]{:S(2)}) %collective-permute-start.17) | collective-permute-done | bytes 442400 | tf_op jit(solution)/shard_map/ppermute | solution.py:53
  155.2 1.5 collective-permute-done.18
  156.8 1.4 maximum_select_fusion
  (48 shorter events, 5.9 us)
Async XLA Ops:
  0.6 14.2 %collective-permute-start.1 = (bf16[1024,128]{1,0:T(8,128)(2,1)}, bf16[1024,128]{1,0:T(8,128)(2,1)S(1)}, u32[]{:S(2)}, u32[]{:S(2)}) collective-permute-start(bf16[1024,128]{1,0:T(8,128)(2,1)} %param.8), channel_id=1, source_target_pairs={{1,0},{2,1},{3,2},{4,3},{5,4},{6,5},{7,6},{8,7},{9,8},{10,9},{11,1... | collective-permute-start | bytes 786440 | tf_op jit(solution)/shard_map/ppermute | solution.py:17
  3.2 12.0 %collective-permute-start = (bf16[1024,128]{1,0:T(8,128)(2,1)}, bf16[1024,128]{1,0:T(8,128)(2,1)S(1)}, u32[]{:S(2)}, u32[]{:S(2)}) collective-permute-start(bf16[1024,128]{1,0:T(8,128)(2,1)} %param.8), channel_id=1, source_target_pairs={{0,1},{1,2},{2,3},{3,4},{4,5},{5,6},{6,7},{7,8},{8,9},{9,10},{10,1... | collective-permute-start | bytes 786440 | tf_op jit(solution)/shard_map/ppermute | solution.py:17
  30.9 2.6 %collective-permute-start.2 = (f32[221184]{0:T(1024)S(1)}, f32[221184]{0:T(1024)}, u32[]{:S(2)}, u32[]{:S(2)}) collective-permute-start(f32[221184]{0:T(1024)S(1)} %slice_select_fusion), channel_id=1, source_target_pairs={{0,1},{1,0},{2,3},{3,2},{4,5},{5,4},{6,7},{7,6},{8,9},{9,8},{10,11... | collective-permute-start | bytes 2654216 | tf_op jit(solution)/shard_map/ppermute | solution.py:43
  31.0 4.0 %copy-start.1 = (bf16[27,128,128]{2,1,0:T(8,128)(2,1)S(1)}, bf16[27,128,128]{2,1,0:T(8,128)(2,1)}, u32[]{:S(2)}) copy-start(bf16[27,128,128]{2,1,0:T(8,128)(2,1)} %param.9) | copy-start | bytes 2654212
  34.9 11.7 %collective-permute-start.3 = (f32[110592]{0:T(1024)S(1)}, f32[110592]{0:T(1024)S(1)}, u32[]{:S(2)}, u32[]{:S(2)}) collective-permute-start(f32[110592]{0:T(1024)S(1)} %slice_select_fusion.1), channel_id=1, source_target_pairs={{0,2},{1,3},{2,0},{3,1},{4,6},{5,7},{6,4},{7,5},{8,10},{9,11},{10,... | collective-permute-start | bytes 1327112 | tf_op jit(solution)/shard_map/ppermute | solution.py:43
  46.6 7.6 %collective-permute-start.4 = (f32[55296]{0:T(1024)S(1)}, f32[55296]{0:T(1024)S(1)}, u32[]{:S(2)}, u32[]{:S(2)}) collective-permute-start(f32[55296]{0:T(1024)S(1)} %slice_select_fusion.2), channel_id=1, source_target_pairs={{0,4},{1,5},{2,6},{3,7},{4,0},{5,1},{6,2},{7,3},{8,12},{9,13},{10,... | collective-permute-start | bytes 663560 | tf_op jit(solution)/shard_map/ppermute | solution.py:43
  54.3 6.5 %collective-permute-start.5 = (f32[27648]{0:T(1024)S(1)}, f32[27648]{0:T(1024)S(1)}, u32[]{:S(2)}, u32[]{:S(2)}) collective-permute-start(f32[27648]{0:T(1024)S(1)} %slice_select_fusion.3), channel_id=1, source_target_pairs={{0,8},{1,9},{2,10},{3,11},{4,12},{5,13},{6,14},{7,15},{8,0},{9,1},... | collective-permute-start | bytes 331784 | tf_op jit(solution)/shard_map/ppermute | solution.py:43
  60.8 10.4 %collective-permute-start.6 = (f32[13824]{0:T(1024)S(1)}, f32[13824]{0:T(1024)S(1)}, u32[]{:S(2)}, u32[]{:S(2)}) collective-permute-start(f32[13824]{0:T(1024)S(1)} %slice_select_fusion.4), channel_id=1, source_target_pairs={{0,16},{1,17},{2,18},{3,19},{4,20},{5,21},{6,22},{7,23},{8,24},{9,... | collective-permute-start | bytes 165896 | tf_op jit(solution)/shard_map/ppermute | solution.py:43
  71.3 6.5 %collective-permute-start.7 = (f32[6912]{0:T(1024)S(1)}, f32[6912]{0:T(1024)S(1)}, u32[]{:S(2)}, u32[]{:S(2)}) collective-permute-start(f32[6912]{0:T(1024)S(1)} %slice_select_fusion.5), channel_id=1, source_target_pairs={{0,32},{1,33},{2,34},{3,35},{4,36},{5,37},{6,38},{7,39},{8,40},{9,... | collective-permute-start | bytes 82952 | tf_op jit(solution)/shard_map/ppermute | solution.py:43
  77.8 13.8 %collective-permute-start.10 = (f32[6912]{0:T(1024)S(1)}, f32[6912]{0:T(1024)S(1)}, u32[]{:S(2)}, u32[]{:S(2)}) collective-permute-start(f32[6912]{0:T(1024)S(1)} %select_add_fusion.5), channel_id=1, source_target_pairs={{0,192},{1,193},{2,194},{3,195},{4,196},{5,197},{6,198},{7,199},{8... | collective-permute-start | bytes 82952 | tf_op jit(solution)/shard_map/ppermute | solution.py:46
  83.1 8.5 %collective-permute-start.9 = (f32[6912]{0:T(1024)S(1)}, f32[6912]{0:T(1024)S(1)}, u32[]{:S(2)}, u32[]{:S(2)}) collective-permute-start(f32[6912]{0:T(1024)S(1)} %select_add_fusion.5), channel_id=1, source_target_pairs={{0,128},{1,129},{2,130},{3,131},{4,132},{5,133},{6,134},{7,135},{8... | collective-permute-start | bytes 82952 | tf_op jit(solution)/shard_map/ppermute | solution.py:46
  83.7 7.9 %collective-permute-start.8 = (f32[6912]{0:T(1024)S(1)}, f32[6912]{0:T(1024)S(1)}, u32[]{:S(2)}, u32[]{:S(2)}) collective-permute-start(f32[6912]{0:T(1024)S(1)} %select_add_fusion.5), channel_id=1, source_target_pairs={{0,64},{1,65},{2,66},{3,67},{4,68},{5,69},{6,70},{7,71},{8,72},{9,... | collective-permute-start | bytes 82952 | tf_op jit(solution)/shard_map/ppermute | solution.py:46
  91.6 6.9 %collective-permute-start.11 = (f32[6912]{0:T(1024)S(1)}, f32[6912]{0:T(1024)S(1)}, u32[]{:S(2)}, u32[]{:S(2)}) collective-permute-start(f32[6912]{0:T(1024)S(1)} %add_add_fusion), channel_id=1, source_target_pairs={{0,32},{1,33},{2,34},{3,35},{4,36},{5,37},{6,38},{7,39},{8,40},{9,... | collective-permute-start | bytes 82952 | tf_op jit(solution)/shard_map/ppermute | solution.py:53
  98.5 6.5 %collective-permute-start.12 = (f32[13824]{0:T(1024)S(1)}, f32[13824]{0:T(1024)S(1)}, u32[]{:S(2)}, u32[]{:S(2)}) collective-permute-start(f32[13824]{0:T(1024)S(1)} %maximum_select_fusion.5), channel_id=1, source_target_pairs={{0,16},{1,17},{2,18},{3,19},{4,20},{5,21},{6,22},{7,23},{8,24},{9,... | collective-permute-start | bytes 165896 | tf_op jit(solution)/shard_map/ppermute | solution.py:53
  105.0 17.0 %collective-permute-start.13 = (f32[27648]{0:T(1024)S(1)}, f32[27648]{0:T(1024)S(1)}, u32[]{:S(2)}, u32[]{:S(2)}) collective-permute-start(f32[27648]{0:T(1024)S(1)} %maximum_select_fusion.4), channel_id=1, source_target_pairs={{0,8},{1,9},{2,10},{3,11},{4,12},{5,13},{6,14},{7,15},{8,0},{9,1},... | collective-permute-start | bytes 331784 | tf_op jit(solution)/shard_map/ppermute | solution.py:53
  106.8 19.4 %collective-permute-start.15 = (f32[1024,128]{1,0:T(8,128)S(1)}, f32[1024,128]{1,0:T(8,128)S(1)}, u32[]{:S(2)}, u32[]{:S(2)}) collective-permute-start(f32[1024,128]{1,0:T(8,128)S(1)} %bitcast.50), channel_id=1, source_target_pairs={{0,1},{1,2},{2,3},{3,4},{4,5},{5,6},{6,7},{7,8},{8,9},{9,10},{10,1... | collective-permute-start | bytes 1572872 | tf_op jit(solution)/shard_map/ppermute | solution.py:17
  120.1 19.7 %collective-permute-start.14 = (f32[1024,128]{1,0:T(8,128)S(1)}, f32[1024,128]{1,0:T(8,128)S(1)}, u32[]{:S(2)}, u32[]{:S(2)}) collective-permute-start(f32[1024,128]{1,0:T(8,128)S(1)} %bitcast.49), channel_id=1, source_target_pairs={{1,0},{2,1},{3,2},{4,3},{5,4},{6,5},{7,6},{8,7},{9,8},{10,9},{11,1... | collective-permute-start | bytes 1572872 | tf_op jit(solution)/shard_map/ppermute | solution.py:17
  140.6 13.7 %copy-start = (f32[8,128,128]{2,1,0:T(8,128)S(1)}, f32[8,128,128]{2,1,0:T(8,128)}, u32[]{:S(2)}) copy-start(f32[8,128,128]{2,1,0:T(8,128)} %get-tuple-element.90) | copy-start | bytes 1572868
  140.6 6.3 %collective-permute-start.16 = (f32[55296]{0:T(1024)S(1)}, f32[55296]{0:T(1024)S(1)}, u32[]{:S(2)}, u32[]{:S(2)}) collective-permute-start(f32[55296]{0:T(1024)S(1)} %maximum_select_fusion.3), channel_id=1, source_target_pairs={{0,4},{1,5},{2,6},{3,7},{4,0},{5,1},{6,2},{7,3},{8,12},{9,13},{10,... | collective-permute-start | bytes 663560 | tf_op jit(solution)/shard_map/ppermute | solution.py:53
  146.9 7.2 %collective-permute-start.17 = (f32[110592]{0:T(1024)S(1)}, f32[110592]{0:T(1024)S(1)}, u32[]{:S(2)}, u32[]{:S(2)}) collective-permute-start(f32[110592]{0:T(1024)S(1)} %maximum_select_fusion.2), channel_id=1, source_target_pairs={{0,2},{1,3},{2,0},{3,1},{4,6},{5,7},{6,4},{7,5},{8,10},{9,11},{10,... | collective-permute-start | bytes 1327112 | tf_op jit(solution)/shard_map/ppermute | solution.py:53
  154.2 2.5 %collective-permute-start.18 = (f32[221184]{0:T(1024)S(1)}, f32[221184]{0:T(1024)S(1)}, u32[]{:S(2)}, u32[]{:S(2)}) collective-permute-start(f32[221184]{0:T(1024)S(1)} %maximum_select_fusion.1), channel_id=1, source_target_pairs={{0,1},{1,0},{2,3},{3,2},{4,5},{5,4},{6,7},{7,6},{8,9},{9,8},{10,11... | collective-permute-start | bytes 2654216 | tf_op jit(solution)/shard_map/ppermute | solution.py:53

commit v9 on v8

--- a/solution.py
+++ b/solution.py
@@ -202,11 +202,13 @@
     scalars = rulebook_scalars(rulebook, myself, blocks, kernel_count)
     grad_sum, gathered = grad_sweep(window, grad_blocks, scalars, kernel_count)
     grad_sum = grad_sum * (1.0 / math.sqrt(axis_count * local_rows))
-    weights_t = weights.transpose(0, 2, 1)
     pair_slots = pair_offset.shape[0]
     chunk_count = CHUNKS if pair_slots % CHUNKS == 0 else 1
     chunk_size = pair_slots // chunk_count
-    first_step = FIRST_STEP if axis_count & (axis_count - 1) == 0 else 0
+    power_of_two = axis_count & (axis_count - 1) == 0 and grad_sum.size % axis_count == 0
+    first_step = FIRST_STEP if power_of_two else 0
+    split = max(axis_count.bit_length() - 3, 0)
+    exchange_step = max(first_step + chunk_count, 2 * split - 1)
 
     def exchanged(sums):
         out_t, returned_sum = sums
@@ -217,24 +219,27 @@
         from_prev = passed_along(high_part, ("space", "sub"), 1)
         return out_t, (middle + from_next + from_prev).astype(jnp.bfloat16)
 
-    def work(step, sums):
+    def work(step, state):
+        weights_t, sums = state
+        if weights_t is None:
+            weights_t = weights.transpose(0, 2, 1)
         chunk = step - first_step
         if 0 <= chunk < chunk_count:
-            return forward_chunk(weights_t, grad_blocks, scalars, gathered, sums, chunk, chunk_size)
-        if chunk == chunk_count:
-            return exchanged(sums)
-        return sums
-
-    sums = None
-    if axis_count & (axis_count - 1) or grad_sum.size % axis_count:
+            sums = forward_chunk(weights_t, grad_blocks, scalars, gathered, sums, chunk, chunk_size)
+        elif step == exchange_step:
+            sums = exchanged(sums)
+        return weights_t, sums
+
+    state = (None, None)
+    if power_of_two:
+        grand_total, state = summed_everywhere(
+            grad_sum, ("space", "sub"), work, state, exchange_step
+        )
+    else:
         grand_total = lax.psum(grad_sum, ("space", "sub"))
-        for chunk in range(chunk_count + 1):
-            sums = work(chunk + first_step, sums)
-    else:
-        grand_total, sums = summed_everywhere(
-            grad_sum, ("space", "sub"), work, sums, first_step + chunk_count
-        )
-    out_t, grad_features = sums
+        for step in range(exchange_step + 1):
+            state = work(step, state)
+    out_t, grad_features = state[1]
     out_sum = out_t.transpose(0, 2, 1)
     output = out_sum.reshape(local_rows, channels).astype(jnp.bfloat16)
     return (output, grad_features, grand_total)

time: 159 us -> 154 us (0.969)
  waiting for transfers between devices: 40.9 us -> 31.6 us
  starting transfers between devices: 39.3 us -> 43.3 us
    ppermute x6, waiting for transfers between devices: 14.9 us -> 10.2 us  [summed_everywhere(): other = lax.ppermute(flat, axis, [(i, i ^ mask) for i in range(count)])]
    ppermute x4, waiting for transfers between devices: 18.2 us -> 14.4 us  [passed_along(): lax.ppermute(value, axis, [(source, source + steps) for source in range(l...]
    ppermute x4, starting transfers between devices: 26.2 us -> 28.6 us  [passed_along(): lax.ppermute(value, axis, [(source, source + steps) for source in range(l...]
    ppermute x6, starting transfers between devices: 1.11 us -> 2.92 us  [summed_everywhere(): other = lax.ppermute(flat, axis, [(i, i ^ mask) for i in range(count)])]
  transfers between devices with their start and end apart: 19 -> 19, of which waited for: 9 -> 8; matrix products, arithmetic and copies ran while one was open for 4% -> 4% of each run, Pallas kernels for 32% -> 33%
where the time goes in v9:
time: 154 us
  Pallas kernels  61.9 us (40%)
  starting transfers between devices  43.3 us (28%)
  waiting for transfers between devices  31.6 us (21%)
  other arithmetic  9.15 us (6%)
  local copies, waits for them, and re-layouts  6.18 us (4%)
  between operations  1.55 us (1%)
    pallas_call x8, Pallas kernels, forward_chunk(): pl.pallas_call(functools.partial(sweep_kernel, chunk * chunk_size), grid=...  50.3 us
    ppermute x4, starting transfers between devices, passed_along(): lax.ppermute(value, axis, [(source, source + steps) for source in range(l...  28.6 us
    ppermute x4, waiting for transfers between devices, passed_along(): lax.ppermute(value, axis, [(source, source + steps) for source in range(l...  14.4 us
    pallas_call x1, Pallas kernels, grad_sweep(): pl.pallas_call(grad_kernel, out_shape=(jax.ShapeDtypeStruct((kernel_count...  11.6 us
    ppermute x6, waiting for transfers between devices, summed_everywhere(): other = lax.ppermute(flat, axis, [(i, i ^ mask) for i in range(count)])  10.2 us
    ppermute x3, starting transfers between devices, summed_everywhere(): lax.ppermute(flat, axis, [(i, i ^ mask) for i in range(count)])  7.47 us
    ppermute x6, waiting for transfers between devices, summed_everywhere(): received = lax.ppermute(send, axis, [(i, i ^ mask) for i in range(count)])  7.05 us
    ppermute x6, starting transfers between devices, summed_everywhere(): received = lax.ppermute(send, axis, [(i, i ^ mask) for i in range(count)])  4.33 us
  transfers between devices with their start and end apart: 19, of which 8 were waited for; matrix products, arithmetic and copies ran while one was open for 4% of the time, Pallas kernels for 33%

profile of v9, /device:TPU:127, one launch (start us, length us, event | category | flops | bytes accessed | tf_op | source)
XLA Modules:
  0.0 153.6 jit_solution(9865235046149396844)
XLA Ops:
  0.6 2.6 %collective-permute-start.1 = (bf16[1024,128]{1,0:T(8,128)(2,1)}, bf16[1024,128]{1,0:T(8,128)(2,1)S(1)}, u32[]{:S(2)}, u32[]{:S(2)}) collective-permute-start(bf16[1024,128]{1,0:T(8,128)(2,1)} %param.8), channel_id=1, source_target_pairs={{1,0},{2,1},{3,2},{4,3},{5,4},{6,5},{7,6},{8,7},{9,8},{10,9},{11,1... | collective-permute-start | bytes 786440 | tf_op jit(solution)/shard_map/ppermute | solution.py:17
  3.2 8.4 %collective-permute-start = (bf16[1024,128]{1,0:T(8,128)(2,1)}, bf16[1024,128]{1,0:T(8,128)(2,1)S(1)}, u32[]{:S(2)}, u32[]{:S(2)}) collective-permute-start(bf16[1024,128]{1,0:T(8,128)(2,1)} %param.8), channel_id=1, source_target_pairs={{0,1},{1,2},{2,3},{3,4},{4,5},{5,6},{6,7},{7,8},{8,9},{9,10},{10,1... | collective-permute-start | bytes 786440 | tf_op jit(solution)/shard_map/ppermute | solution.py:17
  11.6 1.2 broadcast_clamp_fusion.1.offsets
  13.5 1.3 fusion.3
  16.3 1.2 copy.26
  17.5 11.6 %shard_map.103 = (f32[27,128,128]{2,1,0:T(8,128)}, bf16[256,128,128]{2,1,0:T(8,128)(2,1)}) custom-call(s32[256]{0:T(256)} %broadcast_clamp_fusion.1.offsets, s32[256]{0:T(256)} %get-tuple-element.126.blocks_at, s32[256]{0:T(256)} %get-tuple-element.127.targets, s32[1]{0:T(128)S(6)} %min.29.live, bf16[24,128,128]{2,1,0:T(8,128)(2,1)} %bitcast.46, ...), custom_call_target="tpu_custom_call" | custom-call | tf_op jit(solution)/shard_map/pallas_call | solution.py:146
  29.1 1.6 %broadcast_multiply_fusion = f32[27,128,128]{2,1,0:T(8,128)S(1)} fusion(f32[27,128,128]{2,1,0:T(8,128)} %get-tuple-element.63), kind=kLoop, calls=%fused_computation.3 | loop fusion | flops 442368 | bytes 3538944 | tf_op jit(solution)/shard_map/mul | solution.py:204
  31.9 1.6 %copy.27 = bf16[27,128,128]{1,2,0:T(8,128)(2,1)} copy(bf16[27,128,128]{2,1,0:T(8,128)(2,1)S(1)} %copy-done.1) | data formatting | bytes 1769472 | tf_op args[1]
  33.6 1.3 select_add_fusion
  35.0 5.8 %shard_map.104 = (f32[8,128,128]{2,1,0:T(8,128)}, f32[24,128,128]{2,1,0:T(8,128)}) custom-call(s32[256]{0:T(256)} %broadcast_clamp_fusion.1.offsets, s32[256]{0:T(256)} %get-tuple-element.126.blocks_at, s32[256]{0:T(256)} %get-tuple-element.127.targets, s32[1]{0:T(128)S(6)} %min.29.live, bf16[27,128,128]{2,1,0:T(8,128)(2,1)} %bitcast.18, ...), custom_call_target="tpu_custom_call" | custom-call | tf_op jit(solution)/shard_map/pallas_call | solution.py:169
  40.8 5.8 %collective-permute-done.3 = f32[110592]{0:T(1024)S(1)} collective-permute-done((f32[110592]{0:T(1024)S(1)}, f32[110592]{0:T(1024)S(1)}, u32[]{:S(2)}, u32[]{:S(2)}) %collective-permute-start.3) | collective-permute-done | bytes 442400 | tf_op jit(solution)/shard_map/ppermute | solution.py:43
  46.9 6.3 %shard_map.105 = (f32[8,128,128]{2,1,0:T(8,128)}, f32[24,128,128]{2,1,0:T(8,128)}) custom-call(s32[256]{0:T(256)} %broadcast_clamp_fusion.1.offsets, s32[256]{0:T(256)} %get-tuple-element.126.blocks_at, s32[256]{0:T(256)} %get-tuple-element.127.targets, s32[1]{0:T(128)S(6)} %min.29.live, ...), custom_call_target="tpu_custom_call", output_to_operand_aliasing={{0}: (8, {}), {1}: (9, {})} | custom-call | tf_op jit(solution)/shard_map/pallas_call | solution.py:169
  53.2 1.2 collective-permute-done.4
  54.6 6.3 %shard_map.106 = (f32[8,128,128]{2,1,0:T(8,128)}, f32[24,128,128]{2,1,0:T(8,128)}) custom-call(s32[256]{0:T(256)} %broadcast_clamp_fusion.1.offsets, s32[256]{0:T(256)} %get-tuple-element.126.blocks_at, s32[256]{0:T(256)} %get-tuple-element.127.targets, s32[1]{0:T(128)S(6)} %min.29.live, ...), custom_call_target="tpu_custom_call", output_to_operand_aliasing={{0}: (8, {}), {1}: (9, {})} | custom-call | tf_op jit(solution)/shard_map/pallas_call | solution.py:169
  61.0 3.9 %collective-permute-start.6 = (f32[13824]{0:T(1024)S(1)}, f32[13824]{0:T(1024)S(1)}, u32[]{:S(2)}, u32[]{:S(2)}) collective-permute-start(f32[13824]{0:T(1024)S(1)} %slice_select_fusion.4), channel_id=1, source_target_pairs={{0,16},{1,17},{2,18},{3,19},{4,20},{5,21},{6,22},{7,23},{8,24},{9,... | collective-permute-start | bytes 165896 | tf_op jit(solution)/shard_map/ppermute | solution.py:43
  64.9 6.3 %shard_map.107 = (f32[8,128,128]{2,1,0:T(8,128)}, f32[24,128,128]{2,1,0:T(8,128)}) custom-call(s32[256]{0:T(256)} %broadcast_clamp_fusion.1.offsets, s32[256]{0:T(256)} %get-tuple-element.126.blocks_at, s32[256]{0:T(256)} %get-tuple-element.127.targets, s32[1]{0:T(128)S(6)} %min.29.live, ...), custom_call_target="tpu_custom_call", output_to_operand_aliasing={{0}: (8, {}), {1}: (9, {})} | custom-call | tf_op jit(solution)/shard_map/pallas_call | solution.py:169
  71.3 6.4 %shard_map.108 = (f32[8,128,128]{2,1,0:T(8,128)}, f32[24,128,128]{2,1,0:T(8,128)}) custom-call(s32[256]{0:T(256)} %broadcast_clamp_fusion.1.offsets, s32[256]{0:T(256)} %get-tuple-element.126.blocks_at, s32[256]{0:T(256)} %get-tuple-element.127.targets, s32[1]{0:T(128)S(6)} %min.29.live, ...), custom_call_target="tpu_custom_call", output_to_operand_aliasing={{0}: (8, {}), {1}: (9, {})} | custom-call | tf_op jit(solution)/shard_map/pallas_call | solution.py:169
  77.7 5.3 %collective-permute-start.10 = (f32[6912]{0:T(1024)S(1)}, f32[6912]{0:T(1024)S(1)}, u32[]{:S(2)}, u32[]{:S(2)}) collective-permute-start(f32[6912]{0:T(1024)S(1)} %select_add_fusion.5), channel_id=1, source_target_pairs={{0,192},{1,193},{2,194},{3,195},{4,196},{5,197},{6,198},{7,199},{8... | collective-permute-start | bytes 82952 | tf_op jit(solution)/shard_map/ppermute | solution.py:46
  83.7 1.5 collective-permute-start.8
  85.2 6.4 %shard_map.109 = (f32[8,128,128]{2,1,0:T(8,128)}, f32[24,128,128]{2,1,0:T(8,128)}) custom-call(s32[256]{0:T(256)} %broadcast_clamp_fusion.1.offsets, s32[256]{0:T(256)} %get-tuple-element.126.blocks_at, s32[256]{0:T(256)} %get-tuple-element.127.targets, s32[1]{0:T(128)S(6)} %min.29.live, ...), custom_call_target="tpu_custom_call", output_to_operand_aliasing={{0}: (8, {}), {1}: (9, {})} | custom-call | tf_op jit(solution)/shard_map/pallas_call | solution.py:169
  92.1 6.4 %shard_map.110 = (f32[8,128,128]{2,1,0:T(8,128)}, f32[24,128,128]{2,1,0:T(8,128)}) custom-call(s32[256]{0:T(256)} %broadcast_clamp_fusion.1.offsets, s32[256]{0:T(256)} %get-tuple-element.126.blocks_at, s32[256]{0:T(256)} %get-tuple-element.127.targets, s32[1]{0:T(128)S(6)} %min.29.live, ...), custom_call_target="tpu_custom_call", output_to_operand_aliasing={{0}: (8, {}), {1}: (9, {})} | custom-call | tf_op jit(solution)/shard_map/pallas_call | solution.py:169
  98.6 6.3 %shard_map.111 = (f32[8,128,128]{2,1,0:T(8,128)}, f32[24,128,128]{2,1,0:T(8,128)}) custom-call(s32[256]{0:T(256)} %broadcast_clamp_fusion.1.offsets, s32[256]{0:T(256)} %get-tuple-element.126.blocks_at, s32[256]{0:T(256)} %get-tuple-element.127.targets, s32[1]{0:T(128)S(6)} %min.29.live, ...), custom_call_target="tpu_custom_call", output_to_operand_aliasing={{0}: (8, {}), {1}: (9, {})} | custom-call | tf_op jit(solution)/shard_map/pallas_call | solution.py:169
  105.4 3.5 %collective-permute-done.13 = f32[27648]{0:T(1024)S(1)} collective-permute-done((f32[27648]{0:T(1024)S(1)}, f32[27648]{0:T(1024)S(1)}, u32[]{:S(2)}, u32[]{:S(2)}) %collective-permute-start.13) | collective-permute-done | bytes 110624 | tf_op jit(solution)/shard_map/ppermute | solution.py:53
  108.9 1.2 collective-permute-start.14
  110.1 5.2 %collective-permute-done.14 = f32[55296]{0:T(1024)S(1)} collective-permute-done((f32[55296]{0:T(1024)S(1)}, f32[55296]{0:T(1024)S(1)}, u32[]{:S(2)}, u32[]{:S(2)}) %collective-permute-start.14) | collective-permute-done | bytes 221216 | tf_op jit(solution)/shard_map/ppermute | solution.py:53
  116.0 1.5 fusion.4
  117.4 15.5 %collective-permute-start.17 = (f32[1024,128]{1,0:T(8,128)S(1)}, f32[1024,128]{1,0:T(8,128)S(1)}, u32[]{:S(2)}, u32[]{:S(2)}) collective-permute-start(f32[1024,128]{1,0:T(8,128)S(1)} %bitcast.50), channel_id=1, source_target_pairs={{0,1},{1,2},{2,3},{3,4},{4,5},{5,6},{6,7},{7,8},{8,9},{9,10},{10,1... | collective-permute-start | bytes 1572872 | tf_op jit(solution)/shard_map/ppermute | solution.py:17
  133.0 2.1 %collective-permute-start.16 = (f32[1024,128]{1,0:T(8,128)S(1)}, f32[1024,128]{1,0:T(8,128)S(1)}, u32[]{:S(2)}, u32[]{:S(2)}) collective-permute-start(f32[1024,128]{1,0:T(8,128)S(1)} %bitcast.49), channel_id=1, source_target_pairs={{1,0},{2,1},{3,2},{4,3},{5,4},{6,5},{7,6},{8,7},{9,8},{10,9},{11,1... | collective-permute-start | bytes 1572872 | tf_op jit(solution)/shard_map/ppermute | solution.py:17
  135.1 4.0 %collective-permute-done.17 = f32[1024,128]{1,0:T(8,128)S(1)} collective-permute-done((f32[1024,128]{1,0:T(8,128)S(1)}, f32[1024,128]{1,0:T(8,128)S(1)}, u32[]{:S(2)}, u32[]{:S(2)}) %collective-permute-start.17) | collective-permute-done | bytes 524320 | tf_op jit(solution)/shard_map/ppermute | solution.py:17
  139.1 10.0 %collective-permute-done.16 = f32[1024,128]{1,0:T(8,128)S(1)} collective-permute-done((f32[1024,128]{1,0:T(8,128)S(1)}, f32[1024,128]{1,0:T(8,128)S(1)}, u32[]{:S(2)}, u32[]{:S(2)}) %collective-permute-start.16) | collective-permute-done | bytes 524320 | tf_op jit(solution)/shard_map/ppermute | solution.py:17
  150.7 1.5 collective-permute-done.18
  152.3 1.4 maximum_select_fusion
  (48 shorter events, 7.5 us)
Async XLA Ops:
  0.6 14.2 %collective-permute-start.1 = (bf16[1024,128]{1,0:T(8,128)(2,1)}, bf16[1024,128]{1,0:T(8,128)(2,1)S(1)}, u32[]{:S(2)}, u32[]{:S(2)}) collective-permute-start(bf16[1024,128]{1,0:T(8,128)(2,1)} %param.8), channel_id=1, source_target_pairs={{1,0},{2,1},{3,2},{4,3},{5,4},{6,5},{7,6},{8,7},{9,8},{10,9},{11,1... | collective-permute-start | bytes 786440 | tf_op jit(solution)/shard_map/ppermute | solution.py:17
  3.2 12.0 %collective-permute-start = (bf16[1024,128]{1,0:T(8,128)(2,1)}, bf16[1024,128]{1,0:T(8,128)(2,1)S(1)}, u32[]{:S(2)}, u32[]{:S(2)}) collective-permute-start(bf16[1024,128]{1,0:T(8,128)(2,1)} %param.8), channel_id=1, source_target_pairs={{0,1},{1,2},{2,3},{3,4},{4,5},{5,6},{6,7},{7,8},{8,9},{9,10},{10,1... | collective-permute-start | bytes 786440 | tf_op jit(solution)/shard_map/ppermute | solution.py:17
  30.8 1.2 copy-start.1
  30.9 2.7 %collective-permute-start.2 = (f32[221184]{0:T(1024)S(1)}, f32[221184]{0:T(1024)}, u32[]{:S(2)}, u32[]{:S(2)}) collective-permute-start(f32[221184]{0:T(1024)S(1)} %slice_select_fusion), channel_id=1, source_target_pairs={{0,1},{1,0},{2,3},{3,2},{4,5},{5,4},{6,7},{7,6},{8,9},{9,8},{10,11... | collective-permute-start | bytes 2654216 | tf_op jit(solution)/shard_map/ppermute | solution.py:43
  34.9 11.7 %collective-permute-start.3 = (f32[110592]{0:T(1024)S(1)}, f32[110592]{0:T(1024)S(1)}, u32[]{:S(2)}, u32[]{:S(2)}) collective-permute-start(f32[110592]{0:T(1024)S(1)} %slice_select_fusion.1), channel_id=1, source_target_pairs={{0,2},{1,3},{2,0},{3,1},{4,6},{5,7},{6,4},{7,5},{8,10},{9,11},{10,... | collective-permute-start | bytes 1327112 | tf_op jit(solution)/shard_map/ppermute | solution.py:43
  46.8 7.6 %collective-permute-start.4 = (f32[55296]{0:T(1024)S(1)}, f32[55296]{0:T(1024)S(1)}, u32[]{:S(2)}, u32[]{:S(2)}) collective-permute-start(f32[55296]{0:T(1024)S(1)} %slice_select_fusion.2), channel_id=1, source_target_pairs={{0,4},{1,5},{2,6},{3,7},{4,0},{5,1},{6,2},{7,3},{8,12},{9,13},{10,... | collective-permute-start | bytes 663560 | tf_op jit(solution)/shard_map/ppermute | solution.py:43
  54.5 6.5 %collective-permute-start.5 = (f32[27648]{0:T(1024)S(1)}, f32[27648]{0:T(1024)S(1)}, u32[]{:S(2)}, u32[]{:S(2)}) collective-permute-start(f32[27648]{0:T(1024)S(1)} %slice_select_fusion.3), channel_id=1, source_target_pairs={{0,8},{1,9},{2,10},{3,11},{4,12},{5,13},{6,14},{7,15},{8,0},{9,1},... | collective-permute-start | bytes 331784 | tf_op jit(solution)/shard_map/ppermute | solution.py:43
  61.0 10.2 %collective-permute-start.6 = (f32[13824]{0:T(1024)S(1)}, f32[13824]{0:T(1024)S(1)}, u32[]{:S(2)}, u32[]{:S(2)}) collective-permute-start(f32[13824]{0:T(1024)S(1)} %slice_select_fusion.4), channel_id=1, source_target_pairs={{0,16},{1,17},{2,18},{3,19},{4,20},{5,21},{6,22},{7,23},{8,24},{9,... | collective-permute-start | bytes 165896 | tf_op jit(solution)/shard_map/ppermute | solution.py:43
  71.2 6.5 %collective-permute-start.7 = (f32[6912]{0:T(1024)S(1)}, f32[6912]{0:T(1024)S(1)}, u32[]{:S(2)}, u32[]{:S(2)}) collective-permute-start(f32[6912]{0:T(1024)S(1)} %slice_select_fusion.5), channel_id=1, source_target_pairs={{0,32},{1,33},{2,34},{3,35},{4,36},{5,37},{6,38},{7,39},{8,40},{9,... | collective-permute-start | bytes 82952 | tf_op jit(solution)/shard_map/ppermute | solution.py:43
  77.7 13.8 %collective-permute-start.10 = (f32[6912]{0:T(1024)S(1)}, f32[6912]{0:T(1024)S(1)}, u32[]{:S(2)}, u32[]{:S(2)}) collective-permute-start(f32[6912]{0:T(1024)S(1)} %select_add_fusion.5), channel_id=1, source_target_pairs={{0,192},{1,193},{2,194},{3,195},{4,196},{5,197},{6,198},{7,199},{8... | collective-permute-start | bytes 82952 | tf_op jit(solution)/shard_map/ppermute | solution.py:46
  83.0 8.6 %collective-permute-start.9 = (f32[6912]{0:T(1024)S(1)}, f32[6912]{0:T(1024)S(1)}, u32[]{:S(2)}, u32[]{:S(2)}) collective-permute-start(f32[6912]{0:T(1024)S(1)} %select_add_fusion.5), channel_id=1, source_target_pairs={{0,128},{1,129},{2,130},{3,131},{4,132},{5,133},{6,134},{7,135},{8... | collective-permute-start | bytes 82952 | tf_op jit(solution)/shard_map/ppermute | solution.py:46
  83.7 7.8 %collective-permute-start.8 = (f32[6912]{0:T(1024)S(1)}, f32[6912]{0:T(1024)S(1)}, u32[]{:S(2)}, u32[]{:S(2)}) collective-permute-start(f32[6912]{0:T(1024)S(1)} %select_add_fusion.5), channel_id=1, source_target_pairs={{0,64},{1,65},{2,66},{3,67},{4,68},{5,69},{6,70},{7,71},{8,72},{9,... | collective-permute-start | bytes 82952 | tf_op jit(solution)/shard_map/ppermute | solution.py:46
  91.6 6.8 %collective-permute-start.11 = (f32[6912]{0:T(1024)S(1)}, f32[6912]{0:T(1024)S(1)}, u32[]{:S(2)}, u32[]{:S(2)}) collective-permute-start(f32[6912]{0:T(1024)S(1)} %add_add_fusion), channel_id=1, source_target_pairs={{0,32},{1,33},{2,34},{3,35},{4,36},{5,37},{6,38},{7,39},{8,40},{9,... | collective-permute-start | bytes 82952 | tf_op jit(solution)/shard_map/ppermute | solution.py:53
  98.4 6.5 %collective-permute-start.12 = (f32[13824]{0:T(1024)S(1)}, f32[13824]{0:T(1024)S(1)}, u32[]{:S(2)}, u32[]{:S(2)}) collective-permute-start(f32[13824]{0:T(1024)S(1)} %maximum_select_fusion.5), channel_id=1, source_target_pairs={{0,16},{1,17},{2,18},{3,19},{4,20},{5,21},{6,22},{7,23},{8,24},{9,... | collective-permute-start | bytes 165896 | tf_op jit(solution)/shard_map/ppermute | solution.py:53
  104.9 3.9 %collective-permute-start.13 = (f32[27648]{0:T(1024)S(1)}, f32[27648]{0:T(1024)S(1)}, u32[]{:S(2)}, u32[]{:S(2)}) collective-permute-start(f32[27648]{0:T(1024)S(1)} %maximum_select_fusion.4), channel_id=1, source_target_pairs={{0,8},{1,9},{2,10},{3,11},{4,12},{5,13},{6,14},{7,15},{8,0},{9,1},... | collective-permute-start | bytes 331784 | tf_op jit(solution)/shard_map/ppermute | solution.py:53
  108.9 6.4 %collective-permute-start.14 = (f32[55296]{0:T(1024)S(1)}, f32[55296]{0:T(1024)S(1)}, u32[]{:S(2)}, u32[]{:S(2)}) collective-permute-start(f32[55296]{0:T(1024)S(1)} %maximum_select_fusion.3), channel_id=1, source_target_pairs={{0,4},{1,5},{2,6},{3,7},{4,0},{5,1},{6,2},{7,3},{8,12},{9,13},{10,... | collective-permute-start | bytes 663560 | tf_op jit(solution)/shard_map/ppermute | solution.py:53
  115.3 19.8 %collective-permute-start.15 = (f32[110592]{0:T(1024)S(1)}, f32[110592]{0:T(1024)S(1)}, u32[]{:S(2)}, u32[]{:S(2)}) collective-permute-start(f32[110592]{0:T(1024)S(1)} %maximum_select_fusion.2), channel_id=1, source_target_pairs={{0,2},{1,3},{2,0},{3,1},{4,6},{5,7},{6,4},{7,5},{8,10},{9,11},{10,... | collective-permute-start | bytes 1327112 | tf_op jit(solution)/shard_map/ppermute | solution.py:53
  117.4 21.6 %collective-permute-start.17 = (f32[1024,128]{1,0:T(8,128)S(1)}, f32[1024,128]{1,0:T(8,128)S(1)}, u32[]{:S(2)}, u32[]{:S(2)}) collective-permute-start(f32[1024,128]{1,0:T(8,128)S(1)} %bitcast.50), channel_id=1, source_target_pairs={{0,1},{1,2},{2,3},{3,4},{4,5},{5,6},{6,7},{7,8},{8,9},{9,10},{10,1... | collective-permute-start | bytes 1572872 | tf_op jit(solution)/shard_map/ppermute | solution.py:17
  133.0 16.9 %copy-start = (f32[8,128,128]{2,1,0:T(8,128)S(1)}, f32[8,128,128]{2,1,0:T(8,128)}, u32[]{:S(2)}) copy-start(f32[8,128,128]{2,1,0:T(8,128)} %get-tuple-element.120) | copy-start | bytes 1572868
  133.0 16.1 %collective-permute-start.16 = (f32[1024,128]{1,0:T(8,128)S(1)}, f32[1024,128]{1,0:T(8,128)S(1)}, u32[]{:S(2)}, u32[]{:S(2)}) collective-permute-start(f32[1024,128]{1,0:T(8,128)S(1)} %bitcast.49), channel_id=1, source_target_pairs={{1,0},{2,1},{3,2},{4,3},{5,4},{6,5},{7,6},{8,7},{9,8},{10,9},{11,1... | collective-permute-start | bytes 1572872 | tf_op jit(solution)/shard_map/ppermute | solution.py:17
  149.8 2.4 %collective-permute-start.18 = (f32[221184]{0:T(1024)S(1)}, f32[221184]{0:T(1024)S(1)}, u32[]{:S(2)}, u32[]{:S(2)}) collective-permute-start(f32[221184]{0:T(1024)S(1)} %maximum_select_fusion.1), channel_id=1, source_target_pairs={{0,1},{1,0},{2,3},{3,2},{4,5},{5,4},{6,7},{7,6},{8,9},{9,8},{10,11... | collective-permute-start | bytes 2654216 | tf_op jit(solution)/shard_map/ppermute | solution.py:53

commit v10 on v9

--- a/solution.py
+++ b/solution.py
@@ -123,7 +123,7 @@
 
 UNROLL = 32
 CHUNKS = 8
-FIRST_STEP = 1
+FIRST_STEP = 0
 
 
 def rulebook_scalars(rulebook, myself, blocks, kernel_count):

time: 154 us -> 154 us (level)
  waiting for transfers between devices: 31.6 us -> 37 us
  starting transfers between devices: 43.3 us -> 39.2 us
    ppermute x6, waiting for transfers between devices: 10.2 us -> 15.1 us  [summed_everywhere(): other = lax.ppermute(flat, axis, [(i, i ^ mask) for i in range(count)])]
    ppermute x6, starting transfers between devices: 4.33 us -> 2.28 us  [summed_everywhere(): received = lax.ppermute(send, axis, [(i, i ^ mask) for i in range(count)])]
    ppermute x4, starting transfers between devices: 28.6 us -> 26.9 us  [passed_along(): lax.ppermute(value, axis, [(source, source + steps) for source in range(l...]
  transfers between devices with their start and end apart: 19 -> 19, of which waited for: 8 -> 9; matrix products, arithmetic and copies ran while one was open for 4% -> 3% of each run, Pallas kernels for 33% -> 33%
where the time goes in v10:
time: 154 us
  Pallas kernels  62 us (40%)
  starting transfers between devices  39.2 us (25%)
  waiting for transfers between devices  37 us (24%)
  other arithmetic  9.15 us (6%)
  local copies, waits for them, and re-layouts  4.83 us (3%)
  between operations  1.56 us (1%)
    pallas_call x8, Pallas kernels, forward_chunk(): pl.pallas_call(functools.partial(sweep_kernel, chunk * chunk_size), grid=...  50.4 us
    ppermute x4, starting transfers between devices, passed_along(): lax.ppermute(value, axis, [(source, source + steps) for source in range(l...  26.9 us
    ppermute x6, waiting for transfers between devices, summed_everywhere(): other = lax.ppermute(flat, axis, [(i, i ^ mask) for i in range(count)])  15.1 us
    ppermute x4, waiting for transfers between devices, passed_along(): lax.ppermute(value, axis, [(source, source + steps) for source in range(l...  14.4 us
    pallas_call x1, Pallas kernels, grad_sweep(): pl.pallas_call(grad_kernel, out_shape=(jax.ShapeDtypeStruct((kernel_count...  11.6 us
    ppermute x6, waiting for transfers between devices, summed_everywhere(): received = lax.ppermute(send, axis, [(i, i ^ mask) for i in range(count)])  7.48 us
    ppermute x3, starting transfers between devices, summed_everywhere(): lax.ppermute(flat, axis, [(i, i ^ mask) for i in range(count)])  7.47 us
  transfers between devices with their start and end apart: 19, of which 9 were waited for; matrix products, arithmetic and copies ran while one was open for 3% of the time, Pallas kernels for 33%

profile of v10, /device:TPU:127, one launch (start us, length us, event | category | flops | bytes accessed | tf_op | source)
XLA Modules:
  0.0 153.7 jit_solution(15777482982113497224)
XLA Ops:
  0.6 2.6 %collective-permute-start.1 = (bf16[1024,128]{1,0:T(8,128)(2,1)}, bf16[1024,128]{1,0:T(8,128)(2,1)S(1)}, u32[]{:S(2)}, u32[]{:S(2)}) collective-permute-start(bf16[1024,128]{1,0:T(8,128)(2,1)} %param.8), channel_id=1, source_target_pairs={{1,0},{2,1},{3,2},{4,3},{5,4},{6,5},{7,6},{8,7},{9,8},{10,9},{11,1... | collective-permute-start | bytes 786440 | tf_op jit(solution)/shard_map/ppermute | solution.py:17
  3.2 8.4 %collective-permute-start = (bf16[1024,128]{1,0:T(8,128)(2,1)}, bf16[1024,128]{1,0:T(8,128)(2,1)S(1)}, u32[]{:S(2)}, u32[]{:S(2)}) collective-permute-start(bf16[1024,128]{1,0:T(8,128)(2,1)} %param.8), channel_id=1, source_target_pairs={{0,1},{1,2},{2,3},{3,4},{4,5},{5,6},{6,7},{7,8},{8,9},{9,10},{10,1... | collective-permute-start | bytes 786440 | tf_op jit(solution)/shard_map/ppermute | solution.py:17
  11.6 1.2 broadcast_clamp_fusion.1.offsets
  13.5 1.3 fusion.3
  15.3 1.0 pad_maximum_fusion
  16.3 1.2 copy.26
  17.5 11.6 %shard_map.103 = (f32[27,128,128]{2,1,0:T(8,128)}, bf16[256,128,128]{2,1,0:T(8,128)(2,1)}) custom-call(s32[256]{0:T(256)} %broadcast_clamp_fusion.1.offsets, s32[256]{0:T(256)} %get-tuple-element.128.blocks_at, s32[256]{0:T(256)} %get-tuple-element.129.targets, s32[1]{0:T(128)S(6)} %min.29.live, bf16[24,128,128]{2,1,0:T(8,128)(2,1)} %bitcast.46, ...), custom_call_target="tpu_custom_call" | custom-call | tf_op jit(solution)/shard_map/pallas_call | solution.py:146
  29.1 1.6 %broadcast_multiply_fusion = f32[27,128,128]{2,1,0:T(8,128)S(1)} fusion(f32[27,128,128]{2,1,0:T(8,128)} %get-tuple-element.64), kind=kLoop, calls=%fused_computation.3 | loop fusion | flops 442368 | bytes 3538944 | tf_op jit(solution)/shard_map/mul | solution.py:204
  31.9 1.6 %copy.27 = bf16[27,128,128]{1,2,0:T(8,128)(2,1)} copy(bf16[27,128,128]{2,1,0:T(8,128)(2,1)S(1)} %copy-done.2) | data formatting | bytes 1769472 | tf_op args[1]
  33.6 5.8 %shard_map.104 = (f32[8,128,128]{2,1,0:T(8,128)}, f32[24,128,128]{2,1,0:T(8,128)}) custom-call(s32[256]{0:T(256)} %broadcast_clamp_fusion.1.offsets, s32[256]{0:T(256)} %get-tuple-element.128.blocks_at, s32[256]{0:T(256)} %get-tuple-element.129.targets, s32[1]{0:T(128)S(6)} %min.29.live, bf16[27,128,128]{2,1,0:T(8,128)(2,1)} %bitcast.18, ...), custom_call_target="tpu_custom_call" | custom-call | tf_op jit(solution)/shard_map/pallas_call | solution.py:169
  39.4 1.3 select_add_fusion
  40.8 6.4 %shard_map.105 = (f32[8,128,128]{2,1,0:T(8,128)}, f32[24,128,128]{2,1,0:T(8,128)}) custom-call(s32[256]{0:T(256)} %broadcast_clamp_fusion.1.offsets, s32[256]{0:T(256)} %get-tuple-element.128.blocks_at, s32[256]{0:T(256)} %get-tuple-element.129.targets, s32[1]{0:T(128)S(6)} %min.29.live, ...), custom_call_target="tpu_custom_call", output_to_operand_aliasing={{0}: (8, {}), {1}: (9, {})} | custom-call | tf_op jit(solution)/shard_map/pallas_call | solution.py:169
  47.2 5.8 %collective-permute-done.3 = f32[110592]{0:T(1024)S(1)} collective-permute-done((f32[110592]{0:T(1024)S(1)}, f32[110592]{0:T(1024)S(1)}, u32[]{:S(2)}, u32[]{:S(2)}) %collective-permute-start.3) | collective-permute-done | bytes 442400 | tf_op jit(solution)/shard_map/ppermute | solution.py:43
  53.2 6.4 %shard_map.106 = (f32[8,128,128]{2,1,0:T(8,128)}, f32[24,128,128]{2,1,0:T(8,128)}) custom-call(s32[256]{0:T(256)} %broadcast_clamp_fusion.1.offsets, s32[256]{0:T(256)} %get-tuple-element.128.blocks_at, s32[256]{0:T(256)} %get-tuple-element.129.targets, s32[1]{0:T(128)S(6)} %min.29.live, ...), custom_call_target="tpu_custom_call", output_to_operand_aliasing={{0}: (8, {}), {1}: (9, {})} | custom-call | tf_op jit(solution)/shard_map/pallas_call | solution.py:169
  59.6 1.7 %collective-permute-done.4 = f32[55296]{0:T(1024)S(1)} collective-permute-done((f32[55296]{0:T(1024)S(1)}, f32[55296]{0:T(1024)S(1)}, u32[]{:S(2)}, u32[]{:S(2)}) %collective-permute-start.4) | collective-permute-done | bytes 221216 | tf_op jit(solution)/shard_map/ppermute | solution.py:43
  61.4 6.4 %shard_map.107 = (f32[8,128,128]{2,1,0:T(8,128)}, f32[24,128,128]{2,1,0:T(8,128)}) custom-call(s32[256]{0:T(256)} %broadcast_clamp_fusion.1.offsets, s32[256]{0:T(256)} %get-tuple-element.128.blocks_at, s32[256]{0:T(256)} %get-tuple-element.129.targets, s32[1]{0:T(128)S(6)} %min.29.live, ...), custom_call_target="tpu_custom_call", output_to_operand_aliasing={{0}: (8, {}), {1}: (9, {})} | custom-call | tf_op jit(solution)/shard_map/pallas_call | solution.py:169
  67.8 1.8 %collective-permute-start.6 = (f32[13824]{0:T(1024)S(1)}, f32[13824]{0:T(1024)S(1)}, u32[]{:S(2)}, u32[]{:S(2)}) collective-permute-start(f32[13824]{0:T(1024)S(1)} %slice_select_fusion.4), channel_id=1, source_target_pairs={{0,16},{1,17},{2,18},{3,19},{4,20},{5,21},{6,22},{7,23},{8,24},{9,... | collective-permute-start | bytes 165896 | tf_op jit(solution)/shard_map/ppermute | solution.py:43
  69.7 6.4 %shard_map.108 = (f32[8,128,128]{2,1,0:T(8,128)}, f32[24,128,128]{2,1,0:T(8,128)}) custom-call(s32[256]{0:T(256)} %broadcast_clamp_fusion.1.offsets, s32[256]{0:T(256)} %get-tuple-element.128.blocks_at, s32[256]{0:T(256)} %get-tuple-element.129.targets, s32[1]{0:T(128)S(6)} %min.29.live, ...), custom_call_target="tpu_custom_call", output_to_operand_aliasing={{0}: (8, {}), {1}: (9, {})} | custom-call | tf_op jit(solution)/shard_map/pallas_call | solution.py:169
  76.2 6.4 %shard_map.109 = (f32[8,128,128]{2,1,0:T(8,128)}, f32[24,128,128]{2,1,0:T(8,128)}) custom-call(s32[256]{0:T(256)} %broadcast_clamp_fusion.1.offsets, s32[256]{0:T(256)} %get-tuple-element.128.blocks_at, s32[256]{0:T(256)} %get-tuple-element.129.targets, s32[1]{0:T(128)S(6)} %min.29.live, ...), custom_call_target="tpu_custom_call", output_to_operand_aliasing={{0}: (8, {}), {1}: (9, {})} | custom-call | tf_op jit(solution)/shard_map/pallas_call | solution.py:169
  82.6 5.3 %collective-permute-start.10 = (f32[6912]{0:T(1024)S(1)}, f32[6912]{0:T(1024)S(1)}, u32[]{:S(2)}, u32[]{:S(2)}) collective-permute-start(f32[6912]{0:T(1024)S(1)} %select_add_fusion.5), channel_id=1, source_target_pairs={{0,192},{1,193},{2,194},{3,195},{4,196},{5,197},{6,198},{7,199},{8... | collective-permute-start | bytes 82952 | tf_op jit(solution)/shard_map/ppermute | solution.py:46
  88.5 1.5 collective-permute-start.8
  90.0 6.4 %shard_map.110 = (f32[8,128,128]{2,1,0:T(8,128)}, f32[24,128,128]{2,1,0:T(8,128)}) custom-call(s32[256]{0:T(256)} %broadcast_clamp_fusion.1.offsets, s32[256]{0:T(256)} %get-tuple-element.128.blocks_at, s32[256]{0:T(256)} %get-tuple-element.129.targets, s32[1]{0:T(128)S(6)} %min.29.live, ...), custom_call_target="tpu_custom_call", output_to_operand_aliasing={{0}: (8, {}), {1}: (9, {})} | custom-call | tf_op jit(solution)/shard_map/pallas_call | solution.py:169
  96.9 6.4 %shard_map.111 = (f32[8,128,128]{2,1,0:T(8,128)}, f32[24,128,128]{2,1,0:T(8,128)}) custom-call(s32[256]{0:T(256)} %broadcast_clamp_fusion.1.offsets, s32[256]{0:T(256)} %get-tuple-element.128.blocks_at, s32[256]{0:T(256)} %get-tuple-element.129.targets, s32[1]{0:T(128)S(6)} %min.29.live, ...), custom_call_target="tpu_custom_call", output_to_operand_aliasing={{0}: (8, {}), {1}: (9, {})} | custom-call | tf_op jit(solution)/shard_map/pallas_call | solution.py:169
  104.1 3.8 %collective-permute-done.12 = f32[13824]{0:T(1024)S(1)} collective-permute-done((f32[13824]{0:T(1024)S(1)}, f32[13824]{0:T(1024)S(1)}, u32[]{:S(2)}, u32[]{:S(2)}) %collective-permute-start.12) | collective-permute-done | bytes 55328 | tf_op jit(solution)/shard_map/ppermute | solution.py:53
  108.1 4.2 %collective-permute-done.13 = f32[27648]{0:T(1024)S(1)} collective-permute-done((f32[27648]{0:T(1024)S(1)}, f32[27648]{0:T(1024)S(1)}, u32[]{:S(2)}, u32[]{:S(2)}) %collective-permute-start.13) | collective-permute-done | bytes 110624 | tf_op jit(solution)/shard_map/ppermute | solution.py:53
  113.1 5.6 %collective-permute-done.14 = f32[55296]{0:T(1024)S(1)} collective-permute-done((f32[55296]{0:T(1024)S(1)}, f32[55296]{0:T(1024)S(1)}, u32[]{:S(2)}, u32[]{:S(2)}) %collective-permute-start.14) | collective-permute-done | bytes 221216 | tf_op jit(solution)/shard_map/ppermute | solution.py:53
  119.1 13.9 %collective-permute-start.17 = (f32[1024,128]{1,0:T(8,128)S(1)}, f32[1024,128]{1,0:T(8,128)S(1)}, u32[]{:S(2)}, u32[]{:S(2)}) collective-permute-start(f32[1024,128]{1,0:T(8,128)S(1)} %bitcast.50), channel_id=1, source_target_pairs={{0,1},{1,2},{2,3},{3,4},{4,5},{5,6},{6,7},{7,8},{8,9},{9,10},{10,1... | collective-permute-start | bytes 1572872 | tf_op jit(solution)/shard_map/ppermute | solution.py:17
  133.1 2.1 %collective-permute-start.16 = (f32[1024,128]{1,0:T(8,128)S(1)}, f32[1024,128]{1,0:T(8,128)S(1)}, u32[]{:S(2)}, u32[]{:S(2)}) collective-permute-start(f32[1024,128]{1,0:T(8,128)S(1)} %bitcast.49), channel_id=1, source_target_pairs={{1,0},{2,1},{3,2},{4,3},{5,4},{6,5},{7,6},{8,7},{9,8},{10,9},{11,1... | collective-permute-start | bytes 1572872 | tf_op jit(solution)/shard_map/ppermute | solution.py:17
  135.2 4.0 %collective-permute-done.17 = f32[1024,128]{1,0:T(8,128)S(1)} collective-permute-done((f32[1024,128]{1,0:T(8,128)S(1)}, f32[1024,128]{1,0:T(8,128)S(1)}, u32[]{:S(2)}, u32[]{:S(2)}) %collective-permute-start.17) | collective-permute-done | bytes 524320 | tf_op jit(solution)/shard_map/ppermute | solution.py:17
  139.2 10.0 %collective-permute-done.16 = f32[1024,128]{1,0:T(8,128)S(1)} collective-permute-done((f32[1024,128]{1,0:T(8,128)S(1)}, f32[1024,128]{1,0:T(8,128)S(1)}, u32[]{:S(2)}, u32[]{:S(2)}) %collective-permute-start.16) | collective-permute-done | bytes 524320 | tf_op jit(solution)/shard_map/ppermute | solution.py:17
  150.8 1.5 collective-permute-done.18
  152.3 1.4 maximum_select_fusion
  (50 shorter events, 7.3 us)
Async XLA Ops:
  0.6 14.2 %collective-permute-start.1 = (bf16[1024,128]{1,0:T(8,128)(2,1)}, bf16[1024,128]{1,0:T(8,128)(2,1)S(1)}, u32[]{:S(2)}, u32[]{:S(2)}) collective-permute-start(bf16[1024,128]{1,0:T(8,128)(2,1)} %param.8), channel_id=1, source_target_pairs={{1,0},{2,1},{3,2},{4,3},{5,4},{6,5},{7,6},{8,7},{9,8},{10,9},{11,1... | collective-permute-start | bytes 786440 | tf_op jit(solution)/shard_map/ppermute | solution.py:17
  3.2 12.0 %collective-permute-start = (bf16[1024,128]{1,0:T(8,128)(2,1)}, bf16[1024,128]{1,0:T(8,128)(2,1)S(1)}, u32[]{:S(2)}, u32[]{:S(2)}) collective-permute-start(bf16[1024,128]{1,0:T(8,128)(2,1)} %param.8), channel_id=1, source_target_pairs={{0,1},{1,2},{2,3},{3,4},{4,5},{5,6},{6,7},{7,8},{8,9},{9,10},{10,1... | collective-permute-start | bytes 786440 | tf_op jit(solution)/shard_map/ppermute | solution.py:17
  30.8 1.2 copy-start.2
  30.9 8.5 %collective-permute-start.2 = (f32[221184]{0:T(1024)S(1)}, f32[221184]{0:T(1024)}, u32[]{:S(2)}, u32[]{:S(2)}) collective-permute-start(f32[221184]{0:T(1024)S(1)} %slice_select_fusion), channel_id=1, source_target_pairs={{0,1},{1,0},{2,3},{3,2},{4,5},{5,4},{6,7},{7,6},{8,9},{9,8},{10,11... | collective-permute-start | bytes 2654216 | tf_op jit(solution)/shard_map/ppermute | solution.py:43
  40.7 12.3 %collective-permute-start.3 = (f32[110592]{0:T(1024)S(1)}, f32[110592]{0:T(1024)S(1)}, u32[]{:S(2)}, u32[]{:S(2)}) collective-permute-start(f32[110592]{0:T(1024)S(1)} %slice_select_fusion.1), channel_id=1, source_target_pairs={{0,2},{1,3},{2,0},{3,1},{4,6},{5,7},{6,4},{7,5},{8,10},{9,11},{10,... | collective-permute-start | bytes 1327112 | tf_op jit(solution)/shard_map/ppermute | solution.py:43
  53.1 8.2 %collective-permute-start.4 = (f32[55296]{0:T(1024)S(1)}, f32[55296]{0:T(1024)S(1)}, u32[]{:S(2)}, u32[]{:S(2)}) collective-permute-start(f32[55296]{0:T(1024)S(1)} %slice_select_fusion.2), channel_id=1, source_target_pairs={{0,4},{1,5},{2,6},{3,7},{4,0},{5,1},{6,2},{7,3},{8,12},{9,13},{10,... | collective-permute-start | bytes 663560 | tf_op jit(solution)/shard_map/ppermute | solution.py:43
  61.3 6.5 %collective-permute-start.5 = (f32[27648]{0:T(1024)S(1)}, f32[27648]{0:T(1024)S(1)}, u32[]{:S(2)}, u32[]{:S(2)}) collective-permute-start(f32[27648]{0:T(1024)S(1)} %slice_select_fusion.3), channel_id=1, source_target_pairs={{0,8},{1,9},{2,10},{3,11},{4,12},{5,13},{6,14},{7,15},{8,0},{9,1},... | collective-permute-start | bytes 331784 | tf_op jit(solution)/shard_map/ppermute | solution.py:43
  67.8 8.2 %collective-permute-start.6 = (f32[13824]{0:T(1024)S(1)}, f32[13824]{0:T(1024)S(1)}, u32[]{:S(2)}, u32[]{:S(2)}) collective-permute-start(f32[13824]{0:T(1024)S(1)} %slice_select_fusion.4), channel_id=1, source_target_pairs={{0,16},{1,17},{2,18},{3,19},{4,20},{5,21},{6,22},{7,23},{8,24},{9,... | collective-permute-start | bytes 165896 | tf_op jit(solution)/shard_map/ppermute | solution.py:43
  76.1 6.5 %collective-permute-start.7 = (f32[6912]{0:T(1024)S(1)}, f32[6912]{0:T(1024)S(1)}, u32[]{:S(2)}, u32[]{:S(2)}) collective-permute-start(f32[6912]{0:T(1024)S(1)} %slice_select_fusion.5), channel_id=1, source_target_pairs={{0,32},{1,33},{2,34},{3,35},{4,36},{5,37},{6,38},{7,39},{8,40},{9,... | collective-permute-start | bytes 82952 | tf_op jit(solution)/shard_map/ppermute | solution.py:43
  82.6 13.8 %collective-permute-start.10 = (f32[6912]{0:T(1024)S(1)}, f32[6912]{0:T(1024)S(1)}, u32[]{:S(2)}, u32[]{:S(2)}) collective-permute-start(f32[6912]{0:T(1024)S(1)} %select_add_fusion.5), channel_id=1, source_target_pairs={{0,192},{1,193},{2,194},{3,195},{4,196},{5,197},{6,198},{7,199},{8... | collective-permute-start | bytes 82952 | tf_op jit(solution)/shard_map/ppermute | solution.py:46
  87.8 8.6 %collective-permute-start.9 = (f32[6912]{0:T(1024)S(1)}, f32[6912]{0:T(1024)S(1)}, u32[]{:S(2)}, u32[]{:S(2)}) collective-permute-start(f32[6912]{0:T(1024)S(1)} %select_add_fusion.5), channel_id=1, source_target_pairs={{0,128},{1,129},{2,130},{3,131},{4,132},{5,133},{6,134},{7,135},{8... | collective-permute-start | bytes 82952 | tf_op jit(solution)/shard_map/ppermute | solution.py:46
  88.5 7.9 %collective-permute-start.8 = (f32[6912]{0:T(1024)S(1)}, f32[6912]{0:T(1024)S(1)}, u32[]{:S(2)}, u32[]{:S(2)}) collective-permute-start(f32[6912]{0:T(1024)S(1)} %select_add_fusion.5), channel_id=1, source_target_pairs={{0,64},{1,65},{2,66},{3,67},{4,68},{5,69},{6,70},{7,71},{8,72},{9,... | collective-permute-start | bytes 82952 | tf_op jit(solution)/shard_map/ppermute | solution.py:46
  96.4 6.9 %collective-permute-start.11 = (f32[6912]{0:T(1024)S(1)}, f32[6912]{0:T(1024)S(1)}, u32[]{:S(2)}, u32[]{:S(2)}) collective-permute-start(f32[6912]{0:T(1024)S(1)} %add_add_fusion), channel_id=1, source_target_pairs={{0,32},{1,33},{2,34},{3,35},{4,36},{5,37},{6,38},{7,39},{8,40},{9,... | collective-permute-start | bytes 82952 | tf_op jit(solution)/shard_map/ppermute | solution.py:53
  103.3 15.7 %copy-start = (f32[24,128,128]{2,1,0:T(8,128)S(1)}, f32[24,128,128]{2,1,0:T(8,128)}, u32[]{:S(2)}) copy-start(f32[24,128,128]{2,1,0:T(8,128)} %get-tuple-element.121) | copy-start | bytes 4718596
  103.3 4.6 %collective-permute-start.12 = (f32[13824]{0:T(1024)S(1)}, f32[13824]{0:T(1024)S(1)}, u32[]{:S(2)}, u32[]{:S(2)}) collective-permute-start(f32[13824]{0:T(1024)S(1)} %maximum_select_fusion.5), channel_id=1, source_target_pairs={{0,16},{1,17},{2,18},{3,19},{4,20},{5,21},{6,22},{7,23},{8,24},{9,... | collective-permute-start | bytes 165896 | tf_op jit(solution)/shard_map/ppermute | solution.py:53
  108.0 4.3 %collective-permute-start.13 = (f32[27648]{0:T(1024)S(1)}, f32[27648]{0:T(1024)S(1)}, u32[]{:S(2)}, u32[]{:S(2)}) collective-permute-start(f32[27648]{0:T(1024)S(1)} %maximum_select_fusion.4), channel_id=1, source_target_pairs={{0,8},{1,9},{2,10},{3,11},{4,12},{5,13},{6,14},{7,15},{8,0},{9,1},... | collective-permute-start | bytes 331784 | tf_op jit(solution)/shard_map/ppermute | solution.py:53
  112.3 6.4 %collective-permute-start.14 = (f32[55296]{0:T(1024)S(1)}, f32[55296]{0:T(1024)S(1)}, u32[]{:S(2)}, u32[]{:S(2)}) collective-permute-start(f32[55296]{0:T(1024)S(1)} %maximum_select_fusion.3), channel_id=1, source_target_pairs={{0,4},{1,5},{2,6},{3,7},{4,0},{5,1},{6,2},{7,3},{8,12},{9,13},{10,... | collective-permute-start | bytes 663560 | tf_op jit(solution)/shard_map/ppermute | solution.py:53
  118.7 16.4 %collective-permute-start.15 = (f32[110592]{0:T(1024)S(1)}, f32[110592]{0:T(1024)S(1)}, u32[]{:S(2)}, u32[]{:S(2)}) collective-permute-start(f32[110592]{0:T(1024)S(1)} %maximum_select_fusion.2), channel_id=1, source_target_pairs={{0,2},{1,3},{2,0},{3,1},{4,6},{5,7},{6,4},{7,5},{8,10},{9,11},{10,... | collective-permute-start | bytes 1327112 | tf_op jit(solution)/shard_map/ppermute | solution.py:53
  119.1 20.0 %collective-permute-start.17 = (f32[1024,128]{1,0:T(8,128)S(1)}, f32[1024,128]{1,0:T(8,128)S(1)}, u32[]{:S(2)}, u32[]{:S(2)}) collective-permute-start(f32[1024,128]{1,0:T(8,128)S(1)} %bitcast.50), channel_id=1, source_target_pairs={{0,1},{1,2},{2,3},{3,4},{4,5},{5,6},{6,7},{7,8},{8,9},{9,10},{10,1... | collective-permute-start | bytes 1572872 | tf_op jit(solution)/shard_map/ppermute | solution.py:17
  133.1 16.9 %copy-start.1 = (f32[8,128,128]{2,1,0:T(8,128)S(1)}, f32[8,128,128]{2,1,0:T(8,128)}, u32[]{:S(2)}) copy-start(f32[8,128,128]{2,1,0:T(8,128)} %get-tuple-element.122) | copy-start | bytes 1572868
  133.1 16.1 %collective-permute-start.16 = (f32[1024,128]{1,0:T(8,128)S(1)}, f32[1024,128]{1,0:T(8,128)S(1)}, u32[]{:S(2)}, u32[]{:S(2)}) collective-permute-start(f32[1024,128]{1,0:T(8,128)S(1)} %bitcast.49), channel_id=1, source_target_pairs={{1,0},{2,1},{3,2},{4,3},{5,4},{6,5},{7,6},{8,7},{9,8},{10,9},{11,1... | collective-permute-start | bytes 1572872 | tf_op jit(solution)/shard_map/ppermute | solution.py:17
  149.9 2.4 %collective-permute-start.18 = (f32[221184]{0:T(1024)S(1)}, f32[221184]{0:T(1024)S(1)}, u32[]{:S(2)}, u32[]{:S(2)}) collective-permute-start(f32[221184]{0:T(1024)S(1)} %maximum_select_fusion.1), channel_id=1, source_target_pairs={{0,1},{1,0},{2,3},{3,2},{4,5},{5,4},{6,7},{7,6},{8,9},{9,8},{10,11... | collective-permute-start | bytes 2654216 | tf_op jit(solution)/shard_map/ppermute | solution.py:53

commit v11 on v10

--- a/solution.py
+++ b/solution.py
@@ -87,7 +87,7 @@
         )
         return carry
 
-    lax.fori_loop(0, rows_ref.shape[0], advance, 0, unroll=UNROLL)
+    lax.fori_loop(0, rows_ref.shape[0], advance, 0, unroll=min(UNROLL, rows_ref.shape[0]))
 
 
 def sweep_kernel(first, offsets, blocks_at, targets, live, weights_t_ref, cot_ref, rows_ref,
@@ -118,10 +118,10 @@
         )
         return carry
 
-    lax.fori_loop(0, rows_ref.shape[0], advance, 0, unroll=UNROLL)
-
-
-UNROLL = 32
+    lax.fori_loop(0, rows_ref.shape[0], advance, 0, unroll=min(UNROLL, rows_ref.shape[0]))
+
+
+UNROLL = 64
 CHUNKS = 8
 FIRST_STEP = 0
 

time: 154 us -> 153 us (level)
  no operation moved by 1% of the time
where the time goes in v11:
time: 153 us
  Pallas kernels  61 us (40%)
  starting transfers between devices  39.4 us (26%)
  waiting for transfers between devices  36.9 us (24%)
  other arithmetic  9.15 us (6%)
  local copies, waits for them, and re-layouts  4.83 us (3%)
  between operations  1.56 us (1%)
    pallas_call x8, Pallas kernels, forward_chunk(): pl.pallas_call(functools.partial(sweep_kernel, chunk * chunk_size), grid=...  50.4 us
    ppermute x4, starting transfers between devices, passed_along(): lax.ppermute(value, axis, [(source, source + steps) for source in range(l...  26.9 us
    ppermute x6, waiting for transfers between devices, summed_everywhere(): other = lax.ppermute(flat, axis, [(i, i ^ mask) for i in range(count)])  15.1 us
    ppermute x4, waiting for transfers between devices, passed_along(): lax.ppermute(value, axis, [(source, source + steps) for source in range(l...  14.4 us
    pallas_call x1, Pallas kernels, grad_sweep(): pl.pallas_call(grad_kernel, out_shape=(jax.ShapeDtypeStruct((kernel_count...  10.6 us
    ppermute x3, starting transfers between devices, summed_everywhere(): lax.ppermute(flat, axis, [(i, i ^ mask) for i in range(count)])  7.48 us
    ppermute x6, waiting for transfers between devices, summed_everywhere(): received = lax.ppermute(send, axis, [(i, i ^ mask) for i in range(count)])  7.44 us
  transfers between devices with their start and end apart: 19, of which 9 were waited for; matrix products, arithmetic and copies ran while one was open for 3% of the time, Pallas kernels for 33%

profile of v11, /device:TPU:127, one launch (start us, length us, event | category | flops | bytes accessed | tf_op | source)
XLA Modules:
  0.0 152.9 jit_solution(13647235104371792957)
XLA Ops:
  0.6 2.6 %collective-permute-start.1 = (bf16[1024,128]{1,0:T(8,128)(2,1)}, bf16[1024,128]{1,0:T(8,128)(2,1)S(1)}, u32[]{:S(2)}, u32[]{:S(2)}) collective-permute-start(bf16[1024,128]{1,0:T(8,128)(2,1)} %param.8), channel_id=1, source_target_pairs={{1,0},{2,1},{3,2},{4,3},{5,4},{6,5},{7,6},{8,7},{9,8},{10,9},{11,1... | collective-permute-start | bytes 786440 | tf_op jit(solution)/shard_map/ppermute | solution.py:17
  3.2 8.4 %collective-permute-start = (bf16[1024,128]{1,0:T(8,128)(2,1)}, bf16[1024,128]{1,0:T(8,128)(2,1)S(1)}, u32[]{:S(2)}, u32[]{:S(2)}) collective-permute-start(bf16[1024,128]{1,0:T(8,128)(2,1)} %param.8), channel_id=1, source_target_pairs={{0,1},{1,2},{2,3},{3,4},{4,5},{5,6},{6,7},{7,8},{8,9},{9,10},{10,1... | collective-permute-start | bytes 786440 | tf_op jit(solution)/shard_map/ppermute | solution.py:17
  11.6 1.2 broadcast_clamp_fusion.1.offsets
  13.5 1.3 fusion.3
  15.3 1.0 pad_maximum_fusion
  16.3 1.2 copy.26
  17.5 10.6 %shard_map.103 = (f32[27,128,128]{2,1,0:T(8,128)}, bf16[256,128,128]{2,1,0:T(8,128)(2,1)}) custom-call(s32[256]{0:T(256)} %broadcast_clamp_fusion.1.offsets, s32[256]{0:T(256)} %get-tuple-element.128.blocks_at, s32[256]{0:T(256)} %get-tuple-element.129.targets, s32[1]{0:T(128)S(6)} %min.29.live, bf16[24,128,128]{2,1,0:T(8,128)(2,1)} %bitcast.46, ...), custom_call_target="tpu_custom_call" | custom-call | tf_op jit(solution)/shard_map/pallas_call | solution.py:146
  28.1 1.6 %broadcast_multiply_fusion = f32[27,128,128]{2,1,0:T(8,128)S(1)} fusion(f32[27,128,128]{2,1,0:T(8,128)} %get-tuple-element.64), kind=kLoop, calls=%fused_computation.3 | loop fusion | flops 442368 | bytes 3538944 | tf_op jit(solution)/shard_map/mul | solution.py:204
  30.9 1.6 %copy.27 = bf16[27,128,128]{1,2,0:T(8,128)(2,1)} copy(bf16[27,128,128]{2,1,0:T(8,128)(2,1)S(1)} %copy-done.2) | data formatting | bytes 1769472 | tf_op args[1]
  32.5 5.8 %shard_map.104 = (f32[8,128,128]{2,1,0:T(8,128)}, f32[24,128,128]{2,1,0:T(8,128)}) custom-call(s32[256]{0:T(256)} %broadcast_clamp_fusion.1.offsets, s32[256]{0:T(256)} %get-tuple-element.128.blocks_at, s32[256]{0:T(256)} %get-tuple-element.129.targets, s32[1]{0:T(128)S(6)} %min.29.live, bf16[27,128,128]{2,1,0:T(8,128)(2,1)} %bitcast.18, ...), custom_call_target="tpu_custom_call" | custom-call | tf_op jit(solution)/shard_map/pallas_call | solution.py:169
  38.3 1.3 select_add_fusion
  39.8 6.4 %shard_map.105 = (f32[8,128,128]{2,1,0:T(8,128)}, f32[24,128,128]{2,1,0:T(8,128)}) custom-call(s32[256]{0:T(256)} %broadcast_clamp_fusion.1.offsets, s32[256]{0:T(256)} %get-tuple-element.128.blocks_at, s32[256]{0:T(256)} %get-tuple-element.129.targets, s32[1]{0:T(128)S(6)} %min.29.live, ...), custom_call_target="tpu_custom_call", output_to_operand_aliasing={{0}: (8, {}), {1}: (9, {})} | custom-call | tf_op jit(solution)/shard_map/pallas_call | solution.py:169
  46.2 5.8 %collective-permute-done.3 = f32[110592]{0:T(1024)S(1)} collective-permute-done((f32[110592]{0:T(1024)S(1)}, f32[110592]{0:T(1024)S(1)}, u32[]{:S(2)}, u32[]{:S(2)}) %collective-permute-start.3) | collective-permute-done | bytes 442400 | tf_op jit(solution)/shard_map/ppermute | solution.py:43
  52.1 6.4 %shard_map.106 = (f32[8,128,128]{2,1,0:T(8,128)}, f32[24,128,128]{2,1,0:T(8,128)}) custom-call(s32[256]{0:T(256)} %broadcast_clamp_fusion.1.offsets, s32[256]{0:T(256)} %get-tuple-element.128.blocks_at, s32[256]{0:T(256)} %get-tuple-element.129.targets, s32[1]{0:T(128)S(6)} %min.29.live, ...), custom_call_target="tpu_custom_call", output_to_operand_aliasing={{0}: (8, {}), {1}: (9, {})} | custom-call | tf_op jit(solution)/shard_map/pallas_call | solution.py:169
  58.5 1.7 %collective-permute-done.4 = f32[55296]{0:T(1024)S(1)} collective-permute-done((f32[55296]{0:T(1024)S(1)}, f32[55296]{0:T(1024)S(1)}, u32[]{:S(2)}, u32[]{:S(2)}) %collective-permute-start.4) | collective-permute-done | bytes 221216 | tf_op jit(solution)/shard_map/ppermute | solution.py:43
  60.5 6.4 %shard_map.107 = (f32[8,128,128]{2,1,0:T(8,128)}, f32[24,128,128]{2,1,0:T(8,128)}) custom-call(s32[256]{0:T(256)} %broadcast_clamp_fusion.1.offsets, s32[256]{0:T(256)} %get-tuple-element.128.blocks_at, s32[256]{0:T(256)} %get-tuple-element.129.targets, s32[1]{0:T(128)S(6)} %min.29.live, ...), custom_call_target="tpu_custom_call", output_to_operand_aliasing={{0}: (8, {}), {1}: (9, {})} | custom-call | tf_op jit(solution)/shard_map/pallas_call | solution.py:169
  67.0 1.6 %collective-permute-start.6 = (f32[13824]{0:T(1024)S(1)}, f32[13824]{0:T(1024)S(1)}, u32[]{:S(2)}, u32[]{:S(2)}) collective-permute-start(f32[13824]{0:T(1024)S(1)} %slice_select_fusion.4), channel_id=1, source_target_pairs={{0,16},{1,17},{2,18},{3,19},{4,20},{5,21},{6,22},{7,23},{8,24},{9,... | collective-permute-start | bytes 165896 | tf_op jit(solution)/shard_map/ppermute | solution.py:43
  68.6 6.4 %shard_map.108 = (f32[8,128,128]{2,1,0:T(8,128)}, f32[24,128,128]{2,1,0:T(8,128)}) custom-call(s32[256]{0:T(256)} %broadcast_clamp_fusion.1.offsets, s32[256]{0:T(256)} %get-tuple-element.128.blocks_at, s32[256]{0:T(256)} %get-tuple-element.129.targets, s32[1]{0:T(128)S(6)} %min.29.live, ...), custom_call_target="tpu_custom_call", output_to_operand_aliasing={{0}: (8, {}), {1}: (9, {})} | custom-call | tf_op jit(solution)/shard_map/pallas_call | solution.py:169
  75.1 6.4 %shard_map.109 = (f32[8,128,128]{2,1,0:T(8,128)}, f32[24,128,128]{2,1,0:T(8,128)}) custom-call(s32[256]{0:T(256)} %broadcast_clamp_fusion.1.offsets, s32[256]{0:T(256)} %get-tuple-element.128.blocks_at, s32[256]{0:T(256)} %get-tuple-element.129.targets, s32[1]{0:T(128)S(6)} %min.29.live, ...), custom_call_target="tpu_custom_call", output_to_operand_aliasing={{0}: (8, {}), {1}: (9, {})} | custom-call | tf_op jit(solution)/shard_map/pallas_call | solution.py:169
  81.5 5.3 %collective-permute-start.10 = (f32[6912]{0:T(1024)S(1)}, f32[6912]{0:T(1024)S(1)}, u32[]{:S(2)}, u32[]{:S(2)}) collective-permute-start(f32[6912]{0:T(1024)S(1)} %select_add_fusion.5), channel_id=1, source_target_pairs={{0,192},{1,193},{2,194},{3,195},{4,196},{5,197},{6,198},{7,199},{8... | collective-permute-start | bytes 82952 | tf_op jit(solution)/shard_map/ppermute | solution.py:46
  87.4 1.5 %collective-permute-start.8 = (f32[6912]{0:T(1024)S(1)}, f32[6912]{0:T(1024)S(1)}, u32[]{:S(2)}, u32[]{:S(2)}) collective-permute-start(f32[6912]{0:T(1024)S(1)} %select_add_fusion.5), channel_id=1, source_target_pairs={{0,64},{1,65},{2,66},{3,67},{4,68},{5,69},{6,70},{7,71},{8,72},{9,... | collective-permute-start | bytes 82952 | tf_op jit(solution)/shard_map/ppermute | solution.py:46
  89.0 6.4 %shard_map.110 = (f32[8,128,128]{2,1,0:T(8,128)}, f32[24,128,128]{2,1,0:T(8,128)}) custom-call(s32[256]{0:T(256)} %broadcast_clamp_fusion.1.offsets, s32[256]{0:T(256)} %get-tuple-element.128.blocks_at, s32[256]{0:T(256)} %get-tuple-element.129.targets, s32[1]{0:T(128)S(6)} %min.29.live, ...), custom_call_target="tpu_custom_call", output_to_operand_aliasing={{0}: (8, {}), {1}: (9, {})} | custom-call | tf_op jit(solution)/shard_map/pallas_call | solution.py:169
  95.9 6.4 %shard_map.111 = (f32[8,128,128]{2,1,0:T(8,128)}, f32[24,128,128]{2,1,0:T(8,128)}) custom-call(s32[256]{0:T(256)} %broadcast_clamp_fusion.1.offsets, s32[256]{0:T(256)} %get-tuple-element.128.blocks_at, s32[256]{0:T(256)} %get-tuple-element.129.targets, s32[1]{0:T(128)S(6)} %min.29.live, ...), custom_call_target="tpu_custom_call", output_to_operand_aliasing={{0}: (8, {}), {1}: (9, {})} | custom-call | tf_op jit(solution)/shard_map/pallas_call | solution.py:169
  103.3 3.8 %collective-permute-done.12 = f32[13824]{0:T(1024)S(1)} collective-permute-done((f32[13824]{0:T(1024)S(1)}, f32[13824]{0:T(1024)S(1)}, u32[]{:S(2)}, u32[]{:S(2)}) %collective-permute-start.12) | collective-permute-done | bytes 55328 | tf_op jit(solution)/shard_map/ppermute | solution.py:53
  107.2 4.2 %collective-permute-done.13 = f32[27648]{0:T(1024)S(1)} collective-permute-done((f32[27648]{0:T(1024)S(1)}, f32[27648]{0:T(1024)S(1)}, u32[]{:S(2)}, u32[]{:S(2)}) %collective-permute-start.13) | collective-permute-done | bytes 110624 | tf_op jit(solution)/shard_map/ppermute | solution.py:53
  112.3 5.6 %collective-permute-done.14 = f32[55296]{0:T(1024)S(1)} collective-permute-done((f32[55296]{0:T(1024)S(1)}, f32[55296]{0:T(1024)S(1)}, u32[]{:S(2)}, u32[]{:S(2)}) %collective-permute-start.14) | collective-permute-done | bytes 221216 | tf_op jit(solution)/shard_map/ppermute | solution.py:53
  118.3 13.9 %collective-permute-start.17 = (f32[1024,128]{1,0:T(8,128)S(1)}, f32[1024,128]{1,0:T(8,128)S(1)}, u32[]{:S(2)}, u32[]{:S(2)}) collective-permute-start(f32[1024,128]{1,0:T(8,128)S(1)} %bitcast.50), channel_id=1, source_target_pairs={{0,1},{1,2},{2,3},{3,4},{4,5},{5,6},{6,7},{7,8},{8,9},{9,10},{10,1... | collective-permute-start | bytes 1572872 | tf_op jit(solution)/shard_map/ppermute | solution.py:17
  132.2 2.1 %collective-permute-start.16 = (f32[1024,128]{1,0:T(8,128)S(1)}, f32[1024,128]{1,0:T(8,128)S(1)}, u32[]{:S(2)}, u32[]{:S(2)}) collective-permute-start(f32[1024,128]{1,0:T(8,128)S(1)} %bitcast.49), channel_id=1, source_target_pairs={{1,0},{2,1},{3,2},{4,3},{5,4},{6,5},{7,6},{8,7},{9,8},{10,9},{11,1... | collective-permute-start | bytes 1572872 | tf_op jit(solution)/shard_map/ppermute | solution.py:17
  134.4 4.0 %collective-permute-done.17 = f32[1024,128]{1,0:T(8,128)S(1)} collective-permute-done((f32[1024,128]{1,0:T(8,128)S(1)}, f32[1024,128]{1,0:T(8,128)S(1)}, u32[]{:S(2)}, u32[]{:S(2)}) %collective-permute-start.17) | collective-permute-done | bytes 524320 | tf_op jit(solution)/shard_map/ppermute | solution.py:17
  138.3 10.0 %collective-permute-done.16 = f32[1024,128]{1,0:T(8,128)S(1)} collective-permute-done((f32[1024,128]{1,0:T(8,128)S(1)}, f32[1024,128]{1,0:T(8,128)S(1)}, u32[]{:S(2)}, u32[]{:S(2)}) %collective-permute-start.16) | collective-permute-done | bytes 524320 | tf_op jit(solution)/shard_map/ppermute | solution.py:17
  150.0 1.5 collective-permute-done.18
  151.5 1.4 maximum_select_fusion
  (50 shorter events, 7.7 us)
Async XLA Ops:
  0.6 14.2 %collective-permute-start.1 = (bf16[1024,128]{1,0:T(8,128)(2,1)}, bf16[1024,128]{1,0:T(8,128)(2,1)S(1)}, u32[]{:S(2)}, u32[]{:S(2)}) collective-permute-start(bf16[1024,128]{1,0:T(8,128)(2,1)} %param.8), channel_id=1, source_target_pairs={{1,0},{2,1},{3,2},{4,3},{5,4},{6,5},{7,6},{8,7},{9,8},{10,9},{11,1... | collective-permute-start | bytes 786440 | tf_op jit(solution)/shard_map/ppermute | solution.py:17
  3.2 12.0 %collective-permute-start = (bf16[1024,128]{1,0:T(8,128)(2,1)}, bf16[1024,128]{1,0:T(8,128)(2,1)S(1)}, u32[]{:S(2)}, u32[]{:S(2)}) collective-permute-start(bf16[1024,128]{1,0:T(8,128)(2,1)} %param.8), channel_id=1, source_target_pairs={{0,1},{1,2},{2,3},{3,4},{4,5},{5,6},{6,7},{7,8},{8,9},{9,10},{10,1... | collective-permute-start | bytes 786440 | tf_op jit(solution)/shard_map/ppermute | solution.py:17
  29.7 1.2 copy-start.2
  29.8 8.5 %collective-permute-start.2 = (f32[221184]{0:T(1024)S(1)}, f32[221184]{0:T(1024)}, u32[]{:S(2)}, u32[]{:S(2)}) collective-permute-start(f32[221184]{0:T(1024)S(1)} %slice_select_fusion), channel_id=1, source_target_pairs={{0,1},{1,0},{2,3},{3,2},{4,5},{5,4},{6,7},{7,6},{8,9},{9,8},{10,11... | collective-permute-start | bytes 2654216 | tf_op jit(solution)/shard_map/ppermute | solution.py:43
  39.7 12.2 %collective-permute-start.3 = (f32[110592]{0:T(1024)S(1)}, f32[110592]{0:T(1024)S(1)}, u32[]{:S(2)}, u32[]{:S(2)}) collective-permute-start(f32[110592]{0:T(1024)S(1)} %slice_select_fusion.1), channel_id=1, source_target_pairs={{0,2},{1,3},{2,0},{3,1},{4,6},{5,7},{6,4},{7,5},{8,10},{9,11},{10,... | collective-permute-start | bytes 1327112 | tf_op jit(solution)/shard_map/ppermute | solution.py:43
  52.0 8.2 %collective-permute-start.4 = (f32[55296]{0:T(1024)S(1)}, f32[55296]{0:T(1024)S(1)}, u32[]{:S(2)}, u32[]{:S(2)}) collective-permute-start(f32[55296]{0:T(1024)S(1)} %slice_select_fusion.2), channel_id=1, source_target_pairs={{0,4},{1,5},{2,6},{3,7},{4,0},{5,1},{6,2},{7,3},{8,12},{9,13},{10,... | collective-permute-start | bytes 663560 | tf_op jit(solution)/shard_map/ppermute | solution.py:43
  60.2 6.7 %collective-permute-start.5 = (f32[27648]{0:T(1024)S(1)}, f32[27648]{0:T(1024)S(1)}, u32[]{:S(2)}, u32[]{:S(2)}) collective-permute-start(f32[27648]{0:T(1024)S(1)} %slice_select_fusion.3), channel_id=1, source_target_pairs={{0,8},{1,9},{2,10},{3,11},{4,12},{5,13},{6,14},{7,15},{8,0},{9,1},... | collective-permute-start | bytes 331784 | tf_op jit(solution)/shard_map/ppermute | solution.py:43
  67.0 8.0 %collective-permute-start.6 = (f32[13824]{0:T(1024)S(1)}, f32[13824]{0:T(1024)S(1)}, u32[]{:S(2)}, u32[]{:S(2)}) collective-permute-start(f32[13824]{0:T(1024)S(1)} %slice_select_fusion.4), channel_id=1, source_target_pairs={{0,16},{1,17},{2,18},{3,19},{4,20},{5,21},{6,22},{7,23},{8,24},{9,... | collective-permute-start | bytes 165896 | tf_op jit(solution)/shard_map/ppermute | solution.py:43
  75.0 6.5 %collective-permute-start.7 = (f32[6912]{0:T(1024)S(1)}, f32[6912]{0:T(1024)S(1)}, u32[]{:S(2)}, u32[]{:S(2)}) collective-permute-start(f32[6912]{0:T(1024)S(1)} %slice_select_fusion.5), channel_id=1, source_target_pairs={{0,32},{1,33},{2,34},{3,35},{4,36},{5,37},{6,38},{7,39},{8,40},{9,... | collective-permute-start | bytes 82952 | tf_op jit(solution)/shard_map/ppermute | solution.py:43
  81.5 13.9 %collective-permute-start.10 = (f32[6912]{0:T(1024)S(1)}, f32[6912]{0:T(1024)S(1)}, u32[]{:S(2)}, u32[]{:S(2)}) collective-permute-start(f32[6912]{0:T(1024)S(1)} %select_add_fusion.5), channel_id=1, source_target_pairs={{0,192},{1,193},{2,194},{3,195},{4,196},{5,197},{6,198},{7,199},{8... | collective-permute-start | bytes 82952 | tf_op jit(solution)/shard_map/ppermute | solution.py:46
  86.8 8.6 %collective-permute-start.9 = (f32[6912]{0:T(1024)S(1)}, f32[6912]{0:T(1024)S(1)}, u32[]{:S(2)}, u32[]{:S(2)}) collective-permute-start(f32[6912]{0:T(1024)S(1)} %select_add_fusion.5), channel_id=1, source_target_pairs={{0,128},{1,129},{2,130},{3,131},{4,132},{5,133},{6,134},{7,135},{8... | collective-permute-start | bytes 82952 | tf_op jit(solution)/shard_map/ppermute | solution.py:46
  87.4 7.9 %collective-permute-start.8 = (f32[6912]{0:T(1024)S(1)}, f32[6912]{0:T(1024)S(1)}, u32[]{:S(2)}, u32[]{:S(2)}) collective-permute-start(f32[6912]{0:T(1024)S(1)} %select_add_fusion.5), channel_id=1, source_target_pairs={{0,64},{1,65},{2,66},{3,67},{4,68},{5,69},{6,70},{7,71},{8,72},{9,... | collective-permute-start | bytes 82952 | tf_op jit(solution)/shard_map/ppermute | solution.py:46
  95.4 6.9 %collective-permute-start.11 = (f32[6912]{0:T(1024)S(1)}, f32[6912]{0:T(1024)S(1)}, u32[]{:S(2)}, u32[]{:S(2)}) collective-permute-start(f32[6912]{0:T(1024)S(1)} %add_add_fusion), channel_id=1, source_target_pairs={{0,32},{1,33},{2,34},{3,35},{4,36},{5,37},{6,38},{7,39},{8,40},{9,... | collective-permute-start | bytes 82952 | tf_op jit(solution)/shard_map/ppermute | solution.py:53
  102.2 16.0 %copy-start = (f32[24,128,128]{2,1,0:T(8,128)S(1)}, f32[24,128,128]{2,1,0:T(8,128)}, u32[]{:S(2)}) copy-start(f32[24,128,128]{2,1,0:T(8,128)} %get-tuple-element.121) | copy-start | bytes 4718596
  102.3 4.8 %collective-permute-start.12 = (f32[13824]{0:T(1024)S(1)}, f32[13824]{0:T(1024)S(1)}, u32[]{:S(2)}, u32[]{:S(2)}) collective-permute-start(f32[13824]{0:T(1024)S(1)} %maximum_select_fusion.5), channel_id=1, source_target_pairs={{0,16},{1,17},{2,18},{3,19},{4,20},{5,21},{6,22},{7,23},{8,24},{9,... | collective-permute-start | bytes 165896 | tf_op jit(solution)/shard_map/ppermute | solution.py:53
  107.1 4.3 %collective-permute-start.13 = (f32[27648]{0:T(1024)S(1)}, f32[27648]{0:T(1024)S(1)}, u32[]{:S(2)}, u32[]{:S(2)}) collective-permute-start(f32[27648]{0:T(1024)S(1)} %maximum_select_fusion.4), channel_id=1, source_target_pairs={{0,8},{1,9},{2,10},{3,11},{4,12},{5,13},{6,14},{7,15},{8,0},{9,1},... | collective-permute-start | bytes 331784 | tf_op jit(solution)/shard_map/ppermute | solution.py:53
  111.5 6.4 %collective-permute-start.14 = (f32[55296]{0:T(1024)S(1)}, f32[55296]{0:T(1024)S(1)}, u32[]{:S(2)}, u32[]{:S(2)}) collective-permute-start(f32[55296]{0:T(1024)S(1)} %maximum_select_fusion.3), channel_id=1, source_target_pairs={{0,4},{1,5},{2,6},{3,7},{4,0},{5,1},{6,2},{7,3},{8,12},{9,13},{10,... | collective-permute-start | bytes 663560 | tf_op jit(solution)/shard_map/ppermute | solution.py:53
  117.9 16.4 %collective-permute-start.15 = (f32[110592]{0:T(1024)S(1)}, f32[110592]{0:T(1024)S(1)}, u32[]{:S(2)}, u32[]{:S(2)}) collective-permute-start(f32[110592]{0:T(1024)S(1)} %maximum_select_fusion.2), channel_id=1, source_target_pairs={{0,2},{1,3},{2,0},{3,1},{4,6},{5,7},{6,4},{7,5},{8,10},{9,11},{10,... | collective-permute-start | bytes 1327112 | tf_op jit(solution)/shard_map/ppermute | solution.py:53
  118.3 20.0 %collective-permute-start.17 = (f32[1024,128]{1,0:T(8,128)S(1)}, f32[1024,128]{1,0:T(8,128)S(1)}, u32[]{:S(2)}, u32[]{:S(2)}) collective-permute-start(f32[1024,128]{1,0:T(8,128)S(1)} %bitcast.50), channel_id=1, source_target_pairs={{0,1},{1,2},{2,3},{3,4},{4,5},{5,6},{6,7},{7,8},{8,9},{9,10},{10,1... | collective-permute-start | bytes 1572872 | tf_op jit(solution)/shard_map/ppermute | solution.py:17
  132.2 16.9 %copy-start.1 = (f32[8,128,128]{2,1,0:T(8,128)S(1)}, f32[8,128,128]{2,1,0:T(8,128)}, u32[]{:S(2)}) copy-start(f32[8,128,128]{2,1,0:T(8,128)} %get-tuple-element.122) | copy-start | bytes 1572868
  132.2 16.1 %collective-permute-start.16 = (f32[1024,128]{1,0:T(8,128)S(1)}, f32[1024,128]{1,0:T(8,128)S(1)}, u32[]{:S(2)}, u32[]{:S(2)}) collective-permute-start(f32[1024,128]{1,0:T(8,128)S(1)} %bitcast.49), channel_id=1, source_target_pairs={{1,0},{2,1},{3,2},{4,3},{5,4},{6,5},{7,6},{8,7},{9,8},{10,9},{11,1... | collective-permute-start | bytes 1572872 | tf_op jit(solution)/shard_map/ppermute | solution.py:17
  149.1 2.4 %collective-permute-start.18 = (f32[221184]{0:T(1024)S(1)}, f32[221184]{0:T(1024)S(1)}, u32[]{:S(2)}, u32[]{:S(2)}) collective-permute-start(f32[221184]{0:T(1024)S(1)} %maximum_select_fusion.1), channel_id=1, source_target_pairs={{0,1},{1,0},{2,3},{3,2},{4,5},{5,4},{6,7},{7,6},{8,9},{9,8},{10,11... | collective-permute-start | bytes 2654216 | tf_op jit(solution)/shard_map/ppermute | solution.py:53
